TPU v7x, 128 devices: a whole 4x4x4 slice. The times are simulated.
128 devices in a mesh: serve: 8 (over x, core), store: 16 (over z, y).
Axes of the slice: x: 4, y: 4, z: 4, core: 2. Of those that a mesh axis runs over, the one named last changes fastest.
Arguments:
- normalized_hidden_states: bfloat16 [65536, 2048], P(('serve', 'store')), may hold values from -20 to 20
- query_weight_matrix: bfloat16 [2048, 2048], replicated, may hold values from -0.125 to 0.125
- key_weight_matrix: bfloat16 [2048, 512], replicated, may hold values from -0.125 to 0.125
- value_weight_matrix: bfloat16 [2048, 512], replicated, may hold values from -0.125 to 0.125
- adapter_down_weight: bfloat16 [512, 32, 2048], P('store', None, 'serve'), may hold values from -0.125 to 0.125
- adapter_up_query_weight: bfloat16 [512, 16, 2048], P('store', None, 'serve'), may hold values from -1.5 to 1.5
- adapter_up_value_weight: bfloat16 [512, 16, 512], P('store', None, 'serve'), may hold values from -1.5 to 1.5
- adapter_panel_slot: int32 [512], replicated, may hold values from 0 to 511, as said below
- adapter_per_request: int32 [128, 16], P(('serve', 'store')), may hold values from 0 to 511, as said below
- request_token_length: int32 [128, 16], P(('serve', 'store')), may hold values from 1 to 64, 512 in all within a row
Outputs:
- attended: bfloat16 [65536, 2048], P(('serve', 'store'))
Inputs may be any that keep to these rules, and one draw needn't show every extreme that they name: Each number appears once; adapter a's panels are entry adapter_panel_slot[a] of the three panel arrays, whose owner is index adapter_panel_slot[a] // 32 of store. `adapter_per_request`: the 16 requests of one device use adapters of 16 different owners. `request_token_length`: each row sums to 512; the longest request of each device has exactly 64 tokens.
All inputs are finite; a program needn't handle non-finite values.
Results may differ from a plain program's by a relative error of at most 0.012.
Values may be sent and summed in bfloat16 or wider, within the bound.
No kernel may reach another device: no remote copies, remote signals or barrier semaphores. Data moves between devices by JAX's collectives and lax.ppermute only.
A program may use at most 128 MiB of HBM per device.

v0:
```python
import jax
import jax.numpy as jnp
from jax import lax
from jax.sharding import PartitionSpec as P

HEADS = 32
KV_HEADS = 8
HEAD_DIM = 64
ADAPTER_RANK = 16
ADP_DEV = 32
LEN_MAX = 64


def rotary(heads_in, positions):
    half_dim = HEAD_DIM // 2
    frequency = 500000.0 ** (-(jnp.arange(half_dim).astype(jnp.float32) * 2.0 / HEAD_DIM))
    angles = positions.astype(jnp.float32)[:, None] * frequency[None, :]
    cosine_table = jnp.cos(angles)[:, None, :]
    sine_table = jnp.sin(angles)[:, None, :]
    first_half = heads_in[..., :half_dim]
    second_half = heads_in[..., half_dim:]
    return jnp.concatenate(
        [
            first_half * cosine_table - second_half * sine_table,
            second_half * cosine_table + first_half * sine_table,
        ],
        axis=-1,
    )


def table_lookup(table, wanted):
    entries = jnp.arange(table.shape[0], dtype=jnp.int32)
    return jnp.sum(jnp.where(wanted[..., None] == entries, table, 0), axis=-1)


def reduced_rank_products(block_list, down_panels, up_query, up_value):
    low = jnp.einsum(
        "jkd,jrd->jkr", block_list, down_panels, preferred_element_type=jnp.float32
    ).astype(jnp.bfloat16)
    query_update = jnp.einsum(
        "jkr,jrd->jkd", low[..., :ADAPTER_RANK], up_query, preferred_element_type=jnp.float32
    ).astype(jnp.bfloat16)
    value_update = jnp.einsum(
        "jkr,jrd->jkd", low[..., ADAPTER_RANK:], up_value, preferred_element_type=jnp.float32
    ).astype(jnp.bfloat16)
    return (query_update, value_update)


def local_choice(panel_set, lists, adapter_panel_slot, my_store):
    source_slots = table_lookup(adapter_panel_slot, lists)
    mine_mask = source_slots // ADP_DEV == my_store
    local_source = jnp.sum(jnp.where(mine_mask, source_slots % ADP_DEV, 0), axis=1)
    return tuple((jnp.take(panel, local_source, axis=0) for panel in panel_set))


def attention(query_rot, key_rot, value_rows, request_ids):
    tok_rows = query_rot.shape[0]
    per_group = HEADS // KV_HEADS
    block_rows = min(128, tok_rows)
    reach = LEN_MAX
    key_pad = jnp.concatenate(
        [jnp.zeros((reach,) + key_rot.shape[1:], key_rot.dtype), key_rot], axis=0
    )
    value_pad = jnp.concatenate(
        [jnp.zeros((reach,) + value_rows.shape[1:], value_rows.dtype), value_rows], axis=0
    )
    ids_pad = jnp.concatenate([jnp.full((reach,), -1, jnp.int32), request_ids], axis=0)
    token_order = jnp.arange(tok_rows, dtype=jnp.int32)
    order_pad = jnp.concatenate([jnp.full((reach,), -1, jnp.int32), token_order], axis=0)
    outputs = []
    for block_index in range(tok_rows // block_rows):
        first = block_index * block_rows
        query_block = query_rot[first : first + block_rows]
        query_ids = request_ids[first : first + block_rows]
        query_order = token_order[first : first + block_rows]
        key_block = key_pad[first : first + reach + block_rows]
        value_block = value_pad[first : first + reach + block_rows]
        key_ids = ids_pad[first : first + reach + block_rows]
        key_order = order_pad[first : first + reach + block_rows]
        allowed = (query_ids[:, None] == key_ids[None, :]) & (
            key_order[None, :] <= query_order[:, None]
        )
        pieces = []
        for group_index in range(KV_HEADS):
            query_part = query_block[:, group_index * per_group : (group_index + 1) * per_group, :]
            key_part = key_block[:, group_index, :]
            value_part = value_block[:, group_index, :]
            scores = jnp.einsum(
                "qhd,kd->hqk", query_part, key_part, preferred_element_type=jnp.float32
            ) * HEAD_DIM ** (-0.5)
            scores = jnp.where(allowed[None], scores, -jnp.inf)
            row_max = jnp.max(scores, axis=-1, keepdims=True)
            raised = jnp.exp(scores - row_max)
            row_total = jnp.sum(raised, axis=-1)
            weights = raised.astype(jnp.bfloat16)
            mixed_heads = (
                jnp.einsum("hqk,kd->qhd", weights, value_part, preferred_element_type=jnp.float32)
                / jnp.transpose(row_total)[:, :, None]
            )
            pieces.append(mixed_heads)
        outputs.append(
            jnp.concatenate(pieces, axis=1)
            .reshape(block_rows, HEADS * HEAD_DIM)
            .astype(jnp.bfloat16)
        )
    return jnp.concatenate(outputs, axis=0)


def local(
    normalized_hidden_states,
    query_weight_matrix,
    key_weight_matrix,
    value_weight_matrix,
    adapter_down_weight,
    adapter_up_query_weight,
    adapter_up_value_weight,
    adapter_panel_slot,
    adapter_per_request,
    request_token_length,
):
    store_count = lax.axis_size("store")
    my_store = lax.axis_index("store")
    tok_rows = normalized_hidden_states.shape[0]
    request_count = request_token_length.shape[1]
    group_lists = lax.all_gather(adapter_per_request, "store", axis=0, tiled=True)
    lengths = request_token_length[0]
    adapters = adapter_per_request[0]
    request_ends = jnp.cumsum(lengths)
    starts = request_ends - lengths
    token_order = jnp.arange(tok_rows, dtype=jnp.int32)
    request_ids = jnp.sum((token_order[:, None] >= request_ends[None, :]).astype(jnp.int32), axis=1)
    member = request_ids[:, None] == jnp.arange(request_count, dtype=jnp.int32)[None, :]
    positions = token_order - jnp.sum(jnp.where(member, starts[None, :], 0), axis=1)
    slot_index_list = table_lookup(adapter_panel_slot, adapters)
    owners = slot_index_list // ADP_DEV
    owner_pick = owners[None, :] == jnp.arange(store_count, dtype=jnp.int32)[:, None]
    start_for = jnp.sum(jnp.where(owner_pick, starts[None, :], 0), axis=1)
    length_for = jnp.sum(jnp.where(owner_pick, lengths[None, :], 0), axis=1)
    offsets = jnp.arange(LEN_MAX, dtype=jnp.int32)
    valid_rows = offsets[None, :] < length_for[:, None]
    row_index = jnp.where(valid_rows, start_for[:, None] + offsets[None, :], 0)
    block_list = jnp.where(
        valid_rows[..., None], normalized_hidden_states[row_index], jnp.zeros((), jnp.bfloat16)
    )
    owner_token = jnp.sum(jnp.where(member, owners[None, :], 0), axis=1)
    back_index = owner_token * LEN_MAX + positions
    panels = (
        lax.all_gather(adapter_down_weight, "serve", axis=2, tiled=True),
        lax.all_gather(adapter_up_query_weight, "serve", axis=2, tiled=True),
        lax.all_gather(adapter_up_value_weight, "serve", axis=2, tiled=True),
    )
    down_chosen, upq_chosen, upv_chosen = local_choice(
        panels, group_lists, adapter_panel_slot, my_store
    )
    arrived = lax.all_to_all(block_list, "store", split_axis=0, concat_axis=0, tiled=True)
    query_update, value_update = reduced_rank_products(arrived, down_chosen, upq_chosen, upv_chosen)
    query_update, value_update = (
        lax.all_to_all(query_update, "store", split_axis=0, concat_axis=0, tiled=True),
        lax.all_to_all(value_update, "store", split_axis=0, concat_axis=0, tiled=True),
    )
    delta_query = query_update.reshape(-1, query_update.shape[2])[back_index]
    delta_value = value_update.reshape(-1, value_update.shape[2])[back_index]
    base_query = jnp.dot(
        normalized_hidden_states, query_weight_matrix, preferred_element_type=jnp.float32
    ) + delta_query.astype(jnp.float32)
    query_rot = rotary(base_query.reshape(tok_rows, HEADS, HEAD_DIM), positions).astype(
        jnp.bfloat16
    )
    base_key = jnp.dot(
        normalized_hidden_states, key_weight_matrix, preferred_element_type=jnp.float32
    )
    key_rot = rotary(base_key.reshape(tok_rows, KV_HEADS, HEAD_DIM), positions).astype(jnp.bfloat16)
    value_rows = (
        jnp.dot(normalized_hidden_states, value_weight_matrix, preferred_element_type=jnp.float32)
        + delta_value.astype(jnp.float32)
    ).astype(jnp.bfloat16)
    value_rows = value_rows.reshape(tok_rows, KV_HEADS, HEAD_DIM)
    return attention(query_rot, key_rot, value_rows, request_ids)


def solution(mesh):
    return jax.shard_map(
        local,
        mesh=mesh,
        in_specs=(
            P(("serve", "store"), None),
            P(),
            P(),
            P(),
            P("store", None, "serve"),
            P("store", None, "serve"),
            P("store", None, "serve"),
            P(),
            P(("serve", "store"), None),
            P(("serve", "store"), None),
        ),
        out_specs=P(("serve", "store"), None),
        check_vma=False,
    )
```

profile of v0, /device:TPU:6, one launch (start us, length us, event | category | flops | bytes accessed | tf_op | source)
XLA Modules:
  0.0 278.1 jit_solution(15129915523642141510)
XLA Ops:
  8.1 0.9 select_reduce_fusion.3
  10.6 6.1 %gather_fusion = bf16[1024,2048]{1,0:T(8,128)(2,1)} fusion(bf16[512,2048]{1,0:T(8,128)(2,1)S(1)} %copy-done, s32[1024]{0:T(1024)S(1)} %broadcast_clamp_fusion), kind=kCustom, calls=%fused_computation | custom fusion | bytes 8392704 | tf_op jit(solution)/shard_map/gather | solution.py:143
  16.8 4.5 %broadcast_select_fusion = bf16[16,64,2048]{2,1,0:T(8,128)(2,1)} fusion(bf16[16,64,2048]{2,1,0:T(8,128)(2,1)} %bitcast.784, pred[16,64]{1,0:T(8,128)(4,1)S(1)} %iota_compare_fusion.6), kind=kLoop, calls=%fused_computation.69 | loop fusion | flops 2097152 | bytes 8389632 | tf_op jit(solution)/shard_map/jit(_where)/select_n | solution.py:142
  21.3 8.3 %all-to-all-start = ((bf16[16,64,2048]{2,1,0:T(8,128)(2,1)}), bf16[16,64,2048]{2,1,0:T(8,128)(2,1)}, u32[]{:S(2)}, u32[]{:S(2)}) async-start(bf16[16,64,2048]{2,1,0:T(8,128)(2,1)} %broadcast_select_fusion), calls=%async_computation | async-start | bytes 8388608 | tf_op jit(solution)/shard_map/all_to_all | solution.py:155
  30.6 21.4 %all_gather.14 = bf16[32,16,512]{0,1,2:T(8,128)(2,1)} all-gather(bf16[32,16,64]{0,1,2:T(8,128)(2,1)S(1)} %copy.78), channel_id=1, replica_groups=mesh['serve'=8,'store'=16] {'serve'}, dimensions={2}, use_global_device_ids=true | all-gather | bytes 589824 | tf_op jit(solution)/shard_map/all_gather | solution.py:150
  52.1 3.1 %copy.79 = bf16[32,16,512]{2,1,0:T(8,128)(2,1)S(1)} copy(bf16[32,16,512]{0,1,2:T(8,128)(2,1)} %all_gather.14) | data formatting | bytes 1048576 | tf_op jit(solution)/shard_map/all_gather | solution.py:150
  55.2 48.8 %all-gather = s32[16,1,16]{2,1,0:T(1,128)S(1)} all-gather(s32[1,1,16]{2,1,0:T(1,128)S(1)} %bitcast.854), channel_id=1, replica_groups=mesh['serve'=8,'store'=16] {'store'}, dimensions={0}, use_global_device_ids=true | all-gather | bytes 1088 | tf_op jit(solution)/shard_map/all_gather | solution.py:125
  105.2 4.2 %gather_fusion.1 = bf16[16,32,2048]{2,1,0:T(8,128)(2,1)} fusion(bf16[32,32,2048]{2,1,0:T(8,128)(2,1)} %all-gather.4.cloned.1.call-done, s32[1024]{0:T(1024)S(1)} %pad_clamp_fusion.1), kind=kCustom, calls=%fused_computation.1 | custom fusion | bytes 4194368 | tf_op jit(solution)/shard_map/jit(_take)/gather | solution.py:53
  109.4 4.1 %fusion.68 = bf16[16,64,32]{1,2,0:T(8,128)(2,1)S(1)} fusion(bf16[16,64,2048]{2,1,0:T(8,128)(2,1)} %all-to-all-done, bf16[16,32,2048]{2,1,0:T(8,128)(2,1)} %gather_fusion.1, pred[16]{0:T(512)(128)(4,1)S(1)} %compare_and_fusion.4), kind=kOutput, calls=%fused_computation.225 | convolution fusion | flops 135299072 | bytes 6357008 | tf_op jit(solution)/shard_map/jkd,jrd->jkr/dot_general | solution.py:37
  113.5 1.5 convolution_convert_fusion.1
  115.0 4.6 %all-to-all-start.1 = ((bf16[16,64,512]{2,1,0:T(8,128)(2,1)}), bf16[16,64,512]{2,1,0:T(8,128)(2,1)}, u32[]{:S(2)}, u32[]{:S(2)}) async-start(bf16[16,64,512]{2,1,0:T(8,128)(2,1)} %convolution_convert_fusion.1), calls=%async_computation.1 | async-start | bytes 2097152 | tf_op jit(solution)/shard_map/all_to_all | solution.py:159
  119.7 3.2 %gather_fusion.4 = bf16[16,16,2048]{2,1,0:T(8,128)(2,1)} fusion(bf16[32,16,2048]{2,1,0:T(8,128)(2,1)} %all-gather.6.cloned.1.call-done, s32[1024]{0:T(1024)S(1)} %pad_clamp_fusion.1), kind=kCustom, calls=%fused_computation.4 | custom fusion | bytes 2097216 | tf_op jit(solution)/shard_map/jit(_take)/gather | solution.py:53
  122.8 4.5 %convolution_convert_fusion = bf16[16,64,2048]{2,1,0:T(8,128)(2,1)} fusion(bf16[16,16,2048]{2,1,0:T(8,128)(2,1)} %gather_fusion.4, pred[16]{0:T(512)(128)(4,1)S(1)} %compare_and_fusion.4, bf16[16,64,32]{1,2,0:T(8,128)(2,1)S(1)} %fusion.68), kind=kOutput, calls=%fused_computation.70 | convolution fusion | flops 69730304 | bytes 5308928 | tf_op jit(solution)/shard_map/jkr,jrd->jkd/dot_general | solution.py:40
  127.3 6.5 %all-to-all-done.1 = bf16[16,64,512]{2,1,0:T(8,128)(2,1)} async-done(((bf16[16,64,512]{2,1,0:T(8,128)(2,1)}), bf16[16,64,512]{2,1,0:T(8,128)(2,1)}, u32[]{:S(2)}, u32[]{:S(2)}) %all-to-all-start.1) | async-done | bytes 1048608 | tf_op jit(solution)/shard_map/all_to_all | solution.py:159
  133.8 4.7 %all-to-all-start.2 = ((bf16[16,64,2048]{2,1,0:T(8,128)(2,1)}), bf16[16,64,2048]{2,1,0:T(8,128)(2,1)}, u32[]{:S(2)}, u32[]{:S(2)}) async-start(bf16[16,64,2048]{2,1,0:T(8,128)(2,1)} %convolution_convert_fusion), calls=%async_computation.2 | async-start | bytes 8388608 | tf_op jit(solution)/shard_map/all_to_all | solution.py:158
  139.3 2.9 %fusion.563 = f32[512,512]{0,1:T(8,128)S(1)} fusion(bf16[512,2048]{1,0:T(8,128)(2,1)S(1)} %copy-done, bf16[2048,512]{1,0:T(8,128)(2,1)} %param.12), kind=kOutput, calls=%fused_computation.765 | convolution fusion | flops 1073741824 | bytes 5242880 | tf_op jit(solution)/shard_map/dot_general | solution.py:169
  142.4 0.8 pad_maximum_fusion
  143.7 3.3 %gather_fusion.3 = bf16[512,512]{1,0:T(8,128)(2,1)S(1)} fusion(bf16[1024,512]{1,0:T(8,128)(2,1)} %bitcast.9, s32[1024]{0:T(1024)S(1)} %pad_clamp_fusion), kind=kCustom, calls=%fused_computation.3 | custom fusion | bytes 1050624 | tf_op jit(solution)/shard_map/gather | solution.py:162
  147.1 3.6 %fusion.3 = bf16[512,512]{1,0:T(8,128)(2,1)} fusion(bf16[512,2048]{1,0:T(8,128)(2,1)S(1)} %copy-done, bf16[2048,512]{1,0:T(8,128)(2,1)} %param.13, bf16[512,512]{1,0:T(8,128)(2,1)S(1)} %gather_fusion.3), kind=kOutput, calls=%fused_computation.128 | convolution fusion | flops 1074528256 | bytes 5242880 | tf_op jit(solution)/shard_map/dot_general | solution.py:174
  150.7 1.3 copy.80
  152.0 1.9 fusion.529
  153.9 1.8 copy.84
  155.7 1.8 copy.83
  157.5 1.8 copy.82
  159.2 30.4 %all-to-all-done.2 = bf16[16,64,2048]{2,1,0:T(8,128)(2,1)} async-done(((bf16[16,64,2048]{2,1,0:T(8,128)(2,1)}), bf16[16,64,2048]{2,1,0:T(8,128)(2,1)}, u32[]{:S(2)}, u32[]{:S(2)}) %all-to-all-start.2) | async-done | bytes 4194336 | tf_op jit(solution)/shard_map/all_to_all | solution.py:158
  189.6 8.0 %gather_fusion.5 = bf16[512,2048]{1,0:T(8,128)(2,1)} fusion(bf16[1024,2048]{1,0:T(8,128)(2,1)} %bitcast.19, s32[1024]{0:T(1024)S(1)} %pad_clamp_fusion), kind=kCustom, calls=%fused_computation.5 | custom fusion | bytes 4196352 | tf_op jit(solution)/shard_map/gather | solution.py:161
  197.5 9.7 %convert_add_fusion = f32[512,2048]{1,0:T(8,128)} fusion(bf16[512,2048]{1,0:T(8,128)(2,1)} %gather_fusion.5, bf16[512,2048]{1,0:T(8,128)(2,1)S(1)} %copy-done, bf16[2048,2048]{1,0:T(8,128)(2,1)} %param.11), kind=kOutput, calls=%fused_computation.68 | convolution fusion | flops 4297064448 | bytes 16777216 | tf_op jit(solution)/shard_map/dot_general | solution.py:163
  207.3 5.3 %copy.81 = f32[512,2048]{0,1:T(8,128)} copy(f32[512,2048]{1,0:T(8,128)} %convert_add_fusion) | data formatting | bytes 8388608 | tf_op jit(solution)/shard_map/add | solution.py:163
  212.6 2.9 %add_convert_fusion = (bf16[512,32,32]{0,2,1:T(8,128)(2,1)S(1)}, bf16[512,32,32]{0,2,1:T(8,128)(2,1)S(1)}) fusion(f32[512,32,64]{0,2,1:T(8,128)} %bitcast.785, f32[512,32]{0,1:T(8,128)S(1)} %get-tuple-element.17, f32[512,32]{0,1:T(8,128)S(1)} %get-tuple-element.16), kind=kLoop, calls=%fused_computation.121 | loop fusion | flops 4194304 | bytes 6422528 | tf_op jit(solution)/shard_map/convert.33
  218.1 1.0 fusion.539
  219.1 1.1 fusion.540
  220.2 1.1 fusion.541
  221.3 1.1 fusion.542
  222.4 1.1 fusion.543
  223.5 1.1 fusion.544
  224.6 1.1 fusion.545
  225.6 1.0 fusion.546
  226.7 1.1 fusion.547
  227.7 1.1 fusion.548
  228.8 1.1 fusion.549
  229.8 1.1 fusion.550
  230.9 1.1 fusion.551
  231.9 1.1 fusion.552
  233.0 1.1 fusion.553
  234.1 1.1 fusion.554
  235.1 1.1 fusion.555
  236.2 1.1 fusion.556
  237.3 1.1 fusion.557
  238.3 1.1 fusion.558
  239.4 1.1 fusion.559
  240.5 1.1 fusion.560
  245.1 0.8 copy-done.26
  245.9 2.1 copy.88
  248.1 1.0 fusion.136
  249.2 1.0 fusion.138
  250.3 1.0 fusion.140
  252.9 0.8 copy-done.27
  253.7 2.1 copy.87
  255.9 1.0 fusion.120
  257.0 1.0 fusion.122
  258.1 1.0 fusion.124
  261.5 2.1 copy.86
  267.0 1.4 copy.85
  268.4 2.9 %pad_maximum_fusion.1 = bf16[512,2048]{1,0:T(8,128)(2,1)} fusion(bf16[128,2048]{1,0:T(8,128)(2,1)} %copy.88, bf16[128,2048]{1,0:T(8,128)(2,1)} %copy.87, bf16[128,2048]{1,0:T(8,128)(2,1)} %copy.86, bf16[128,2048]{1,0:T(8,128)(2,1)S(1)} %copy.85), kind=kLoop, calls=%fused_computation.120 | loop fusion | flops 8388608 | bytes 4194304 | tf_op jit(solution)/shard_map/concatenate | solution.py:106
  (188 shorter events, 20.3 us)
Async XLA Ops:
  6.5 4.1 %copy-start = (bf16[512,2048]{1,0:T(8,128)(2,1)S(1)}, bf16[512,2048]{1,0:T(8,128)(2,1)}, u32[]{:S(2)}) copy-start(bf16[512,2048]{1,0:T(8,128)(2,1)} %param.10) | copy-start | bytes 6291460
  6.5 98.7 %all-gather.4.cloned.1.call-start = ((), (), s32[]{:S(2)}) async-start(), calls=%async_computation.3 | async-start | bytes 4718592 | tf_op jit(solution)/shard_map/all_gather | solution.py:148
  21.3 9.0 %copy-start.32 = (bf16[32,16,64]{2,1,0:T(8,128)(2,1)S(1)}, bf16[32,16,64]{2,1,0:T(8,128)(2,1)}, u32[]{:S(2)}) copy-start(bf16[32,16,64]{2,1,0:T(8,128)(2,1)} %param.16) | copy-start | bytes 196612
  21.3 88.1 %all-to-all-start = ((bf16[16,64,2048]{2,1,0:T(8,128)(2,1)}), bf16[16,64,2048]{2,1,0:T(8,128)(2,1)}, u32[]{:S(2)}, u32[]{:S(2)}) async-start(bf16[16,64,2048]{2,1,0:T(8,128)(2,1)} %broadcast_select_fusion), calls=%async_computation | async-start | bytes 8388608 | tf_op jit(solution)/shard_map/all_to_all | solution.py:155
  29.6 90.1 %all-gather.6.cloned.1.call-start = ((), (), s32[]{:S(2)}) async-start(), calls=%async_computation.4 | async-start | bytes 2359296 | tf_op jit(solution)/shard_map/all_gather | solution.py:149
  30.6 24.6 %copy-start.35 = (s32[1,16]{1,0:T(1,128)S(1)}, s32[1,16]{1,0:T(1,128)}, u32[]{:S(2)}) copy-start(s32[1,16]{1,0:T(1,128)} %param.18) | copy-start | bytes 196
  30.6 73.4 %copy-start.33 = (s32[512]{0:T(512)S(1)}, s32[512]{0:T(512)}, u32[]{:S(2)}) copy-start(s32[512]{0:T(512)} %param.17) | copy-start | bytes 6148
  115.0 18.8 %all-to-all-start.1 = ((bf16[16,64,512]{2,1,0:T(8,128)(2,1)}), bf16[16,64,512]{2,1,0:T(8,128)(2,1)}, u32[]{:S(2)}, u32[]{:S(2)}) async-start(bf16[16,64,512]{2,1,0:T(8,128)(2,1)} %convolution_convert_fusion.1), calls=%async_computation.1 | async-start | bytes 2097152 | tf_op jit(solution)/shard_map/all_to_all | solution.py:159
  133.8 55.8 %all-to-all-start.2 = ((bf16[16,64,2048]{2,1,0:T(8,128)(2,1)}), bf16[16,64,2048]{2,1,0:T(8,128)(2,1)}, u32[]{:S(2)}, u32[]{:S(2)}) async-start(bf16[16,64,2048]{2,1,0:T(8,128)(2,1)} %convolution_convert_fusion), calls=%async_computation.2 | async-start | bytes 8388608 | tf_op jit(solution)/shard_map/all_to_all | solution.py:158
  138.8 3.4 %copy-start.34 = (s32[512]{0:T(512)}, s32[512]{0:T(512)S(1)}, u32[]{:S(2)}) copy-start(s32[512]{0:T(512)S(1)} %iota.56) | copy-start | bytes 6148
  142.2 1.3 copy-start.36
  142.2 1.3 slice-start
  234.1 1.1 copy-start.2
  241.8 1.0 copy-start.31
  244.2 3.7 %copy-start.24 = (f32[4,128,192]{1,2,0:T(8,128)S(1)}, f32[4,128,192]{1,2,0:T(8,128)}, u32[]{:S(2)}) copy-start(f32[4,128,192]{1,2,0:T(8,128)} %get-tuple-element.43) | copy-start | bytes 1179652
  244.5 4.5 %copy-start.23 = (f32[4,128,192]{1,2,0:T(8,128)S(1)}, f32[4,128,192]{1,2,0:T(8,128)}, u32[]{:S(2)}) copy-start(f32[4,128,192]{1,2,0:T(8,128)} %get-tuple-element.45) | copy-start | bytes 1179652
  244.9 5.3 %copy-start.22 = (f32[4,128,192]{1,2,0:T(8,128)S(1)}, f32[4,128,192]{1,2,0:T(8,128)}, u32[]{:S(2)}) copy-start(f32[4,128,192]{1,2,0:T(8,128)} %get-tuple-element.47) | copy-start | bytes 1179652
  245.1 0.8 copy-start.26
  245.9 5.4 %copy-start.21 = (f32[4,128,192]{1,2,0:T(8,128)S(1)}, f32[4,128,192]{1,2,0:T(8,128)}, u32[]{:S(2)}) copy-start(f32[4,128,192]{1,2,0:T(8,128)} %get-tuple-element.49) | copy-start | bytes 1179652
  248.0 3.4 %copy-start.30 = (bf16[192,512]{0,1:T(8,128)(2,1)S(1)}, bf16[192,512]{0,1:T(8,128)(2,1)}, u32[]{:S(2)}) copy-start(bf16[192,512]{0,1:T(8,128)(2,1)} %copy.83) | copy-start | bytes 589828
  248.0 3.6 %copy-start.20 = (f32[4,128,192]{1,2,0:T(8,128)S(1)}, f32[4,128,192]{1,2,0:T(8,128)}, u32[]{:S(2)}) copy-start(f32[4,128,192]{1,2,0:T(8,128)} %get-tuple-element.51) | copy-start | bytes 1179652
  249.1 2.8 %copy-start.19 = (f32[4,128,192]{1,2,0:T(8,128)S(1)}, f32[4,128,192]{1,2,0:T(8,128)}, u32[]{:S(2)}) copy-start(f32[4,128,192]{1,2,0:T(8,128)} %get-tuple-element.53) | copy-start | bytes 1179652
  250.3 2.0 copy-start.18
  251.4 1.2 copy-start.17
  252.0 3.8 %copy-start.16 = (f32[4,128,192]{1,2,0:T(8,128)S(1)}, f32[4,128,192]{1,2,0:T(8,128)}, u32[]{:S(2)}) copy-start(f32[4,128,192]{1,2,0:T(8,128)} %get-tuple-element.59) | copy-start | bytes 1179652
  252.3 4.5 %copy-start.15 = (f32[4,128,192]{1,2,0:T(8,128)S(1)}, f32[4,128,192]{1,2,0:T(8,128)}, u32[]{:S(2)}) copy-start(f32[4,128,192]{1,2,0:T(8,128)} %get-tuple-element.61) | copy-start | bytes 1179652
  252.6 5.3 %copy-start.14 = (f32[4,128,192]{1,2,0:T(8,128)S(1)}, f32[4,128,192]{1,2,0:T(8,128)}, u32[]{:S(2)}) copy-start(f32[4,128,192]{1,2,0:T(8,128)} %get-tuple-element.63) | copy-start | bytes 1179652
  252.9 0.8 copy-start.27
  253.7 5.4 %copy-start.13 = (f32[4,128,192]{1,2,0:T(8,128)S(1)}, f32[4,128,192]{1,2,0:T(8,128)}, u32[]{:S(2)}) copy-start(f32[4,128,192]{1,2,0:T(8,128)} %get-tuple-element.65) | copy-start | bytes 1179652
  255.8 3.4 %copy-start.29 = (bf16[192,512]{0,1:T(8,128)(2,1)S(1)}, bf16[192,512]{0,1:T(8,128)(2,1)}, u32[]{:S(2)}) copy-start(bf16[192,512]{0,1:T(8,128)(2,1)} %copy.82) | copy-start | bytes 589828
  255.9 3.6 %copy-start.12 = (f32[4,128,192]{1,2,0:T(8,128)S(1)}, f32[4,128,192]{1,2,0:T(8,128)}, u32[]{:S(2)}) copy-start(f32[4,128,192]{1,2,0:T(8,128)} %get-tuple-element.67) | copy-start | bytes 1179652
  257.0 2.8 copy-start.11
  258.1 2.0 copy-start.10
  259.2 1.2 copy-start.9
  259.8 3.8 %copy-start.8 = (f32[4,128,192]{1,2,0:T(8,128)S(1)}, f32[4,128,192]{1,2,0:T(8,128)}, u32[]{:S(2)}) copy-start(f32[4,128,192]{1,2,0:T(8,128)} %get-tuple-element.75) | copy-start | bytes 1179652
  260.1 3.7 %copy-start.7 = (f32[4,128,192]{1,2,0:T(8,128)S(1)}, f32[4,128,192]{1,2,0:T(8,128)}, u32[]{:S(2)}) copy-start(f32[4,128,192]{1,2,0:T(8,128)} %get-tuple-element.77) | copy-start | bytes 1179652
  260.7 0.8 copy-start.28
  261.5 2.7 copy-start.6
  263.6 1.0 copy-start.5
  263.9 1.0 copy-start.4
  264.2 1.1 copy-start.3
  266.2 0.8 copy-start.25
  267.0 4.3 %copy-start.1 = (bf16[512,2048]{1,0:T(8,128)(2,1)S(1)}, bf16[512,2048]{1,0:T(8,128)(2,1)}, u32[]{:S(2)}) copy-start(bf16[512,2048]{1,0:T(8,128)(2,1)} %param.10) | copy-start | bytes 6291460
Sparse Core Ops, SparseCore 0:
  9.0 44.3 all-gather.3
  55.1 27.0 all-gather.5
where the time goes:
time: 279 us; the launch traced here: 278 us
  blocking collectives  70.2 us (25%)
  matrix products  64.4 us (23%)
  local copies, waits for them, and re-layouts  55.3 us (20%)
  waiting for transfers between devices  38.3 us (14%)
  other arithmetic  17.9 us (6%)
  starting transfers between devices  17.6 us (6%)
  between operations  14.4 us (5%)
    all_gather x1, blocking collectives, local(): lax.all_gather(adapter_per_request, 'store', axis=0, tiled=True)  48.8 us
    all_to_all x1, waiting for transfers between devices, local(): lax.all_to_all(query_update, 'store', split_axis=0, concat_axis=0, tiled=...  30.4 us
    dot_general x32, matrix products, attention(): jnp.einsum('qhd,kd->hqk', query_part, key_part, preferred_element_type=jn...  26.6 us
    all_gather x1, blocking collectives, local(): lax.all_gather(adapter_up_value_weight, 'serve', axis=2, tiled=True)  21.4 us
    dot_general x32, matrix products, attention(): jnp.einsum('hqk,kd->qhd', weights, value_part, preferred_element_type=jnp...  11.5 us
    dot_general x1, matrix products, local(): jnp.dot(normalized_hidden_states, query_weight_matrix, preferred_element_...  9.7 us
    all_to_all x1, starting transfers between devices, local(): lax.all_to_all(block_list, 'store', split_axis=0, concat_axis=0, tiled=True)  8.28 us
    gather x1, local copies, waits for them, and re-layouts, local(): delta_query = query_update.reshape(-1, query_update.shape[2])[back_index]  7.95 us
  transfers between devices with their start and end apart: 5, of which 2 were waited for; matrix products, arithmetic and copies ran while one was open for 20% of the time, Pallas kernels for 0%

commit v1 on v0

--- a/solution.py
+++ b/solution.py
@@ -118,11 +118,34 @@
     adapter_per_request,
     request_token_length,
 ):
+    axes = ("serve", "store")
+    serve_count = lax.axis_size("serve")
     store_count = lax.axis_size("store")
     my_store = lax.axis_index("store")
-    tok_rows = normalized_hidden_states.shape[0]
+    tok_rows, width = normalized_hidden_states.shape
     request_count = request_token_length.shape[1]
-    group_lists = lax.all_gather(adapter_per_request, "store", axis=0, tiled=True)
+    adp_dev, rank2, cols = adapter_down_weight.shape
+    vcols = adapter_up_value_weight.shape[2]
+    all_lists = lax.all_gather(adapter_per_request, axes, axis=0, tiled=True)
+    all_slots = table_lookup(adapter_panel_slot, all_lists)
+    mine = all_slots // ADP_DEV == my_store
+    local_pick = jnp.sum(jnp.where(mine, all_slots % ADP_DEV, 0), axis=1)
+    send = jnp.concatenate(
+        [
+            jnp.take(adapter_down_weight, local_pick, axis=0).reshape(local_pick.shape[0], -1),
+            jnp.take(adapter_up_query_weight, local_pick, axis=0).reshape(local_pick.shape[0], -1),
+            jnp.take(adapter_up_value_weight, local_pick, axis=0).reshape(local_pick.shape[0], -1),
+        ],
+        axis=1,
+    )
+    got = lax.all_to_all(send, axes, split_axis=0, concat_axis=0, tiled=True)
+    got = got.reshape(serve_count, store_count, -1)
+    n_down = rank2 * cols
+    n_upq = ADAPTER_RANK * cols
+    down = got[:, :, :n_down].reshape(serve_count, store_count, rank2, cols)
+    upq = got[:, :, n_down : n_down + n_upq].reshape(serve_count, store_count, ADAPTER_RANK, cols)
+    upv = got[:, :, n_down + n_upq :].reshape(serve_count, store_count, ADAPTER_RANK, vcols)
+
     lengths = request_token_length[0]
     adapters = adapter_per_request[0]
     request_ends = jnp.cumsum(lengths)
@@ -131,35 +154,22 @@
     request_ids = jnp.sum((token_order[:, None] >= request_ends[None, :]).astype(jnp.int32), axis=1)
     member = request_ids[:, None] == jnp.arange(request_count, dtype=jnp.int32)[None, :]
     positions = token_order - jnp.sum(jnp.where(member, starts[None, :], 0), axis=1)
-    slot_index_list = table_lookup(adapter_panel_slot, adapters)
-    owners = slot_index_list // ADP_DEV
-    owner_pick = owners[None, :] == jnp.arange(store_count, dtype=jnp.int32)[:, None]
-    start_for = jnp.sum(jnp.where(owner_pick, starts[None, :], 0), axis=1)
-    length_for = jnp.sum(jnp.where(owner_pick, lengths[None, :], 0), axis=1)
-    offsets = jnp.arange(LEN_MAX, dtype=jnp.int32)
-    valid_rows = offsets[None, :] < length_for[:, None]
-    row_index = jnp.where(valid_rows, start_for[:, None] + offsets[None, :], 0)
-    block_list = jnp.where(
-        valid_rows[..., None], normalized_hidden_states[row_index], jnp.zeros((), jnp.bfloat16)
-    )
+    owners = table_lookup(adapter_panel_slot, adapters) // ADP_DEV
     owner_token = jnp.sum(jnp.where(member, owners[None, :], 0), axis=1)
-    back_index = owner_token * LEN_MAX + positions
-    panels = (
-        lax.all_gather(adapter_down_weight, "serve", axis=2, tiled=True),
-        lax.all_gather(adapter_up_query_weight, "serve", axis=2, tiled=True),
-        lax.all_gather(adapter_up_value_weight, "serve", axis=2, tiled=True),
-    )
-    down_chosen, upq_chosen, upv_chosen = local_choice(
-        panels, group_lists, adapter_panel_slot, my_store
-    )
-    arrived = lax.all_to_all(block_list, "store", split_axis=0, concat_axis=0, tiled=True)
-    query_update, value_update = reduced_rank_products(arrived, down_chosen, upq_chosen, upv_chosen)
-    query_update, value_update = (
-        lax.all_to_all(query_update, "store", split_axis=0, concat_axis=0, tiled=True),
-        lax.all_to_all(value_update, "store", split_axis=0, concat_axis=0, tiled=True),
-    )
-    delta_query = query_update.reshape(-1, query_update.shape[2])[back_index]
-    delta_value = value_update.reshape(-1, value_update.shape[2])[back_index]
+
+    states3 = normalized_hidden_states.reshape(tok_rows, serve_count, cols)
+    low = jnp.einsum(
+        "tsf,sorf->tor", states3, down, preferred_element_type=jnp.float32
+    ).astype(jnp.bfloat16)
+    owner_mask = owner_token[:, None, None] == jnp.arange(store_count, dtype=jnp.int32)[None, :, None]
+    low = jnp.where(owner_mask, low, jnp.zeros((), jnp.bfloat16))
+    delta_query = jnp.einsum(
+        "tor,sorf->tsf", low[..., :ADAPTER_RANK], upq, preferred_element_type=jnp.float32
+    ).astype(jnp.bfloat16).reshape(tok_rows, serve_count * cols)
+    delta_value = jnp.einsum(
+        "tor,sorf->tsf", low[..., ADAPTER_RANK:], upv, preferred_element_type=jnp.float32
+    ).astype(jnp.bfloat16).reshape(tok_rows, serve_count * vcols)
+
     base_query = jnp.dot(
         normalized_hidden_states, query_weight_matrix, preferred_element_type=jnp.float32
     ) + delta_query.astype(jnp.float32)

time: 279 us -> 264 us (0.946)
  the two profiles are of different devices: /device:TPU:6 before, /device:TPU:1 now
where the time goes in v1:
time: 264 us; the launch traced here: 262 us
  local copies, waits for them, and re-layouts  77.6 us (29%)
  matrix products  62.8 us (24%)
  blocking collectives  47.9 us (18%)
  waiting for transfers between devices  37.8 us (14%)
  other arithmetic  28.1 us (11%)
  starting transfers between devices  6.88 us (3%)
    all_gather x1, blocking collectives, local(): all_lists = lax.all_gather(adapter_per_request, axes, axis=0, tiled=True)  47.9 us
    unnamed x103, local copies, waits for them, and re-layouts  44.9 us
    all_to_all x1, waiting for transfers between devices, local(): got = lax.all_to_all(send, axes, split_axis=0, concat_axis=0, tiled=True)  37.8 us
    dot_general x32, matrix products, attention(): jnp.einsum('qhd,kd->hqk', query_part, key_part, preferred_element_type=jn...  31.1 us
    dot_general x1, matrix products, local(): jnp.dot(normalized_hidden_states, query_weight_matrix, preferred_element_...  11.6 us
    dot_general x32, matrix products, attention(): jnp.einsum('hqk,kd->qhd', weights, value_part, preferred_element_type=jnp...  11.1 us
    all_to_all x2, other arithmetic, local(): got = lax.all_to_all(send, axes, split_axis=0, concat_axis=0, tiled=True)  7.74 us
    convert_element_type x4, local copies, waits for them, and re-layouts, attention(): outputs.append(jnp.concatenate(pieces, axis=1).reshape(block_rows, HEADS...  6.88 us
  transfers between devices with their start and end apart: 1, of which 1 were waited for; matrix products, arithmetic and copies ran while one was open for 2% of the time, Pallas kernels for 0%

profile of v1, /device:TPU:1, one launch (start us, length us, event | category | flops | bytes accessed | tf_op | source)
XLA Modules:
  0.0 262.2 jit_solution(4690640498416728409)
XLA Ops:
  0.0 47.9 %all-gather = s32[128,1,16]{2,1,0:T(1,128)S(1)} all-gather(s32[1,1,16]{2,1,0:T(1,128)} %bitcast.942), channel_id=1, replica_groups=mesh['serve'=8,'store'=16] {'serve','store'}, dimensions={0}, use_global_device_ids=true | all-gather | bytes 8256 | tf_op jit(solution)/shard_map/all_gather | solution.py:129
  48.0 3.3 %select_reduce_fusion = s32[128,16]{1,0:T(8,128)S(1)} fusion(s32[512]{0:T(512)} %param.17, s32[128,16]{1,0:T(8,128)S(1)} %bitcast.909), kind=kLoop, calls=%fused_computation.66 | loop fusion | flops 3143680 | bytes 18432 | tf_op jit(solution)/shard_map/reduce_sum | solution.py:33
  51.5 1.6 gather_fusion.2
  53.7 1.6 gather_fusion.1
  55.4 1.7 copy.139
  57.1 1.2 broadcast_select_fusion.1
  58.2 2.0 gather_fusion
  60.2 3.0 %copy.138 = bf16[16,8,32,256]{3,1,2,0:T(8,128)(2,1)S(1)} copy(bf16[16,8,32,256]{3,2,1,0:T(8,128)(2,1)} %bitcast.874) | data formatting | bytes 4194304
  64.5 1.9 maximum_bitcast_fusion
  66.9 5.9 %reduce.2 = bf16[128,13312]{1,0:T(8,128)(2,1)} reduce(bf16[128,1,13312]{2,0,1:T(8,128)(2,1)} %maximum_bitcast_fusion, bf16[]{:T(256)} %broadcast.452), dimensions={1}, to_apply=%copy.116.reduce_sub_computation | reduce | bytes 6815746 | tf_op jit(solution)/shard_map/all_to_all | solution.py:141
  72.7 8.4 %reshape.579 = bf16[128,2,6656]{2,1,0:T(2,128)(2,1)} reshape(bf16[128,13312]{1,0:T(8,128)(2,1)} %reduce.2) | data formatting | bytes 6815744
  81.2 6.9 %all-to-all-start = ((bf16[128,2,6656]{2,1,0:T(2,128)(2,1)}), bf16[128,2,6656]{2,1,0:T(2,128)(2,1)}, u32[]{:S(2)}, u32[]{:S(2)}) async-start(bf16[128,2,6656]{2,1,0:T(2,128)(2,1)} %reshape.579), calls=%async_computation | async-start | bytes 6815744 | tf_op jit(solution)/shard_map/all_to_all | solution.py:141
  89.3 2.9 %fusion.562 = f32[512,512]{0,1:T(8,128)S(1)} fusion(bf16[512,2048]{1,0:T(8,128)(2,1)} %param.10, bf16[2048,512]{1,0:T(8,128)(2,1)S(1)} %copy-done), kind=kOutput, calls=%fused_computation.754 | convolution fusion | flops 1073741824 | bytes 5242880 | tf_op jit(solution)/shard_map/dot_general | solution.py:179
  93.2 37.8 %all-to-all-done = bf16[128,2,6656]{2,1,0:T(2,128)(2,1)} async-done(((bf16[128,2,6656]{2,1,0:T(2,128)(2,1)}), bf16[128,2,6656]{2,1,0:T(2,128)(2,1)}, u32[]{:S(2)}, u32[]{:S(2)}) %all-to-all-start) | async-done | bytes 3407904 | tf_op jit(solution)/shard_map/all_to_all | solution.py:141
  131.0 19.9 %reshape.580 = bf16[128,1,13312]{2,1,0:T(2,128)(2,1)} reshape(bf16[128,2,6656]{2,1,0:T(2,128)(2,1)} %all-to-all-done) | data formatting | bytes 6815744
  151.0 4.0 %copy.135 = bf16[128,1,13312]{2,0,1:T(8,128)(2,1)S(1)} copy(bf16[128,1,13312]{2,1,0:T(2,128)(2,1)} %reshape.580) | data formatting | bytes 6815744
  155.0 1.5 slice.592
  156.9 2.3 copy.140
  159.2 1.3 fusion.174
  161.3 1.1 bitcast_convert_fusion.2
  162.5 2.5 copy.119
  165.0 3.7 %fusion.9 = bf16[512,512]{1,0:T(8,128)(2,1)S(1)} fusion(f32[512,512]{1,0:T(8,128)} %copy.119, bf16[512,2048]{1,0:T(8,128)(2,1)} %param.10, bf16[2048,512]{1,0:T(8,128)(2,1)} %param.13), kind=kOutput, calls=%fused_computation.132 | convolution fusion | flops 1074266112 | bytes 5767168 | tf_op jit(solution)/shard_map/dot_general | solution.py:184
  171.0 2.7 %bitcast_convert_fusion.1 = f32[512,2048]{0,1:T(8,128)} fusion(bf16[512,8,256]{0,2,1:T(8,128)(2,1)S(1)} %bitcast_convert_fusion), kind=kLoop, calls=%fused_computation.124 | loop fusion | flops 1048576 | bytes 6291456 | tf_op jit(solution)/shard_map/convert_element_type | solution.py:175
  173.6 5.4 %copy.134 = f32[512,2048]{1,0:T(8,128)} copy(f32[512,2048]{0,1:T(8,128)} %bitcast_convert_fusion.1) | data formatting | bytes 8388608 | tf_op jit(solution)/shard_map/convert_element_type | solution.py:175
  179.0 11.6 %convolution_add_fusion = f32[512,2048]{1,0:T(8,128)} fusion(f32[512,2048]{1,0:T(8,128)} %copy.134, bf16[512,2048]{1,0:T(8,128)(2,1)} %param.10, bf16[2048,2048]{1,0:T(8,128)(2,1)} %param.11), kind=kOutput, calls=%fused_computation.69 | convolution fusion | flops 4296015872 | bytes 18874368 | tf_op jit(solution)/shard_map/dot_general | solution.py:173
  190.7 5.3 %copy.122 = f32[512,2048]{0,1:T(8,128)} copy(f32[512,2048]{1,0:T(8,128)} %convolution_add_fusion) | data formatting | bytes 8388608 | tf_op jit(solution)/shard_map/add | solution.py:173
  196.0 2.9 %add_convert_fusion = (bf16[512,32,32]{0,2,1:T(8,128)(2,1)S(1)}, bf16[512,32,32]{0,2,1:T(8,128)(2,1)S(1)}) fusion(f32[512,32,64]{0,2,1:T(8,128)} %bitcast.868, f32[512,32]{0,1:T(8,128)S(1)} %get-tuple-element.15, f32[512,32]{0,1:T(8,128)S(1)} %get-tuple-element.14), kind=kLoop, calls=%fused_computation.125 | loop fusion | flops 4194304 | bytes 6422528 | tf_op jit(solution)/shard_map/convert.35
  199.0 1.1 fusion.554
  200.0 1.1 fusion.555
  201.1 1.1 fusion.556
  202.1 1.1 fusion.557
  204.5 1.1 fusion.546
  205.6 1.1 fusion.547
  206.6 1.1 fusion.548
  207.7 1.1 fusion.549
  208.7 1.0 fusion.550
  209.8 1.1 fusion.551
  210.9 1.1 fusion.552
  212.0 1.1 fusion.553
  214.1 1.0 fusion.539
  215.1 1.0 fusion.540
  216.2 1.1 fusion.541
  217.3 1.1 fusion.542
  218.3 1.1 fusion.543
  219.4 1.1 fusion.544
  220.5 1.1 fusion.545
  221.5 1.1 fusion.530
  222.6 1.1 fusion.531
  223.6 1.1 fusion.532
  224.7 1.1 fusion.533
  225.8 1.1 fusion.534
  226.8 1.1 fusion.535
  227.9 1.1 fusion.537
  229.0 1.1 fusion.536
  230.0 1.8 copy.123
  232.9 1.2 fusion.178
  234.0 1.2 fusion.111
  235.2 1.1 fusion.180
  236.3 1.2 fusion.113
  240.2 1.3 copy.126
  244.8 1.3 copy.127
  251.9 2.1 copy.128
  257.3 2.2 copy.129
  259.5 2.7 %pad_maximum_fusion.1 = bf16[512,2048]{1,0:T(8,128)(2,1)} fusion(bf16[128,2048]{1,0:T(8,128)(2,1)} %copy.129, bf16[128,2048]{1,0:T(8,128)(2,1)} %copy.128, bf16[128,2048]{1,0:T(8,128)(2,1)S(1)} %copy.127, bf16[128,2048]{1,0:T(8,128)(2,1)S(1)} %copy.126), kind=kLoop, calls=%fused_computation.123 | loop fusion | flops 8388608 | bytes 4194304 | tf_op jit(solution)/shard_map/concatenate | solution.py:106
  (210 shorter events, 25.8 us)
Async XLA Ops:
  0.0 89.3 %copy-start = (bf16[2048,512]{1,0:T(8,128)(2,1)S(1)}, bf16[2048,512]{1,0:T(8,128)(2,1)}, u32[]{:S(2)}) copy-start(bf16[2048,512]{1,0:T(8,128)(2,1)} %param.12) | copy-start | bytes 6291460
  0.0 53.7 %copy-start.3 = (bf16[32,16,256]{2,1,0:T(8,128)(2,1)S(1)}, bf16[32,16,256]{2,1,0:T(8,128)(2,1)}, u32[]{:S(2)}) copy-start(bf16[32,16,256]{2,1,0:T(8,128)(2,1)} %param.15) | copy-start | bytes 786436
  55.4 2.9 %copy-start.2 = (bf16[32,32,256]{2,1,0:T(8,128)(2,1)S(1)}, bf16[32,32,256]{2,1,0:T(8,128)(2,1)}, u32[]{:S(2)}) copy-start(bf16[32,32,256]{2,1,0:T(8,128)(2,1)} %param.14) | copy-start | bytes 1572868
  63.2 1.2 copy-start.4
  81.2 7.2 %copy-start.46 = (s32[1,16]{1,0:T(1,128)S(1)}, s32[1,16]{1,0:T(1,128)}, u32[]{:S(2)}) copy-start(s32[1,16]{1,0:T(1,128)} %param.19) | copy-start | bytes 196
  81.2 7.5 %copy-start.42 = (s32[512]{0:T(512)S(1)}, s32[512]{0:T(512)}, u32[]{:S(2)}) copy-start(s32[512]{0:T(512)} %param.17) | copy-start | bytes 6148
  81.2 7.5 %copy-start.43 = (s32[1,16]{1,0:T(1,128)S(1)}, s32[1,16]{1,0:T(1,128)}, u32[]{:S(2)}) copy-start(s32[1,16]{1,0:T(1,128)} %param.18) | copy-start | bytes 196
  81.2 49.9 %all-to-all-start = ((bf16[128,2,6656]{2,1,0:T(2,128)(2,1)}), bf16[128,2,6656]{2,1,0:T(2,128)(2,1)}, u32[]{:S(2)}, u32[]{:S(2)}) async-start(bf16[128,2,6656]{2,1,0:T(2,128)(2,1)} %reshape.579), calls=%async_computation | async-start | bytes 6815744 | tf_op jit(solution)/shard_map/all_to_all | solution.py:141
  88.3 3.9 %copy-start.44 = (s32[512]{0:T(512)}, s32[512]{0:T(512)S(1)}, u32[]{:S(2)}) copy-start(s32[512]{0:T(512)S(1)} %iota.43) | copy-start | bytes 6148
  92.2 0.7 copy-start.45
  92.2 0.7 slice-start
  156.9 2.4 copy-start.47
  160.5 0.8 copy-start.37
  169.0 1.3 copy-start.38
  229.0 2.9 %copy-start.32 = (bf16[192,512]{1,0:T(8,128)(2,1)S(1)}, bf16[192,512]{1,0:T(8,128)(2,1)}, u32[]{:S(2)}) copy-start(bf16[192,512]{1,0:T(8,128)(2,1)} %get-tuple-element.12) | copy-start | bytes 589828
  229.0 3.7 %copy-start.31 = (bf16[192,512]{1,0:T(8,128)(2,1)S(1)}, bf16[192,512]{1,0:T(8,128)(2,1)}, u32[]{:S(2)}) copy-start(bf16[192,512]{1,0:T(8,128)(2,1)} %get-tuple-element.13) | copy-start | bytes 589828
  230.0 7.5 %copy-start.6 = (f32[4,128,192]{1,2,0:T(8,128)S(1)}, f32[4,128,192]{1,2,0:T(8,128)}, u32[]{:S(2)}) copy-start(f32[4,128,192]{1,2,0:T(8,128)} %get-tuple-element.77) | copy-start | bytes 1179652
  232.8 14.6 %copy-start.40 = (bf16[192,512]{0,1:T(8,128)(2,1)}, bf16[192,512]{0,1:T(8,128)(2,1)S(1)}, u32[]{:S(2)}) copy-start(bf16[192,512]{0,1:T(8,128)(2,1)S(1)} %copy.124) | copy-start | bytes 589828
  232.9 5.0 %copy-start.5 = (f32[4,128,192]{1,2,0:T(8,128)S(1)}, f32[4,128,192]{1,2,0:T(8,128)}, u32[]{:S(2)}) copy-start(f32[4,128,192]{1,2,0:T(8,128)} %get-tuple-element.79) | copy-start | bytes 1179652
  238.8 2.8 %copy-start.30 = (f32[4,128,192]{1,2,0:T(8,128)S(1)}, f32[4,128,192]{1,2,0:T(8,128)}, u32[]{:S(2)}) copy-start(f32[4,128,192]{1,2,0:T(8,128)} %get-tuple-element.57) | copy-start | bytes 1179652
  238.8 2.8 %copy-start.41 = (bf16[192,512]{0,1:T(8,128)(2,1)S(1)}, bf16[192,512]{0,1:T(8,128)(2,1)}, u32[]{:S(2)}) copy-start(bf16[192,512]{0,1:T(8,128)(2,1)} %copy.123) | copy-start | bytes 589828
  238.9 3.0 %copy-start.29 = (f32[4,128,192]{1,2,0:T(8,128)S(1)}, f32[4,128,192]{1,2,0:T(8,128)}, u32[]{:S(2)}) copy-start(f32[4,128,192]{1,2,0:T(8,128)} %get-tuple-element.59) | copy-start | bytes 1179652
  239.2 3.0 %copy-start.28 = (f32[4,128,192]{1,2,0:T(8,128)S(1)}, f32[4,128,192]{1,2,0:T(8,128)}, u32[]{:S(2)}) copy-start(f32[4,128,192]{1,2,0:T(8,128)} %get-tuple-element.61) | copy-start | bytes 1179652
  239.4 0.8 copy-start.33
  240.2 2.2 copy-start.27
  241.6 1.2 copy-start.26
  241.9 1.2 copy-start.25
  242.3 1.2 copy-start.24
  242.6 1.2 copy-start.23
  243.2 2.9 %copy-start.22 = (f32[4,128,192]{1,2,0:T(8,128)S(1)}, f32[4,128,192]{1,2,0:T(8,128)}, u32[]{:S(2)}) copy-start(f32[4,128,192]{1,2,0:T(8,128)} %get-tuple-element.41) | copy-start | bytes 1179652
  243.5 2.9 %copy-start.21 = (f32[4,128,192]{1,2,0:T(8,128)S(1)}, f32[4,128,192]{1,2,0:T(8,128)}, u32[]{:S(2)}) copy-start(f32[4,128,192]{1,2,0:T(8,128)} %get-tuple-element.43) | copy-start | bytes 1179652
  243.8 2.9 %copy-start.20 = (f32[4,128,192]{1,2,0:T(8,128)S(1)}, f32[4,128,192]{1,2,0:T(8,128)}, u32[]{:S(2)}) copy-start(f32[4,128,192]{1,2,0:T(8,128)} %get-tuple-element.45) | copy-start | bytes 1179652
  244.0 0.8 copy-start.34
  244.8 2.2 copy-start.19
  246.2 1.1 copy-start.18
  246.5 1.2 copy-start.17
  246.8 2.0 copy-start.16
  247.1 2.8 %copy-start.15 = (f32[4,128,192]{1,2,0:T(8,128)S(1)}, f32[4,128,192]{1,2,0:T(8,128)}, u32[]{:S(2)}) copy-start(f32[4,128,192]{1,2,0:T(8,128)} %get-tuple-element.55) | copy-start | bytes 1179652
  247.8 6.2 %copy-start.14 = (f32[4,128,192]{1,2,0:T(8,128)S(1)}, f32[4,128,192]{1,2,0:T(8,128)}, u32[]{:S(2)}) copy-start(f32[4,128,192]{1,2,0:T(8,128)} %get-tuple-element.25) | copy-start | bytes 1179652
  247.8 6.3 %copy-start.39 = (bf16[192,512]{0,1:T(8,128)(2,1)S(1)}, bf16[192,512]{0,1:T(8,128)(2,1)}, u32[]{:S(2)}) copy-start(bf16[192,512]{0,1:T(8,128)(2,1)} %copy.125) | copy-start | bytes 589828
  248.9 5.3 %copy-start.13 = (f32[4,128,192]{1,2,0:T(8,128)S(1)}, f32[4,128,192]{1,2,0:T(8,128)}, u32[]{:S(2)}) copy-start(f32[4,128,192]{1,2,0:T(8,128)} %get-tuple-element.27) | copy-start | bytes 1179652
  250.0 4.5 %copy-start.12 = (f32[4,128,192]{1,2,0:T(8,128)S(1)}, f32[4,128,192]{1,2,0:T(8,128)}, u32[]{:S(2)}) copy-start(f32[4,128,192]{1,2,0:T(8,128)} %get-tuple-element.29) | copy-start | bytes 1179652
  251.1 0.8 copy-start.35
  251.9 3.0 %copy-start.11 = (f32[4,128,192]{1,2,0:T(8,128)S(1)}, f32[4,128,192]{1,2,0:T(8,128)}, u32[]{:S(2)}) copy-start(f32[4,128,192]{1,2,0:T(8,128)} %get-tuple-element.31) | copy-start | bytes 1179652
  254.0 1.2 copy-start.10
  254.3 1.2 copy-start.9
  254.6 1.1 copy-start.7
  254.9 1.1 copy-start.8
  256.5 0.8 copy-start.36
  257.3 4.9 %copy-start.1 = (bf16[2048,512]{1,0:T(8,128)(2,1)S(1)}, bf16[2048,512]{1,0:T(8,128)(2,1)}, u32[]{:S(2)}) copy-start(bf16[2048,512]{1,0:T(8,128)(2,1)} %param.12) | copy-start | bytes 6291460

commit v2 on v1

--- a/solution.py
+++ b/solution.py
@@ -126,25 +126,22 @@
     request_count = request_token_length.shape[1]
     adp_dev, rank2, cols = adapter_down_weight.shape
     vcols = adapter_up_value_weight.shape[2]
-    all_lists = lax.all_gather(adapter_per_request, axes, axis=0, tiled=True)
+    device_total = serve_count * store_count
+    all_lists = lax.all_to_all(
+        jnp.broadcast_to(adapter_per_request, (device_total, request_count)), axes, 0, 0, tiled=True
+    )
     all_slots = table_lookup(adapter_panel_slot, all_lists)
     mine = all_slots // ADP_DEV == my_store
     local_pick = jnp.sum(jnp.where(mine, all_slots % ADP_DEV, 0), axis=1)
-    send = jnp.concatenate(
-        [
-            jnp.take(adapter_down_weight, local_pick, axis=0).reshape(local_pick.shape[0], -1),
-            jnp.take(adapter_up_query_weight, local_pick, axis=0).reshape(local_pick.shape[0], -1),
-            jnp.take(adapter_up_value_weight, local_pick, axis=0).reshape(local_pick.shape[0], -1),
-        ],
-        axis=1,
-    )
-    got = lax.all_to_all(send, axes, split_axis=0, concat_axis=0, tiled=True)
-    got = got.reshape(serve_count, store_count, -1)
-    n_down = rank2 * cols
-    n_upq = ADAPTER_RANK * cols
-    down = got[:, :, :n_down].reshape(serve_count, store_count, rank2, cols)
-    upq = got[:, :, n_down : n_down + n_upq].reshape(serve_count, store_count, ADAPTER_RANK, cols)
-    upv = got[:, :, n_down + n_upq :].reshape(serve_count, store_count, ADAPTER_RANK, vcols)
+    down = lax.all_to_all(
+        jnp.take(adapter_down_weight, local_pick, axis=0), axes, 0, 0, tiled=True
+    ).reshape(serve_count, store_count, rank2, cols)
+    upq = lax.all_to_all(
+        jnp.take(adapter_up_query_weight, local_pick, axis=0), axes, 0, 0, tiled=True
+    ).reshape(serve_count, store_count, ADAPTER_RANK, cols)
+    upv = lax.all_to_all(
+        jnp.take(adapter_up_value_weight, local_pick, axis=0), axes, 0, 0, tiled=True
+    ).reshape(serve_count, store_count, ADAPTER_RANK, vcols)
 
     lengths = request_token_length[0]
     adapters = adapter_per_request[0]

time: 264 us -> 240 us (0.909)
  blocking collectives: 47.9 us -> 0 us
  local copies, waits for them, and re-layouts: 77.6 us -> 42.9 us
  matrix products: 62.8 us -> 89.4 us
  starting transfers between devices: 6.88 us -> 25.8 us
  waiting for transfers between devices: 37.8 us -> 48.3 us
  other arithmetic: 28.1 us -> 31 us
    all_gather x1 -> x0, blocking collectives: 47.9 us -> none  [local(): all_lists = lax.all_gather(adapter_per_request, axes, axis=0, tiled=True)]
    unnamed x103 -> x137, local copies, waits for them, and re-layouts: 44.9 us -> 9.94 us
    dot_general x32, matrix products: 31.1 us -> 50.1 us  [attention(): jnp.einsum('qhd,kd->hqk', query_part, key_part, preferred_element_type=jn...]
    all_to_all x1 -> x4, starting transfers between devices: 6.88 us -> 25.8 us  [the longest x1 11.5 us: local(): lax.all_to_all(jnp.broadcast_to(adapter_per_request, (device_total, reque...]
    all_to_all x1 -> x4, waiting for transfers between devices: 37.8 us -> 48.3 us  [the longest x1 22.7 us: local(): lax.all_to_all(jnp.take(adapter_down_weight, local_pick, axis=0), axes, 0...]
    all_to_all x2 -> x0, other arithmetic: 7.74 us -> none  [local(): got = lax.all_to_all(send, axes, split_axis=0, concat_axis=0, tiled=True)]
    reduce_sum x32, other arithmetic: 4.54 us -> 10.8 us  [attention(): row_total = jnp.sum(raised, axis=-1)]
    dot_general x32, matrix products: 11.1 us -> 16.5 us  [attention(): jnp.einsum('hqk,kd->qhd', weights, value_part, preferred_element_type=jnp...]
  transfers between devices with their start and end apart: 1 -> 4, of which waited for: 1 -> 4; matrix products, arithmetic and copies ran while one was open for 2% -> 8% of each run, Pallas kernels for 0% -> 0%
where the time goes in v2:
time: 240 us; the launch traced here: 239 us
  matrix products  89.4 us (37%)
  waiting for transfers between devices  48.3 us (20%)
  local copies, waits for them, and re-layouts  42.9 us (18%)
  other arithmetic  31 us (13%)
  starting transfers between devices  25.8 us (11%)
    dot_general x32, matrix products, attention(): jnp.einsum('qhd,kd->hqk', query_part, key_part, preferred_element_type=jn...  50.1 us
    all_to_all x1, waiting for transfers between devices, local(): lax.all_to_all(jnp.take(adapter_down_weight, local_pick, axis=0), axes, 0...  22.7 us
    dot_general x32, matrix products, attention(): jnp.einsum('hqk,kd->qhd', weights, value_part, preferred_element_type=jnp...  16.5 us
    dot_general x1, matrix products, local(): jnp.dot(normalized_hidden_states, query_weight_matrix, preferred_element_...  11.6 us
    all_to_all x1, starting transfers between devices, local(): lax.all_to_all(jnp.broadcast_to(adapter_per_request, (device_total, reque...  11.5 us
    reduce_sum x32, other arithmetic, attention(): row_total = jnp.sum(raised, axis=-1)  10.8 us
    all_to_all x1, waiting for transfers between devices, local(): lax.all_to_all(jnp.take(adapter_up_query_weight, local_pick, axis=0), axe...  10 us
    unnamed x137, local copies, waits for them, and re-layouts  9.94 us
  transfers between devices with their start and end apart: 4, of which 4 were waited for; matrix products, arithmetic and copies ran while one was open for 8% of the time, Pallas kernels for 0%

profile of v2, /device:TPU:1, one launch (start us, length us, event | category | flops | bytes accessed | tf_op | source)
XLA Modules:
  0.0 238.8 jit_solution(7107805285344764344)
XLA Ops:
  0.0 1.5 broadcast_in_dim.363
  1.5 11.5 %all-to-all-start = ((s32[128,1,16]{2,1,0:T(1,128)}), s32[128,1,16]{2,1,0:T(1,128)S(1)}, u32[]{:S(2)}, u32[]{:S(2)}) async-start(s32[128,1,16]{2,1,0:T(1,128)} %broadcast_in_dim.363), calls=%async_computation | async-start | bytes 131072 | tf_op jit(solution)/shard_map/all_to_all | solution.py:130
  15.4 7.3 %all-to-all-done = s32[128,1,16]{2,1,0:T(1,128)S(1)} async-done(((s32[128,1,16]{2,1,0:T(1,128)}), s32[128,1,16]{2,1,0:T(1,128)S(1)}, u32[]{:S(2)}, u32[]{:S(2)}) %all-to-all-start) | async-done | bytes 8224 | tf_op jit(solution)/shard_map/all_to_all | solution.py:130
  22.7 3.3 %select_reduce_fusion = s32[128,16]{1,0:T(8,128)S(1)} fusion(s32[512]{0:T(512)} %param.17, s32[128,16]{1,0:T(8,128)S(1)} %bitcast.849), kind=kLoop, calls=%fused_computation.66 | loop fusion | flops 3143680 | bytes 18432 | tf_op jit(solution)/shard_map/reduce_sum | solution.py:33
  26.2 3.1 %gather_fusion = bf16[128,32,256]{2,1,0:T(8,128)(2,1)} fusion(bf16[32,32,256]{2,1,0:T(8,128)(2,1)} %param.14, s32[1024]{0:T(1024)S(1)} %pad_clamp_fusion), kind=kCustom, calls=%fused_computation | custom fusion | bytes 4194816 | tf_op jit(solution)/shard_map/jit(_take)/gather | solution.py:137
  31.2 4.3 %all-to-all-start.2 = ((bf16[128,2,512]{2,1,0:T(2,128)(2,1)}), bf16[128,2,512]{2,1,0:T(2,128)(2,1)S(1)}, u32[]{:S(2)}, u32[]{:S(2)}) async-start(bf16[128,2,512]{2,1,0:T(2,128)(2,1)} %reshape.570), calls=%async_computation.2 | async-start | bytes 524288 | tf_op jit(solution)/shard_map/all_to_all | solution.py:142
  35.5 3.2 %broadcast_select_fusion = bf16[128,32,256]{2,1,0:T(8,128)(2,1)} fusion(bf16[128,32,256]{2,1,0:T(8,128)(2,1)} %gather_fusion, pred[128]{0:T(512)(128)(4,1)S(1)} %compare_and_fusion.4), kind=kLoop, calls=%fused_computation.124 | loop fusion | flops 1048576 | bytes 4194432 | tf_op jit(solution)/shard_map/jit(_take)/select_n | solution.py:137
  38.6 8.3 %all-to-all-done.2 = bf16[128,2,512]{2,1,0:T(2,128)(2,1)S(1)} async-done(((bf16[128,2,512]{2,1,0:T(2,128)(2,1)}), bf16[128,2,512]{2,1,0:T(2,128)(2,1)S(1)}, u32[]{:S(2)}, u32[]{:S(2)}) %all-to-all-start.2) | async-done | bytes 262176 | tf_op jit(solution)/shard_map/all_to_all | solution.py:142
  46.9 5.0 %all-to-all-start.1 = ((bf16[128,32,256]{2,1,0:T(8,128)(2,1)}), bf16[128,32,256]{2,1,0:T(8,128)(2,1)}, u32[]{:S(2)}, u32[]{:S(2)}) async-start(bf16[128,32,256]{2,1,0:T(8,128)(2,1)} %broadcast_select_fusion), calls=%async_computation.1 | async-start | bytes 4194304 | tf_op jit(solution)/shard_map/all_to_all | solution.py:136
  52.6 2.9 %fusion.560 = f32[512,512]{0,1:T(8,128)S(1)} fusion(bf16[512,2048]{1,0:T(8,128)(2,1)} %param.10, bf16[2048,512]{1,0:T(8,128)(2,1)S(1)} %copy-done), kind=kOutput, calls=%fused_computation.750 | convolution fusion | flops 1073741824 | bytes 5242880 | tf_op jit(solution)/shard_map/dot_general | solution.py:176
  57.1 1.2 broadcast_select_fusion.1
  58.2 22.7 %all-to-all-done.1 = bf16[128,32,256]{2,1,0:T(8,128)(2,1)} async-done(((bf16[128,32,256]{2,1,0:T(8,128)(2,1)}), bf16[128,32,256]{2,1,0:T(8,128)(2,1)}, u32[]{:S(2)}, u32[]{:S(2)}) %all-to-all-start.1) | async-done | bytes 2097184 | tf_op jit(solution)/shard_map/all_to_all | solution.py:136
  81.0 5.0 %all-to-all-start.3 = ((bf16[128,16,256]{2,1,0:T(8,128)(2,1)}), bf16[128,16,256]{2,1,0:T(8,128)(2,1)S(1)}, u32[]{:S(2)}, u32[]{:S(2)}) async-start(bf16[128,16,256]{2,1,0:T(8,128)(2,1)} %broadcast_select_fusion.1), calls=%async_computation.3 | async-start | bytes 2097152 | tf_op jit(solution)/shard_map/all_to_all | solution.py:139
  86.3 3.6 %copy.95 = bf16[64,8,8,256]{3,2,1,0:T(8,128)(2,1)} copy(bf16[64,8,8,256]{3,1,2,0:T(8,128)(2,1)} %bitcast.817) | data formatting | bytes 4194304
  91.5 3.5 %fusion.77 = bf16[512,16,32]{0,2,1:T(8,128)(2,1)S(1)} fusion(bf16[8,16,32,256]{3,2,1,0:T(8,128)(2,1)} %bitcast.5, bf16[512,8,256,1]{2,1,0,3:T(8,128)(2,1)} %bitcast.818, pred[512,16]{0,1:T(8,128)(4,1)S(1)} %iota_compare_fusion.1), kind=kOutput, calls=%fused_computation.228 | convolution fusion | flops 1074266112 | bytes 4726784 | tf_op jit(solution)/shard_map/tsf,sorf->tor/dot_general | solution.py:158
  95.0 10.0 %all-to-all-done.3 = bf16[128,16,256]{2,1,0:T(8,128)(2,1)S(1)} async-done(((bf16[128,16,256]{2,1,0:T(8,128)(2,1)}), bf16[128,16,256]{2,1,0:T(8,128)(2,1)S(1)}, u32[]{:S(2)}, u32[]{:S(2)}) %all-to-all-start.3) | async-done | bytes 1048608 | tf_op jit(solution)/shard_map/all_to_all | solution.py:139
  105.8 2.7 %bitcast_convert_fusion.1 = f32[512,2048]{0,1:T(8,128)} fusion(bf16[512,8,256]{0,2,1:T(8,128)(2,1)S(1)} %bitcast_convert_fusion), kind=kLoop, calls=%fused_computation.119 | loop fusion | flops 1048576 | bytes 6291456 | tf_op jit(solution)/shard_map/convert_element_type | solution.py:172
  108.5 5.5 %copy.93 = f32[512,2048]{1,0:T(8,128)} copy(f32[512,2048]{0,1:T(8,128)} %bitcast_convert_fusion.1) | data formatting | bytes 8388608 | tf_op jit(solution)/shard_map/convert_element_type | solution.py:172
  113.9 11.6 %convolution_add_fusion = f32[512,2048]{1,0:T(8,128)} fusion(f32[512,2048]{1,0:T(8,128)} %copy.93, bf16[512,2048]{1,0:T(8,128)(2,1)} %param.10, bf16[2048,2048]{1,0:T(8,128)(2,1)} %param.11), kind=kOutput, calls=%fused_computation.68 | convolution fusion | flops 4296015872 | bytes 18874368 | tf_op jit(solution)/shard_map/dot_general | solution.py:170
  125.5 5.4 %copy.80 = f32[512,2048]{0,1:T(8,128)} copy(f32[512,2048]{1,0:T(8,128)} %convolution_add_fusion) | data formatting | bytes 8388608 | tf_op jit(solution)/shard_map/add | solution.py:170
  130.9 2.9 %add_convert_fusion = (bf16[512,32,32]{0,2,1:T(8,128)(2,1)S(1)}, bf16[512,32,32]{0,2,1:T(8,128)(2,1)S(1)}) fusion(f32[512,32,64]{0,2,1:T(8,128)} %bitcast.815, f32[512,32]{0,1:T(8,128)S(1)} %get-tuple-element.15, f32[512,32]{0,1:T(8,128)S(1)} %get-tuple-element.14), kind=kLoop, calls=%fused_computation.122 | loop fusion | flops 4194304 | bytes 6422528 | tf_op jit(solution)/shard_map/convert.35
  133.8 1.7 fusion.528
  135.5 1.6 fusion.529
  137.1 1.6 fusion.530
  138.7 1.6 fusion.531
  140.4 1.6 fusion.532
  142.0 1.7 fusion.533
  143.7 1.7 fusion.534
  145.4 1.6 fusion.535
  147.0 1.6 fusion.536
  148.6 1.6 fusion.537
  150.2 1.6 fusion.538
  151.9 1.6 fusion.539
  153.5 1.7 fusion.540
  155.2 1.6 fusion.541
  156.8 1.6 fusion.542
  158.5 1.6 fusion.543
  160.1 1.6 fusion.544
  161.7 1.6 fusion.545
  163.4 1.6 fusion.546
  165.0 1.6 fusion.547
  166.6 1.6 fusion.548
  168.3 1.7 fusion.549
  169.9 1.6 fusion.550
  171.5 1.6 fusion.551
  174.6 2.5 %copy.77 = f32[512,512]{1,0:T(8,128)} copy(f32[512,512]{0,1:T(8,128)} %bitcast_convert_fusion.2) | data formatting | bytes 2097152 | tf_op jit(solution)/shard_map/convert_element_type | solution.py:182
  177.2 3.7 %fusion.8 = bf16[512,512]{1,0:T(8,128)(2,1)S(1)} fusion(f32[512,512]{1,0:T(8,128)} %copy.77, bf16[512,2048]{1,0:T(8,128)(2,1)} %param.10, bf16[2048,512]{1,0:T(8,128)(2,1)} %param.13), kind=kOutput, calls=%fused_computation.129 | convolution fusion | flops 1074266112 | bytes 5767168 | tf_op jit(solution)/shard_map/dot_general | solution.py:181
  182.6 1.3 copy.78
  183.8 1.7 fusion.552
  185.5 1.6 fusion.553
  187.2 1.6 fusion.554
  188.8 1.6 fusion.555
  195.8 1.2 fusion.224
  197.0 1.2 fusion.161
  199.3 1.3 fusion.163
  204.5 1.8 copy.82
  212.6 1.3 copy.86
  213.9 1.8 copy.81
  216.6 1.2 fusion.129
  218.6 1.3 fusion.131
  220.7 1.3 fusion.133
  225.0 2.1 copy.85
  233.9 2.2 copy.84
  236.1 2.7 %pad_maximum_fusion.1 = bf16[512,2048]{1,0:T(8,128)(2,1)} fusion(bf16[128,2048]{1,0:T(8,128)(2,1)S(1)} %copy.87, bf16[128,2048]{1,0:T(8,128)(2,1)S(1)} %copy.86, bf16[128,2048]{1,0:T(8,128)(2,1)} %copy.85, bf16[128,2048]{1,0:T(8,128)(2,1)} %copy.84), kind=kLoop, calls=%fused_computation.118 | loop fusion | flops 8388608 | bytes 4194304 | tf_op jit(solution)/shard_map/concatenate | solution.py:106
  (240 shorter events, 40.4 us)
Async XLA Ops:
  0.0 52.5 %copy-start = (bf16[2048,512]{1,0:T(8,128)(2,1)S(1)}, bf16[2048,512]{1,0:T(8,128)(2,1)}, u32[]{:S(2)}) copy-start(bf16[2048,512]{1,0:T(8,128)(2,1)} %param.12) | copy-start | bytes 6291460
  1.5 21.2 %all-to-all-start = ((s32[128,1,16]{2,1,0:T(1,128)}), s32[128,1,16]{2,1,0:T(1,128)S(1)}, u32[]{:S(2)}, u32[]{:S(2)}) async-start(s32[128,1,16]{2,1,0:T(1,128)} %broadcast_in_dim.363), calls=%async_computation | async-start | bytes 131072 | tf_op jit(solution)/shard_map/all_to_all | solution.py:130
  26.2 3.1 %copy-start.12 = (bf16[32,16,64]{2,1,0:T(8,128)(2,1)S(1)}, bf16[32,16,64]{2,1,0:T(8,128)(2,1)}, u32[]{:S(2)}) copy-start(bf16[32,16,64]{2,1,0:T(8,128)(2,1)} %param.16) | copy-start | bytes 196612
  31.2 15.7 %all-to-all-start.2 = ((bf16[128,2,512]{2,1,0:T(2,128)(2,1)}), bf16[128,2,512]{2,1,0:T(2,128)(2,1)S(1)}, u32[]{:S(2)}, u32[]{:S(2)}) async-start(bf16[128,2,512]{2,1,0:T(2,128)(2,1)} %reshape.570), calls=%async_computation.2 | async-start | bytes 524288 | tf_op jit(solution)/shard_map/all_to_all | solution.py:142
  46.9 34.1 %all-to-all-start.1 = ((bf16[128,32,256]{2,1,0:T(8,128)(2,1)}), bf16[128,32,256]{2,1,0:T(8,128)(2,1)}, u32[]{:S(2)}, u32[]{:S(2)}) async-start(bf16[128,32,256]{2,1,0:T(8,128)(2,1)} %broadcast_select_fusion), calls=%async_computation.1 | async-start | bytes 4194304 | tf_op jit(solution)/shard_map/all_to_all | solution.py:136
  81.0 24.0 %all-to-all-start.3 = ((bf16[128,16,256]{2,1,0:T(8,128)(2,1)}), bf16[128,16,256]{2,1,0:T(8,128)(2,1)S(1)}, u32[]{:S(2)}, u32[]{:S(2)}) async-start(bf16[128,16,256]{2,1,0:T(8,128)(2,1)} %broadcast_select_fusion.1), calls=%async_computation.3 | async-start | bytes 2097152 | tf_op jit(solution)/shard_map/all_to_all | solution.py:139
  86.3 3.8 %copy-start.66 = (s32[192]{0:T(256)S(1)}, s32[192]{0:T(256)}, u32[]{:S(2)}) copy-start(s32[192]{0:T(256)} %constant.96.clone.1) | copy-start | bytes 2308
  90.3 102.2 %copy-start.13 = (pred[128,192]{0,1:T(8,128)(4,1)}, pred[128,192]{0,1:T(8,128)(4,1)S(1)}, u32[]{:S(2)}) copy-start(pred[128,192]{0,1:T(8,128)(4,1)S(1)} %get-tuple-element.91) | copy-start | bytes 73732
  95.0 13.5 %copy-start.40 = (bf16[512,16,32]{0,2,1:T(8,128)(2,1)}, bf16[512,16,32]{0,2,1:T(8,128)(2,1)S(1)}, u32[]{:S(2)}) copy-start(bf16[512,16,32]{0,2,1:T(8,128)(2,1)S(1)} %fusion.77) | copy-start | bytes 1572868
  171.5 1.6 copy-start.11
  171.5 1.6 copy-start.41
  194.6 6.0 %copy-start.36 = (f32[4,128,192]{1,2,0:T(8,128)S(1)}, f32[4,128,192]{1,2,0:T(8,128)}, u32[]{:S(2)}) copy-start(f32[4,128,192]{1,2,0:T(8,128)} %get-tuple-element.29) | copy-start | bytes 1179652
  194.6 6.0 %copy-start.65 = (f32[4,128]{1,0:T(4,128)S(1)}, f32[4,128]{1,0:T(4,128)}, u32[]{:S(2)}) copy-start(f32[4,128]{1,0:T(4,128)} %get-tuple-element.28) | copy-start | bytes 6148
  194.6 7.1 %copy-start.35 = (f32[4,128,192]{1,2,0:T(8,128)S(1)}, f32[4,128,192]{1,2,0:T(8,128)}, u32[]{:S(2)}) copy-start(f32[4,128,192]{1,2,0:T(8,128)} %get-tuple-element.31) | copy-start | bytes 1179652
  194.7 7.1 %copy-start.64 = (f32[4,128]{1,0:T(4,128)S(1)}, f32[4,128]{1,0:T(4,128)}, u32[]{:S(2)}) copy-start(f32[4,128]{1,0:T(4,128)} %get-tuple-element.30) | copy-start | bytes 6148
  195.8 4.8 %copy-start.42 = (bf16[192,512]{0,1:T(8,128)(2,1)}, bf16[192,512]{0,1:T(8,128)(2,1)S(1)}, u32[]{:S(2)}) copy-start(bf16[192,512]{0,1:T(8,128)(2,1)S(1)} %copy.83) | copy-start | bytes 589828
  197.0 5.9 %copy-start.34 = (f32[4,128,192]{1,2,0:T(8,128)S(1)}, f32[4,128,192]{1,2,0:T(8,128)}, u32[]{:S(2)}) copy-start(f32[4,128,192]{1,2,0:T(8,128)} %get-tuple-element.33) | copy-start | bytes 1179652
  197.0 5.9 %copy-start.63 = (f32[4,128]{1,0:T(4,128)S(1)}, f32[4,128]{1,0:T(4,128)}, u32[]{:S(2)}) copy-start(f32[4,128]{1,0:T(4,128)} %get-tuple-element.32) | copy-start | bytes 6148
  199.3 3.9 %copy-start.33 = (f32[4,128,192]{1,2,0:T(8,128)S(1)}, f32[4,128,192]{1,2,0:T(8,128)}, u32[]{:S(2)}) copy-start(f32[4,128,192]{1,2,0:T(8,128)} %get-tuple-element.35) | copy-start | bytes 1179652
  199.3 3.9 %copy-start.62 = (f32[4,128]{1,0:T(4,128)S(1)}, f32[4,128]{1,0:T(4,128)}, u32[]{:S(2)}) copy-start(f32[4,128]{1,0:T(4,128)} %get-tuple-element.34) | copy-start | bytes 6148
  200.7 2.3 copy-start.43
  200.7 2.9 %copy-start.32 = (f32[4,128,192]{1,2,0:T(8,128)S(1)}, f32[4,128,192]{1,2,0:T(8,128)}, u32[]{:S(2)}) copy-start(f32[4,128,192]{1,2,0:T(8,128)} %get-tuple-element.37) | copy-start | bytes 1179652
  200.7 2.9 %copy-start.61 = (f32[4,128]{1,0:T(4,128)S(1)}, f32[4,128]{1,0:T(4,128)}, u32[]{:S(2)}) copy-start(f32[4,128]{1,0:T(4,128)} %get-tuple-element.36) | copy-start | bytes 6148
  201.9 2.0 copy-start.31
  201.9 2.0 copy-start.60
  203.3 3.0 %copy-start.30 = (f32[4,128,192]{1,2,0:T(8,128)S(1)}, f32[4,128,192]{1,2,0:T(8,128)}, u32[]{:S(2)}) copy-start(f32[4,128,192]{1,2,0:T(8,128)} %get-tuple-element.41) | copy-start | bytes 1179652
  203.6 2.7 %copy-start.59 = (f32[4,128]{1,0:T(4,128)S(1)}, f32[4,128]{1,0:T(4,128)}, u32[]{:S(2)}) copy-start(f32[4,128]{1,0:T(4,128)} %get-tuple-element.40) | copy-start | bytes 6148
  203.9 3.5 %copy-start.29 = (f32[4,128,192]{1,2,0:T(8,128)S(1)}, f32[4,128,192]{1,2,0:T(8,128)}, u32[]{:S(2)}) copy-start(f32[4,128,192]{1,2,0:T(8,128)} %get-tuple-element.43) | copy-start | bytes 1179652
  204.2 5.0 %copy-start.28 = (f32[4,128,192]{1,2,0:T(8,128)S(1)}, f32[4,128,192]{1,2,0:T(8,128)}, u32[]{:S(2)}) copy-start(f32[4,128,192]{1,2,0:T(8,128)} %get-tuple-element.45) | copy-start | bytes 1179652
  204.4 5.5 %copy-start.58 = (f32[4,128]{1,0:T(4,128)S(1)}, f32[4,128]{1,0:T(4,128)}, u32[]{:S(2)}) copy-start(f32[4,128]{1,0:T(4,128)} %get-tuple-element.44) | copy-start | bytes 6148
  204.4 5.8 %copy-start.27 = (f32[4,128,192]{1,2,0:T(8,128)S(1)}, f32[4,128,192]{1,2,0:T(8,128)}, u32[]{:S(2)}) copy-start(f32[4,128,192]{1,2,0:T(8,128)} %get-tuple-element.47) | copy-start | bytes 1179652
  204.5 5.8 %copy-start.57 = (f32[4,128]{1,0:T(4,128)S(1)}, f32[4,128]{1,0:T(4,128)}, u32[]{:S(2)}) copy-start(f32[4,128]{1,0:T(4,128)} %get-tuple-element.46) | copy-start | bytes 6148
  206.3 3.7 %copy-start.44 = (bf16[192,512]{0,1:T(8,128)(2,1)S(1)}, bf16[192,512]{0,1:T(8,128)(2,1)}, u32[]{:S(2)}) copy-start(bf16[192,512]{0,1:T(8,128)(2,1)} %copy.82) | copy-start | bytes 589828
  206.4 4.2 %copy-start.26 = (f32[4,128,192]{1,2,0:T(8,128)S(1)}, f32[4,128,192]{1,2,0:T(8,128)}, u32[]{:S(2)}) copy-start(f32[4,128,192]{1,2,0:T(8,128)} %get-tuple-element.49) | copy-start | bytes 1179652
  206.4 4.2 %copy-start.56 = (f32[4,128]{1,0:T(4,128)S(1)}, f32[4,128]{1,0:T(4,128)}, u32[]{:S(2)}) copy-start(f32[4,128]{1,0:T(4,128)} %get-tuple-element.48) | copy-start | bytes 6148
  208.2 2.7 %copy-start.25 = (f32[4,128,192]{1,2,0:T(8,128)S(1)}, f32[4,128,192]{1,2,0:T(8,128)}, u32[]{:S(2)}) copy-start(f32[4,128,192]{1,2,0:T(8,128)} %get-tuple-element.51) | copy-start | bytes 1179652
  208.2 2.7 %copy-start.55 = (f32[4,128]{1,0:T(4,128)S(1)}, f32[4,128]{1,0:T(4,128)}, u32[]{:S(2)}) copy-start(f32[4,128]{1,0:T(4,128)} %get-tuple-element.50) | copy-start | bytes 6148
  210.0 1.2 copy-start.24
  210.0 1.2 copy-start.54
  210.3 1.2 copy-start.23
  211.0 4.8 %copy-start.22 = (f32[4,128,192]{1,2,0:T(8,128)S(1)}, f32[4,128,192]{1,2,0:T(8,128)}, u32[]{:S(2)}) copy-start(f32[4,128,192]{1,2,0:T(8,128)} %get-tuple-element.57) | copy-start | bytes 1179652
  211.5 6.4 %copy-start.21 = (f32[4,128,192]{1,2,0:T(8,128)S(1)}, f32[4,128,192]{1,2,0:T(8,128)}, u32[]{:S(2)}) copy-start(f32[4,128,192]{1,2,0:T(8,128)} %get-tuple-element.59) | copy-start | bytes 1179652
  212.6 7.3 %copy-start.20 = (f32[4,128,192]{1,2,0:T(8,128)S(1)}, f32[4,128,192]{1,2,0:T(8,128)}, u32[]{:S(2)}) copy-start(f32[4,128,192]{1,2,0:T(8,128)} %get-tuple-element.61) | copy-start | bytes 1179652
  213.9 8.0 %copy-start.18 = (f32[4,128,192]{1,2,0:T(8,128)S(1)}, f32[4,128,192]{1,2,0:T(8,128)}, u32[]{:S(2)}) copy-start(f32[4,128,192]{1,2,0:T(8,128)} %get-tuple-element.63) | copy-start | bytes 1179652
  215.7 4.9 %copy-start.45 = (bf16[192,512]{0,1:T(8,128)(2,1)S(1)}, bf16[192,512]{0,1:T(8,128)(2,1)}, u32[]{:S(2)}) copy-start(bf16[192,512]{0,1:T(8,128)(2,1)} %copy.81) | copy-start | bytes 589828
  215.7 7.0 %copy-start.19 = (f32[4,128,192]{1,2,0:T(8,128)S(1)}, f32[4,128,192]{1,2,0:T(8,128)}, u32[]{:S(2)}) copy-start(f32[4,128,192]{1,2,0:T(8,128)} %get-tuple-element.63) | copy-start | bytes 1179652
  215.8 7.0 %copy-start.52 = (f32[4,128]{1,0:T(4,128)S(1)}, f32[4,128]{1,0:T(4,128)}, u32[]{:S(2)}) copy-start(f32[4,128]{1,0:T(4,128)} %get-tuple-element.62) | copy-start | bytes 6148
  216.6 6.4 %copy-start.17 = (f32[4,128,192]{1,2,0:T(8,128)S(1)}, f32[4,128,192]{1,2,0:T(8,128)}, u32[]{:S(2)}) copy-start(f32[4,128,192]{1,2,0:T(8,128)} %get-tuple-element.65) | copy-start | bytes 1179652
  216.6 6.4 %copy-start.51 = (f32[4,128]{1,0:T(4,128)S(1)}, f32[4,128]{1,0:T(4,128)}, u32[]{:S(2)}) copy-start(f32[4,128]{1,0:T(4,128)} %get-tuple-element.64) | copy-start | bytes 6148
  218.6 4.6 %copy-start.16 = (f32[4,128,192]{1,2,0:T(8,128)S(1)}, f32[4,128,192]{1,2,0:T(8,128)}, u32[]{:S(2)}) copy-start(f32[4,128,192]{1,2,0:T(8,128)} %get-tuple-element.67) | copy-start | bytes 1179652
  218.6 4.6 %copy-start.50 = (f32[4,128]{1,0:T(4,128)S(1)}, f32[4,128]{1,0:T(4,128)}, u32[]{:S(2)}) copy-start(f32[4,128]{1,0:T(4,128)} %get-tuple-element.66) | copy-start | bytes 6148
  220.7 2.9 %copy-start.15 = (f32[4,128,192]{1,2,0:T(8,128)S(1)}, f32[4,128,192]{1,2,0:T(8,128)}, u32[]{:S(2)}) copy-start(f32[4,128,192]{1,2,0:T(8,128)} %get-tuple-element.69) | copy-start | bytes 1179652
  220.7 2.9 %copy-start.49 = (f32[4,128]{1,0:T(4,128)S(1)}, f32[4,128]{1,0:T(4,128)}, u32[]{:S(2)}) copy-start(f32[4,128]{1,0:T(4,128)} %get-tuple-element.68) | copy-start | bytes 6148
  222.7 1.2 copy-start.14
  222.7 1.2 copy-start.48
  223.3 3.8 %copy-start.9 = (f32[4,128,192]{1,2,0:T(8,128)S(1)}, f32[4,128,192]{1,2,0:T(8,128)}, u32[]{:S(2)}) copy-start(f32[4,128,192]{1,2,0:T(8,128)} %get-tuple-element.73) | copy-start | bytes 1179652
  223.7 5.1 %copy-start.8 = (f32[4,128,192]{1,2,0:T(8,128)S(1)}, f32[4,128,192]{1,2,0:T(8,128)}, u32[]{:S(2)}) copy-start(f32[4,128,192]{1,2,0:T(8,128)} %get-tuple-element.75) | copy-start | bytes 1179652
  225.0 5.5 %copy-start.7 = (f32[4,128,192]{1,2,0:T(8,128)S(1)}, f32[4,128,192]{1,2,0:T(8,128)}, u32[]{:S(2)}) copy-start(f32[4,128,192]{1,2,0:T(8,128)} %get-tuple-element.77) | copy-start | bytes 1179652
  227.1 4.2 %copy-start.47 = (f32[4,128]{1,0:T(4,128)S(1)}, f32[4,128]{1,0:T(4,128)}, u32[]{:S(2)}) copy-start(f32[4,128]{1,0:T(4,128)} %get-tuple-element.76) | copy-start | bytes 6148
  227.1 4.4 %copy-start.6 = (f32[4,128,192]{1,2,0:T(8,128)S(1)}, f32[4,128,192]{1,2,0:T(8,128)}, u32[]{:S(2)}) copy-start(f32[4,128,192]{1,2,0:T(8,128)} %get-tuple-element.79) | copy-start | bytes 1179652
  227.1 4.4 %copy-start.46 = (f32[4,128]{1,0:T(4,128)S(1)}, f32[4,128]{1,0:T(4,128)}, u32[]{:S(2)}) copy-start(f32[4,128]{1,0:T(4,128)} %get-tuple-element.78) | copy-start | bytes 6148
  228.8 3.1 %copy-start.5 = (f32[4,128,192]{1,2,0:T(8,128)S(1)}, f32[4,128,192]{1,2,0:T(8,128)}, u32[]{:S(2)}) copy-start(f32[4,128,192]{1,2,0:T(8,128)} %get-tuple-element.81) | copy-start | bytes 1179652
  230.5 1.7 copy-start.4
  233.9 4.9 %copy-start.1 = (bf16[2048,512]{1,0:T(8,128)(2,1)S(1)}, bf16[2048,512]{1,0:T(8,128)(2,1)}, u32[]{:S(2)}) copy-start(bf16[2048,512]{1,0:T(8,128)(2,1)} %param.12) | copy-start | bytes 6291460
  (7 other events, 6.3 us)

commit v3 on v2

--- a/solution.py
+++ b/solution.py
@@ -1,6 +1,8 @@
 import jax
 import jax.numpy as jnp
 from jax import lax
+from jax.experimental import pallas as pl
+from jax.experimental.pallas import tpu as pltpu
 from jax.sharding import PartitionSpec as P
 
 HEADS = 32
@@ -167,22 +169,133 @@
         "tor,sorf->tsf", low[..., ADAPTER_RANK:], upv, preferred_element_type=jnp.float32
     ).astype(jnp.bfloat16).reshape(tok_rows, serve_count * vcols)
 
-    base_query = jnp.dot(
+    q_base = jnp.dot(
         normalized_hidden_states, query_weight_matrix, preferred_element_type=jnp.float32
-    ) + delta_query.astype(jnp.float32)
-    query_rot = rotary(base_query.reshape(tok_rows, HEADS, HEAD_DIM), positions).astype(
-        jnp.bfloat16
-    )
-    base_key = jnp.dot(
+    )
+    k_base = jnp.dot(
         normalized_hidden_states, key_weight_matrix, preferred_element_type=jnp.float32
     )
-    key_rot = rotary(base_key.reshape(tok_rows, KV_HEADS, HEAD_DIM), positions).astype(jnp.bfloat16)
-    value_rows = (
-        jnp.dot(normalized_hidden_states, value_weight_matrix, preferred_element_type=jnp.float32)
-        + delta_value.astype(jnp.float32)
-    ).astype(jnp.bfloat16)
-    value_rows = value_rows.reshape(tok_rows, KV_HEADS, HEAD_DIM)
-    return attention(query_rot, key_rot, value_rows, request_ids)
+    v_base = jnp.dot(
+        normalized_hidden_states, value_weight_matrix, preferred_element_type=jnp.float32
+    )
+    return fused_attention(q_base, delta_query, k_base, v_base, delta_value, positions)
+
+
+def _swap_halves(x):
+    return jnp.concatenate([x[:, 32:64], x[:, 0:32], x[:, 96:128], x[:, 64:96]], axis=1)
+
+
+def _attend_kernel(qb_ref, dq_ref, kb_ref, vb_ref, dv_ref, cos_ref, sin_ref, pos_ref, out_ref,
+                   q_s, kd_s, vd_s):
+    rows = qb_ref.shape[0]
+    blk = 128
+    n_blk = rows // blk
+    q_chunks = qb_ref.shape[1] // 128
+    k_chunks = kb_ref.shape[1] // 128
+    lane = lax.broadcasted_iota(jnp.int32, (1, 128), 1)
+
+    def rope_rows(r, carry):
+        r0 = pl.multiple_of(r * blk, blk)
+        cos = cos_ref[pl.ds(r0, blk), :]
+        sin = sin_ref[pl.ds(r0, blk), :]
+
+        def q_col(c, carry2):
+            c0 = pl.multiple_of(c * 128, 128)
+            x = qb_ref[pl.ds(r0, blk), pl.ds(c0, 128)] + dq_ref[pl.ds(r0, blk), pl.ds(c0, 128)].astype(jnp.float32)
+            q_s[pl.ds(r0, blk), pl.ds(c0, 128)] = (x * cos + _swap_halves(x) * sin).astype(jnp.bfloat16)
+            return carry2
+
+        lax.fori_loop(0, q_chunks, q_col, 0)
+        for c in range(k_chunks):
+            x = kb_ref[pl.ds(r0, blk), c * 128:(c + 1) * 128]
+            k = (x * cos + _swap_halves(x) * sin).astype(jnp.bfloat16).astype(jnp.float32)
+            v = (vb_ref[pl.ds(r0, blk), c * 128:(c + 1) * 128]
+                 + dv_ref[pl.ds(r0, blk), c * 128:(c + 1) * 128].astype(jnp.float32))
+            v = v.astype(jnp.bfloat16).astype(jnp.float32)
+            zeros = jnp.zeros((blk, 64), jnp.float32)
+            for half in range(2):
+                g = 2 * c + half
+                kg = k[:, half * 64:(half + 1) * 64]
+                vg = v[:, half * 64:(half + 1) * 64]
+                kd_s[g, pl.ds(r0, blk), :] = jnp.concatenate([kg, kg], axis=1).astype(jnp.bfloat16)
+                vd_s[g, pl.ds(r0, blk), 0:128] = jnp.concatenate([vg, zeros], axis=1).astype(jnp.bfloat16)
+                vd_s[g, pl.ds(r0, blk), 128:256] = jnp.concatenate([zeros, vg], axis=1).astype(jnp.bfloat16)
+        return carry
+
+    lax.fori_loop(0, n_blk, rope_rows, 0)
+
+    window = 2 * blk
+    per_group = HEADS // KV_HEADS
+
+    def query_block(b, carry):
+        q0 = pl.multiple_of(b * blk, blk)
+        ws = pl.multiple_of(jnp.clip(b * blk - blk, 0, rows - window), blk)
+        qpos = pos_ref[pl.ds(q0, blk), :]
+        qidx = q0 + lax.broadcasted_iota(jnp.int32, (blk, 1), 0)
+        kidx = ws + lax.broadcasted_iota(jnp.int32, (1, window), 1)
+        allowed = (kidx >= qidx - qpos) & (kidx <= qidx)
+
+        def head_pair(j, carry2):
+            g = j // (per_group // 2)
+            c0 = pl.multiple_of(j * 128, 128)
+            qc = q_s[pl.ds(q0, blk), pl.ds(c0, 128)]
+            kd = kd_s[g, pl.ds(ws, window), :]
+            vd = vd_s[g, pl.ds(ws, window), :]
+            zero = jnp.zeros_like(qc)
+            probs, totals = [], []
+            for half in range(2):
+                keep = (lane < 64) if half == 0 else (lane >= 64)
+                qh = jnp.where(keep, qc, zero)
+                s = lax.dot_general(qh, kd, (((1,), (1,)), ((), ())),
+                                    preferred_element_type=jnp.float32) * (HEAD_DIM ** -0.5)
+                s = jnp.where(allowed, s, -jnp.inf)
+                m = jnp.max(s, axis=1, keepdims=True)
+                p = jnp.exp(s - m)
+                totals.append(jnp.sum(p, axis=1, keepdims=True))
+                probs.append(p.astype(jnp.bfloat16))
+            o = (jnp.dot(probs[0], vd[:, 0:128], preferred_element_type=jnp.float32)
+                 + jnp.dot(probs[1], vd[:, 128:256], preferred_element_type=jnp.float32))
+            o = jnp.where(lane < 64, o / totals[0], o / totals[1])
+            out_ref[pl.ds(q0, blk), pl.ds(c0, 128)] = o.astype(out_ref.dtype)
+            return carry2
+
+        lax.fori_loop(0, HEADS // 2, head_pair, 0)
+        return carry
+
+    lax.fori_loop(0, n_blk, query_block, 0)
+
+
+def rope_tables(positions):
+    half_dim = HEAD_DIM // 2
+    frequency = 500000.0 ** (-(jnp.arange(half_dim).astype(jnp.float32) * 2.0 / HEAD_DIM))
+    angles = positions.astype(jnp.float32)[:, None] * frequency[None, :]
+    cos = jnp.cos(angles)
+    sin = jnp.sin(angles)
+    cos_t = jnp.concatenate([cos, cos, cos, cos], axis=1)
+    sin_t = jnp.concatenate([-sin, sin, -sin, sin], axis=1)
+    return cos_t, sin_t
+
+
+def fused_attention(q_base, delta_q, k_base, v_base, delta_v, positions):
+    rows = q_base.shape[0]
+    cos_t, sin_t = rope_tables(positions)
+    pos_col = positions.astype(jnp.int32).reshape(rows, 1)
+    vmem = pl.BlockSpec(memory_space=pltpu.VMEM)
+    flops = 2 * rows * 256 * 64 * 2 * HEADS * 2
+    return pl.pallas_call(
+        _attend_kernel,
+        out_shape=jax.ShapeDtypeStruct((rows, HEADS * HEAD_DIM), jnp.bfloat16),
+        in_specs=[vmem] * 8,
+        out_specs=vmem,
+        scratch_shapes=[
+            pltpu.VMEM((rows, HEADS * HEAD_DIM), jnp.bfloat16),
+            pltpu.VMEM((KV_HEADS, rows, 128), jnp.bfloat16),
+            pltpu.VMEM((KV_HEADS, rows, 256), jnp.bfloat16),
+        ],
+        compiler_params=pltpu.CompilerParams(vmem_limit_bytes=48 * 1024 * 1024),
+        cost_estimate=pl.CostEstimate(flops=flops, transcendentals=rows * 256 * HEADS,
+                                      bytes_accessed=rows * (2048 * 6 + 512 * 12 + 256 * 4)),
+    )(q_base, delta_q, k_base, v_base, delta_v, cos_t, sin_t, pos_col)
 
 
 def solution(mesh):

time: 240 us -> 157 us (0.65)
  matrix products: 89.4 us -> 24.2 us
  Pallas kernels: 0 us -> 39.6 us
  waiting for transfers between devices: 48.3 us -> 25.9 us
  local copies, waits for them, and re-layouts: 42.9 us -> 23.7 us
  other arithmetic: 31 us -> 15.9 us
    dot_general x64 -> x0, matrix products: 66.6 us -> none  [the longest x32 50.1 us: attention(): jnp.einsum('qhd,kd->hqk', query_part, key_part, preferred_element_type=jn...]
    pallas_call x0 -> x1, Pallas kernels: none -> 39.6 us  [fused_attention(): pl.pallas_call(_attend_kernel, out_shape=jax.ShapeDtypeStruct((rows, HEAD...]
    all_to_all x1, waiting for transfers between devices: 22.7 us -> 7.49 us  [local(): lax.all_to_all(jnp.take(adapter_down_weight, local_pick, axis=0), axes, 0...]
    convert_element_type x7 -> x0, local copies, waits for them, and re-layouts: 15.1 us -> none  [the longest x4 5.8 us: attention(): outputs.append(jnp.concatenate(pieces, axis=1).reshape(block_rows, HEADS...]
    reduce_sum x32 -> x0, other arithmetic: 10.8 us -> none  [attention(): row_total = jnp.sum(raised, axis=-1)]
    slice x13 -> x0, local copies, waits for them, and re-layouts: 5.94 us -> none  [the longest x4 5.62 us: attention(): value_block = value_pad[first:first + reach + block_rows]]
    add x1 -> x0, local copies, waits for them, and re-layouts: 5.35 us -> none  [local(): jnp.dot(normalized_hidden_states, query_weight_matrix, preferred_element_...]
    reshape x1 -> x3, local copies, waits for them, and re-layouts: 0.73 us -> 5.92 us  [the longest x1 3.94 us: local(): delta_query = jnp.einsum('tor,sorf->tsf', low[..., :ADAPTER_RANK], upq, p...]
  transfers between devices with their start and end apart: 4 -> 4, of which waited for: 4 -> 4; matrix products, arithmetic and copies ran while one was open for 8% -> 27% of each run, Pallas kernels for 0% -> 0%
where the time goes in v3:
time: 157 us
  Pallas kernels  39.6 us (25%)
  starting transfers between devices  27.1 us (17%)
  waiting for transfers between devices  25.9 us (16%)
  matrix products  24.2 us (15%)
  local copies, waits for them, and re-layouts  23.7 us (15%)
  other arithmetic  15.9 us (10%)
    pallas_call x1, Pallas kernels, fused_attention(): pl.pallas_call(_attend_kernel, out_shape=jax.ShapeDtypeStruct((rows, HEAD...  39.6 us
    all_to_all x1, starting transfers between devices, local(): lax.all_to_all(jnp.broadcast_to(adapter_per_request, (device_total, reque...  11.5 us
    unnamed x23, local copies, waits for them, and re-layouts  10.2 us
    dot_general x1, matrix products, local(): jnp.dot(normalized_hidden_states, query_weight_matrix, preferred_element_...  9.39 us
    all_to_all x1, waiting for transfers between devices, local(): lax.all_to_all(jnp.take(adapter_down_weight, local_pick, axis=0), axes, 0...  7.49 us
    all_to_all x1, waiting for transfers between devices, local(): lax.all_to_all(jnp.take(adapter_up_query_weight, local_pick, axis=0), axe...  6.95 us
    all_to_all x1, waiting for transfers between devices, local(): lax.all_to_all(jnp.take(adapter_up_value_weight, local_pick, axis=0), axe...  6.23 us
    all_to_all x1, starting transfers between devices, local(): lax.all_to_all(jnp.take(adapter_up_query_weight, local_pick, axis=0), axe...  6.05 us
  transfers between devices with their start and end apart: 4, of which 4 were waited for; matrix products, arithmetic and copies ran while one was open for 27% of the time, Pallas kernels for 0%

profile of v3, /device:TPU:1, one launch (start us, length us, event | category | flops | bytes accessed | tf_op | source)
XLA Modules:
  0.0 156.6 jit_solution(15557380635285832986)
XLA Ops:
  0.0 0.0 copy-start
  0.0 1.5 broadcast_in_dim.103
  1.5 11.5 %all-to-all-start = ((s32[128,1,16]{2,1,0:T(1,128)}), s32[128,1,16]{2,1,0:T(1,128)S(1)}, u32[]{:S(2)}, u32[]{:S(2)}) async-start(s32[128,1,16]{2,1,0:T(1,128)} %broadcast_in_dim.103), calls=%async_computation | async-start | bytes 131072 | tf_op jit(solution)/shard_map/all_to_all | solution.py:132
  13.0 0.7 copy.33
  13.7 0.1 reduce
  13.9 0.7 fusion.22
  14.5 0.1 convert_reduce_fusion
  14.6 0.9 select_reduce_fusion.3
  15.5 0.1 select_reduce_fusion.1
  15.6 0.0 copy-start.4
  15.6 1.8 %fusion.15 = (f32[512,32]{1,0:T(8,128)S(1)}, f32[512,32]{1,0:T(8,128)}, f32[512,32]{1,0:T(8,128)}) fusion(f32[32]{0:T(128)S(1)} %negate_power_fusion, f32[512]{0:T(512)S(1)} %subtract_convert_fusion), kind=kLoop, calls=%fused_computation.29 | loop fusion | flops 32768 | bytes 198784 | tf_op jit(solution)/shard_map/neg | solution.py:275
  17.5 5.2 %all-to-all-done = s32[128,1,16]{2,1,0:T(1,128)S(1)} async-done(((s32[128,1,16]{2,1,0:T(1,128)}), s32[128,1,16]{2,1,0:T(1,128)S(1)}, u32[]{:S(2)}, u32[]{:S(2)}) %all-to-all-start) | async-done | bytes 8224 | tf_op jit(solution)/shard_map/all_to_all | solution.py:132
  22.7 3.3 %select_reduce_fusion = s32[128,16]{1,0:T(8,128)S(1)} fusion(s32[512]{0:T(512)} %param.17, s32[128,16]{1,0:T(8,128)S(1)} %bitcast.63), kind=kLoop, calls=%fused_computation.4 | loop fusion | flops 3143680 | bytes 18432 | tf_op jit(solution)/shard_map/reduce_sum | solution.py:35
  26.0 0.1 fusion.18
  26.2 2.4 %gather_fusion.2 = bf16[128,16,64]{2,1,0:T(8,128)(2,1)} fusion(bf16[32,16,64]{2,1,0:T(8,128)(2,1)} %param.16, s32[1024]{0:T(1024)S(1)} %pad_clamp_fusion), kind=kCustom, calls=%fused_computation.2 | custom fusion | bytes 524800 | tf_op jit(solution)/shard_map/jit(_take)/gather | solution.py:145
  28.6 1.2 broadcast_select_fusion.2
  29.8 1.0 reshape.162
  30.8 4.5 %all-to-all-start.3 = ((bf16[128,2,512]{2,1,0:T(2,128)(2,1)}), bf16[128,2,512]{2,1,0:T(2,128)(2,1)S(1)}, u32[]{:S(2)}, u32[]{:S(2)}) async-start(bf16[128,2,512]{2,1,0:T(2,128)(2,1)} %reshape.162), calls=%async_computation.3 | async-start | bytes 524288 | tf_op jit(solution)/shard_map/all_to_all | solution.py:144
  35.4 0.0 copy-done.4
  35.4 2.0 %gather_fusion = bf16[128,32,256]{2,1,0:T(8,128)(2,1)} fusion(bf16[32,32,256]{2,1,0:T(8,128)(2,1)S(1)} %copy-done.4, s32[1024]{0:T(1024)S(1)} %pad_clamp_fusion), kind=kCustom, calls=%fused_computation | custom fusion | bytes 4194816 | tf_op jit(solution)/shard_map/jit(_take)/gather | solution.py:139
  37.4 3.2 %broadcast_select_fusion = bf16[128,32,256]{2,1,0:T(8,128)(2,1)} fusion(bf16[128,32,256]{2,1,0:T(8,128)(2,1)} %gather_fusion, pred[128]{0:T(512)(128)(4,1)S(1)} %compare_and_fusion), kind=kLoop, calls=%fused_computation.8 | loop fusion | flops 1048576 | bytes 4194432 | tf_op jit(solution)/shard_map/jit(_take)/select_n | solution.py:139
  40.6 0.0 copy-start.8
  40.6 6.2 %all-to-all-done.3 = bf16[128,2,512]{2,1,0:T(2,128)(2,1)S(1)} async-done(((bf16[128,2,512]{2,1,0:T(2,128)(2,1)}), bf16[128,2,512]{2,1,0:T(2,128)(2,1)S(1)}, u32[]{:S(2)}, u32[]{:S(2)}) %all-to-all-start.3) | async-done | bytes 262176 | tf_op jit(solution)/shard_map/all_to_all | solution.py:144
  46.8 0.0 copy-start.7
  46.8 5.0 %all-to-all-start.1 = ((bf16[128,32,256]{2,1,0:T(8,128)(2,1)}), bf16[128,32,256]{2,1,0:T(8,128)(2,1)}, u32[]{:S(2)}, u32[]{:S(2)}) async-start(bf16[128,32,256]{2,1,0:T(8,128)(2,1)} %broadcast_select_fusion), calls=%async_computation.1 | async-start | bytes 4194304 | tf_op jit(solution)/shard_map/all_to_all | solution.py:138
  51.8 0.0 copy-done.7
  51.8 0.0 copy-done.8
  51.8 1.8 %pad_maximum_fusion = (f32[512,128]{1,0:T(8,128)S(1)}, f32[512,128]{1,0:T(8,128)S(1)}) fusion(f32[512,32]{1,0:T(8,128)} %get-tuple-element.9, f32[512,32]{1,0:T(8,128)S(1)} %copy-done.8, f32[512,32]{1,0:T(8,128)S(1)} %get-tuple-element.7), kind=kLoop, calls=%fused_computation.21 | loop fusion | flops 393216 | bytes 720896 | tf_op jit(solution)/shard_map/concatenate | solution.py:274
  53.7 0.1 copy.38
  53.8 0.0 copy-start.6
  53.8 3.8 %copy.47 = bf16[64,8,8,256]{3,2,1,0:T(8,128)(2,1)} copy(bf16[64,8,8,256]{3,1,2,0:T(8,128)(2,1)} %bitcast.59) | data formatting | bytes 4194304
  57.6 0.0 copy-done
  57.6 0.0 copy-done.6
  57.6 2.3 %fusion.24.kb_ref = f32[512,512]{1,0:T(8,128)} fusion(bf16[512,2048]{1,0:T(8,128)(2,1)S(1)} %copy-done.6, bf16[2048,512]{1,0:T(8,128)(2,1)S(1)} %copy-done), kind=kOutput, calls=%fused_computation.58 | convolution fusion | flops 1073741824 | bytes 5242880 | tf_op jit(solution)/shard_map/dot_general | solution.py:175
  60.0 0.0 copy-start.5
  60.0 9.4 %fusion.23.qb_ref = f32[512,2048]{1,0:T(8,128)} fusion(bf16[512,2048]{1,0:T(8,128)(2,1)S(1)} %copy-done.6, bf16[2048,2048]{1,0:T(8,128)(2,1)} %param.11), kind=kOutput, calls=%fused_computation.57 | convolution fusion | flops 4294967296 | bytes 14680064 | tf_op jit(solution)/shard_map/dot_general | solution.py:172
  69.4 0.0 copy-done.5
  69.4 1.6 %gather_fusion.1 = bf16[128,16,256]{2,1,0:T(8,128)(2,1)} fusion(bf16[32,16,256]{2,1,0:T(8,128)(2,1)S(1)} %copy-done.5, s32[1024]{0:T(1024)S(1)} %pad_clamp_fusion), kind=kCustom, calls=%fused_computation.1 | custom fusion | bytes 2097664 | tf_op jit(solution)/shard_map/jit(_take)/gather | solution.py:142
  71.0 2.4 %broadcast_select_fusion.1 = bf16[128,16,256]{2,1,0:T(8,128)(2,1)} fusion(bf16[128,16,256]{2,1,0:T(8,128)(2,1)} %gather_fusion.1, pred[128]{0:T(512)(128)(4,1)S(1)} %compare_and_fusion), kind=kLoop, calls=%fused_computation.15 | loop fusion | flops 524288 | bytes 2097280 | tf_op jit(solution)/shard_map/jit(_take)/select_n | solution.py:142
  73.4 7.5 %all-to-all-done.1 = bf16[128,32,256]{2,1,0:T(8,128)(2,1)} async-done(((bf16[128,32,256]{2,1,0:T(8,128)(2,1)}), bf16[128,32,256]{2,1,0:T(8,128)(2,1)}, u32[]{:S(2)}, u32[]{:S(2)}) %all-to-all-start.1) | async-done | bytes 2097184 | tf_op jit(solution)/shard_map/all_to_all | solution.py:138
  80.9 6.1 %all-to-all-start.2 = ((bf16[128,16,256]{2,1,0:T(8,128)(2,1)}), bf16[128,16,256]{2,1,0:T(8,128)(2,1)}, u32[]{:S(2)}, u32[]{:S(2)}) async-start(bf16[128,16,256]{2,1,0:T(8,128)(2,1)} %broadcast_select_fusion.1), calls=%async_computation.2 | async-start | bytes 2097152 | tf_op jit(solution)/shard_map/all_to_all | solution.py:141
  86.9 4.4 %fusion.25.vb_ref = f32[512,512]{1,0:T(8,128)} fusion(bf16[512,2048]{1,0:T(8,128)(2,1)} %param.10, bf16[2048,512]{1,0:T(8,128)(2,1)} %param.13), kind=kOutput, calls=%fused_computation.59 | convolution fusion | flops 1073741824 | bytes 5242880 | tf_op jit(solution)/shard_map/dot_general | solution.py:178
  91.4 1.3 reshape.163
  92.7 3.5 %fusion.12 = bf16[512,16,32]{0,2,1:T(8,128)(2,1)S(1)} fusion(bf16[8,16,32,256]{3,2,1,0:T(8,128)(2,1)} %bitcast.5, bf16[512,8,256,1]{2,1,0,3:T(8,128)(2,1)} %bitcast.60, pred[512,16]{0,1:T(8,128)(4,1)S(1)} %iota_compare_fusion.1), kind=kOutput, calls=%fused_computation.14 | convolution fusion | flops 1074266112 | bytes 4726784 | tf_op jit(solution)/shard_map/tsf,sorf->tor/dot_general | solution.py:160
  96.2 0.0 copy-start.9
  96.2 1.1 fusion.8
  97.4 0.0 copy-done.9
  97.4 1.3 copy.39.dv_ref
  98.6 6.9 %all-to-all-done.2 = bf16[128,16,256]{2,1,0:T(8,128)(2,1)} async-done(((bf16[128,16,256]{2,1,0:T(8,128)(2,1)}), bf16[128,16,256]{2,1,0:T(8,128)(2,1)}, u32[]{:S(2)}, u32[]{:S(2)}) %all-to-all-start.2) | async-done | bytes 1048608 | tf_op jit(solution)/shard_map/all_to_all | solution.py:141
  105.6 3.4 %bitcast_convert_fusion = bf16[512,8,256]{0,2,1:T(8,128)(2,1)} fusion(bf16[8,16,16,256]{3,2,1,0:T(8,128)(2,1)} %bitcast.10, bf16[512,16,32]{0,2,1:T(8,128)(2,1)} %copy-done.9), kind=kOutput, calls=%fused_computation.3 | convolution fusion | flops 537919488 | bytes 3407872 | tf_op jit(solution)/shard_map/tor,sorf->tsf/dot_general | solution.py:165
  109.0 3.9 %copy.45.dq_ref = bf16[512,2048]{1,0:T(8,128)(2,1)} copy(bf16[512,2048]{0,1:T(8,128)(2,1)} %bitcast.58) | data formatting | bytes 4194304 | tf_op jit(solution)/shard_map/reshape | solution.py:167
  112.9 0.0 copy-start.1
  112.9 1.6 %copy-done.1 = bf16[512,2048]{1,0:T(8,128)(2,1)S(1)} copy-done((bf16[512,2048]{1,0:T(8,128)(2,1)S(1)}, bf16[512,2048]{1,0:T(8,128)(2,1)}, u32[]{:S(2)}) %copy-start.1) | copy-done | bytes 2097176
  114.5 0.0 copy-start.2
  114.5 1.2 copy-done.2
  115.7 0.0 copy-start.3
  115.7 1.2 copy-done.3
  117.0 39.6 %shard_map.100 = bf16[512,2048]{1,0:T(8,128)(2,1)} custom-call(f32[512,2048]{1,0:T(8,128)} %fusion.23.qb_ref, bf16[512,2048]{1,0:T(8,128)(2,1)S(1)} %copy-done.1, f32[512,512]{1,0:T(8,128)S(1)} %copy-done.2, f32[512,512]{1,0:T(8,128)S(1)} %copy-done.3, bf16[512,512]{1,0:T(8,128)(2,1)S(1)} %copy.39.dv_ref, f32[512,128]{1,0:T(8,128)S(1)} %get-tuple-element.10.cos_ref, ...), custom_call_target="tpu_custom_call" | custom-call | flops 2147483648 | bytes 9961472 | tf_op jit(solution)/shard_map/pallas_call | solution.py:285
  (9 shorter events, 0.1 us)
Async XLA Ops:
  0.0 57.6 %copy-start = (bf16[2048,512]{1,0:T(8,128)(2,1)S(1)}, bf16[2048,512]{1,0:T(8,128)(2,1)}, u32[]{:S(2)}) copy-start(bf16[2048,512]{1,0:T(8,128)(2,1)} %param.12) | copy-start | bytes 6291460
  1.5 21.2 %all-to-all-start = ((s32[128,1,16]{2,1,0:T(1,128)}), s32[128,1,16]{2,1,0:T(1,128)S(1)}, u32[]{:S(2)}, u32[]{:S(2)}) async-start(s32[128,1,16]{2,1,0:T(1,128)} %broadcast_in_dim.103), calls=%async_computation | async-start | bytes 131072 | tf_op jit(solution)/shard_map/all_to_all | solution.py:132
  15.6 19.8 %copy-start.4 = (bf16[32,32,256]{2,1,0:T(8,128)(2,1)S(1)}, bf16[32,32,256]{2,1,0:T(8,128)(2,1)}, u32[]{:S(2)}) copy-start(bf16[32,32,256]{2,1,0:T(8,128)(2,1)} %param.14) | copy-start | bytes 1572868
  30.8 16.0 %all-to-all-start.3 = ((bf16[128,2,512]{2,1,0:T(2,128)(2,1)}), bf16[128,2,512]{2,1,0:T(2,128)(2,1)S(1)}, u32[]{:S(2)}, u32[]{:S(2)}) async-start(bf16[128,2,512]{2,1,0:T(2,128)(2,1)} %reshape.162), calls=%async_computation.3 | async-start | bytes 524288 | tf_op jit(solution)/shard_map/all_to_all | solution.py:144
  40.6 11.3 %copy-start.8 = (f32[512,32]{1,0:T(8,128)S(1)}, f32[512,32]{1,0:T(8,128)}, u32[]{:S(2)}) copy-start(f32[512,32]{1,0:T(8,128)} %get-tuple-element.8) | copy-start | bytes 196612
  46.8 5.0 %copy-start.7 = (bf16[128,2,512]{2,1,0:T(2,128)(2,1)}, bf16[128,2,512]{2,1,0:T(2,128)(2,1)S(1)}, u32[]{:S(2)}) copy-start(bf16[128,2,512]{2,1,0:T(2,128)(2,1)S(1)} %all-to-all-done.3) | copy-start | bytes 786436
  46.8 34.1 %all-to-all-start.1 = ((bf16[128,32,256]{2,1,0:T(8,128)(2,1)}), bf16[128,32,256]{2,1,0:T(8,128)(2,1)}, u32[]{:S(2)}, u32[]{:S(2)}) async-start(bf16[128,32,256]{2,1,0:T(8,128)(2,1)} %broadcast_select_fusion), calls=%async_computation.1 | async-start | bytes 4194304 | tf_op jit(solution)/shard_map/all_to_all | solution.py:138
  53.8 3.8 %copy-start.6 = (bf16[512,2048]{1,0:T(8,128)(2,1)S(1)}, bf16[512,2048]{1,0:T(8,128)(2,1)}, u32[]{:S(2)}) copy-start(bf16[512,2048]{1,0:T(8,128)(2,1)} %param.10) | copy-start | bytes 6291460
  60.0 9.4 %copy-start.5 = (bf16[32,16,256]{2,1,0:T(8,128)(2,1)S(1)}, bf16[32,16,256]{2,1,0:T(8,128)(2,1)}, u32[]{:S(2)}) copy-start(bf16[32,16,256]{2,1,0:T(8,128)(2,1)} %param.15) | copy-start | bytes 786436
  80.9 24.7 %all-to-all-start.2 = ((bf16[128,16,256]{2,1,0:T(8,128)(2,1)}), bf16[128,16,256]{2,1,0:T(8,128)(2,1)}, u32[]{:S(2)}, u32[]{:S(2)}) async-start(bf16[128,16,256]{2,1,0:T(8,128)(2,1)} %broadcast_select_fusion.1), calls=%async_computation.2 | async-start | bytes 2097152 | tf_op jit(solution)/shard_map/all_to_all | solution.py:141
  96.2 1.2 copy-start.9
  112.9 1.6 %copy-start.1 = (bf16[512,2048]{1,0:T(8,128)(2,1)S(1)}, bf16[512,2048]{1,0:T(8,128)(2,1)}, u32[]{:S(2)}) copy-start(bf16[512,2048]{1,0:T(8,128)(2,1)} %copy.45.dq_ref) | copy-start | bytes 6291460
  114.5 1.2 copy-start.2
  115.7 1.2 copy-start.3

commit v4 on v3

--- a/solution.py
+++ b/solution.py
@@ -205,7 +205,7 @@
             q_s[pl.ds(r0, blk), pl.ds(c0, 128)] = (x * cos + _swap_halves(x) * sin).astype(jnp.bfloat16)
             return carry2
 
-        lax.fori_loop(0, q_chunks, q_col, 0)
+        lax.fori_loop(0, q_chunks, q_col, 0, unroll=True)
         for c in range(k_chunks):
             x = kb_ref[pl.ds(r0, blk), c * 128:(c + 1) * 128]
             k = (x * cos + _swap_halves(x) * sin).astype(jnp.bfloat16).astype(jnp.float32)
@@ -259,7 +259,7 @@
             out_ref[pl.ds(q0, blk), pl.ds(c0, 128)] = o.astype(out_ref.dtype)
             return carry2
 
-        lax.fori_loop(0, HEADS // 2, head_pair, 0)
+        lax.fori_loop(0, HEADS // 2, head_pair, 0, unroll=True)
         return carry
 
     lax.fori_loop(0, n_blk, query_block, 0)

time: 157 us -> 143 us (0.911)
  Pallas kernels: 39.6 us -> 25.2 us
    pallas_call x1, Pallas kernels: 39.6 us -> 25.2 us  [fused_attention(): pl.pallas_call(_attend_kernel, out_shape=jax.ShapeDtypeStruct((rows, HEAD...]
  transfers between devices with their start and end apart: 4 -> 4, of which waited for: 4 -> 4; matrix products, arithmetic and copies ran while one was open for 27% -> 30% of each run, Pallas kernels for 0% -> 0%
where the time goes in v4:
time: 143 us; the launch traced here: 142 us
  starting transfers between devices  27.1 us (19%)
  waiting for transfers between devices  25.9 us (18%)
  Pallas kernels  25.2 us (18%)
  matrix products  24.2 us (17%)
  local copies, waits for them, and re-layouts  23.7 us (17%)
  other arithmetic  15.9 us (11%)
    pallas_call x1, Pallas kernels, fused_attention(): pl.pallas_call(_attend_kernel, out_shape=jax.ShapeDtypeStruct((rows, HEAD...  25.2 us
    all_to_all x1, starting transfers between devices, local(): lax.all_to_all(jnp.broadcast_to(adapter_per_request, (device_total, reque...  11.5 us
    unnamed x23, local copies, waits for them, and re-layouts  10.2 us
    dot_general x1, matrix products, local(): jnp.dot(normalized_hidden_states, query_weight_matrix, preferred_element_...  9.39 us
    all_to_all x1, waiting for transfers between devices, local(): lax.all_to_all(jnp.take(adapter_down_weight, local_pick, axis=0), axes, 0...  7.49 us
    all_to_all x1, waiting for transfers between devices, local(): lax.all_to_all(jnp.take(adapter_up_query_weight, local_pick, axis=0), axe...  6.95 us
    all_to_all x1, waiting for transfers between devices, local(): lax.all_to_all(jnp.take(adapter_up_value_weight, local_pick, axis=0), axe...  6.23 us
    all_to_all x1, starting transfers between devices, local(): lax.all_to_all(jnp.take(adapter_up_query_weight, local_pick, axis=0), axe...  6.05 us
  transfers between devices with their start and end apart: 4, of which 4 were waited for; matrix products, arithmetic and copies ran while one was open for 30% of the time, Pallas kernels for 0%

profile of v4, /device:TPU:1, one launch (start us, length us, event | category | flops | bytes accessed | tf_op | source)
XLA Modules:
  0.0 142.2 jit_solution(6713467291333776319)
XLA Ops:
  0.0 0.0 copy-start
  0.0 1.5 %broadcast_in_dim.103 = s32[128,1,16]{2,1,0:T(1,128)} broadcast(s32[16]{0:T(128)} %bitcast.65), dimensions={2} | broadcast | bytes 8256 | tf_op jit(solution)/shard_map/broadcast_in_dim | solution.py:133
  1.5 11.5 %all-to-all-start = ((s32[128,1,16]{2,1,0:T(1,128)}), s32[128,1,16]{2,1,0:T(1,128)S(1)}, u32[]{:S(2)}, u32[]{:S(2)}) async-start(s32[128,1,16]{2,1,0:T(1,128)} %broadcast_in_dim.103), calls=%async_computation | async-start | bytes 131072 | tf_op jit(solution)/shard_map/all_to_all | solution.py:132
  13.0 0.7 copy.33
  13.7 0.1 reduce
  13.9 0.7 fusion.22
  14.5 0.1 convert_reduce_fusion
  14.6 0.9 select_reduce_fusion.3
  15.5 0.1 select_reduce_fusion.1
  15.6 0.0 copy-start.4
  15.6 1.8 %fusion.15 = (f32[512,32]{1,0:T(8,128)S(1)}, f32[512,32]{1,0:T(8,128)}, f32[512,32]{1,0:T(8,128)}) fusion(f32[32]{0:T(128)S(1)} %negate_power_fusion, f32[512]{0:T(512)S(1)} %subtract_convert_fusion), kind=kLoop, calls=%fused_computation.29 | loop fusion | flops 32768 | bytes 198784 | tf_op jit(solution)/shard_map/neg | solution.py:275
  17.5 5.2 %all-to-all-done = s32[128,1,16]{2,1,0:T(1,128)S(1)} async-done(((s32[128,1,16]{2,1,0:T(1,128)}), s32[128,1,16]{2,1,0:T(1,128)S(1)}, u32[]{:S(2)}, u32[]{:S(2)}) %all-to-all-start) | async-done | bytes 8224 | tf_op jit(solution)/shard_map/all_to_all | solution.py:132
  22.7 3.3 %select_reduce_fusion = s32[128,16]{1,0:T(8,128)S(1)} fusion(s32[512]{0:T(512)} %param.17, s32[128,16]{1,0:T(8,128)S(1)} %bitcast.63), kind=kLoop, calls=%fused_computation.4 | loop fusion | flops 3143680 | bytes 18432 | tf_op jit(solution)/shard_map/reduce_sum | solution.py:35
  26.0 0.1 fusion.18
  26.2 2.4 %gather_fusion.2 = bf16[128,16,64]{2,1,0:T(8,128)(2,1)} fusion(bf16[32,16,64]{2,1,0:T(8,128)(2,1)} %param.16, s32[1024]{0:T(1024)S(1)} %pad_clamp_fusion), kind=kCustom, calls=%fused_computation.2 | custom fusion | bytes 524800 | tf_op jit(solution)/shard_map/jit(_take)/gather | solution.py:145
  28.6 1.2 broadcast_select_fusion.2
  29.8 1.0 reshape.162
  30.8 4.5 %all-to-all-start.3 = ((bf16[128,2,512]{2,1,0:T(2,128)(2,1)}), bf16[128,2,512]{2,1,0:T(2,128)(2,1)S(1)}, u32[]{:S(2)}, u32[]{:S(2)}) async-start(bf16[128,2,512]{2,1,0:T(2,128)(2,1)} %reshape.162), calls=%async_computation.3 | async-start | bytes 524288 | tf_op jit(solution)/shard_map/all_to_all | solution.py:144
  35.4 0.0 copy-done.4
  35.4 2.0 %gather_fusion = bf16[128,32,256]{2,1,0:T(8,128)(2,1)} fusion(bf16[32,32,256]{2,1,0:T(8,128)(2,1)S(1)} %copy-done.4, s32[1024]{0:T(1024)S(1)} %pad_clamp_fusion), kind=kCustom, calls=%fused_computation | custom fusion | bytes 4194816 | tf_op jit(solution)/shard_map/jit(_take)/gather | solution.py:139
  37.4 3.2 %broadcast_select_fusion = bf16[128,32,256]{2,1,0:T(8,128)(2,1)} fusion(bf16[128,32,256]{2,1,0:T(8,128)(2,1)} %gather_fusion, pred[128]{0:T(512)(128)(4,1)S(1)} %compare_and_fusion), kind=kLoop, calls=%fused_computation.8 | loop fusion | flops 1048576 | bytes 4194432 | tf_op jit(solution)/shard_map/jit(_take)/select_n | solution.py:139
  40.6 0.0 copy-start.8
  40.6 6.2 %all-to-all-done.3 = bf16[128,2,512]{2,1,0:T(2,128)(2,1)S(1)} async-done(((bf16[128,2,512]{2,1,0:T(2,128)(2,1)}), bf16[128,2,512]{2,1,0:T(2,128)(2,1)S(1)}, u32[]{:S(2)}, u32[]{:S(2)}) %all-to-all-start.3) | async-done | bytes 262176 | tf_op jit(solution)/shard_map/all_to_all | solution.py:144
  46.8 0.0 copy-start.7
  46.8 5.0 %all-to-all-start.1 = ((bf16[128,32,256]{2,1,0:T(8,128)(2,1)}), bf16[128,32,256]{2,1,0:T(8,128)(2,1)}, u32[]{:S(2)}, u32[]{:S(2)}) async-start(bf16[128,32,256]{2,1,0:T(8,128)(2,1)} %broadcast_select_fusion), calls=%async_computation.1 | async-start | bytes 4194304 | tf_op jit(solution)/shard_map/all_to_all | solution.py:138
  51.8 0.0 copy-done.7
  51.8 0.0 copy-done.8
  51.8 1.8 %pad_maximum_fusion = (f32[512,128]{1,0:T(8,128)S(1)}, f32[512,128]{1,0:T(8,128)S(1)}) fusion(f32[512,32]{1,0:T(8,128)} %get-tuple-element.9, f32[512,32]{1,0:T(8,128)S(1)} %copy-done.8, f32[512,32]{1,0:T(8,128)S(1)} %get-tuple-element.7), kind=kLoop, calls=%fused_computation.21 | loop fusion | flops 393216 | bytes 720896 | tf_op jit(solution)/shard_map/concatenate | solution.py:274
  53.7 0.1 copy.38
  53.8 0.0 copy-start.6
  53.8 3.8 %copy.47 = bf16[64,8,8,256]{3,2,1,0:T(8,128)(2,1)} copy(bf16[64,8,8,256]{3,1,2,0:T(8,128)(2,1)} %bitcast.59) | data formatting | bytes 4194304
  57.6 0.0 copy-done
  57.6 0.0 copy-done.6
  57.6 2.3 %fusion.24.kb_ref = f32[512,512]{1,0:T(8,128)} fusion(bf16[512,2048]{1,0:T(8,128)(2,1)S(1)} %copy-done.6, bf16[2048,512]{1,0:T(8,128)(2,1)S(1)} %copy-done), kind=kOutput, calls=%fused_computation.58 | convolution fusion | flops 1073741824 | bytes 5242880 | tf_op jit(solution)/shard_map/dot_general | solution.py:175
  60.0 0.0 copy-start.5
  60.0 9.4 %fusion.23.qb_ref = f32[512,2048]{1,0:T(8,128)} fusion(bf16[512,2048]{1,0:T(8,128)(2,1)S(1)} %copy-done.6, bf16[2048,2048]{1,0:T(8,128)(2,1)} %param.11), kind=kOutput, calls=%fused_computation.57 | convolution fusion | flops 4294967296 | bytes 14680064 | tf_op jit(solution)/shard_map/dot_general | solution.py:172
  69.4 0.0 copy-done.5
  69.4 1.6 %gather_fusion.1 = bf16[128,16,256]{2,1,0:T(8,128)(2,1)} fusion(bf16[32,16,256]{2,1,0:T(8,128)(2,1)S(1)} %copy-done.5, s32[1024]{0:T(1024)S(1)} %pad_clamp_fusion), kind=kCustom, calls=%fused_computation.1 | custom fusion | bytes 2097664 | tf_op jit(solution)/shard_map/jit(_take)/gather | solution.py:142
  71.0 2.4 %broadcast_select_fusion.1 = bf16[128,16,256]{2,1,0:T(8,128)(2,1)} fusion(bf16[128,16,256]{2,1,0:T(8,128)(2,1)} %gather_fusion.1, pred[128]{0:T(512)(128)(4,1)S(1)} %compare_and_fusion), kind=kLoop, calls=%fused_computation.15 | loop fusion | flops 524288 | bytes 2097280 | tf_op jit(solution)/shard_map/jit(_take)/select_n | solution.py:142
  73.4 7.5 %all-to-all-done.1 = bf16[128,32,256]{2,1,0:T(8,128)(2,1)} async-done(((bf16[128,32,256]{2,1,0:T(8,128)(2,1)}), bf16[128,32,256]{2,1,0:T(8,128)(2,1)}, u32[]{:S(2)}, u32[]{:S(2)}) %all-to-all-start.1) | async-done | bytes 2097184 | tf_op jit(solution)/shard_map/all_to_all | solution.py:138
  80.9 6.1 %all-to-all-start.2 = ((bf16[128,16,256]{2,1,0:T(8,128)(2,1)}), bf16[128,16,256]{2,1,0:T(8,128)(2,1)}, u32[]{:S(2)}, u32[]{:S(2)}) async-start(bf16[128,16,256]{2,1,0:T(8,128)(2,1)} %broadcast_select_fusion.1), calls=%async_computation.2 | async-start | bytes 2097152 | tf_op jit(solution)/shard_map/all_to_all | solution.py:141
  86.9 4.4 %fusion.25.vb_ref = f32[512,512]{1,0:T(8,128)} fusion(bf16[512,2048]{1,0:T(8,128)(2,1)} %param.10, bf16[2048,512]{1,0:T(8,128)(2,1)} %param.13), kind=kOutput, calls=%fused_computation.59 | convolution fusion | flops 1073741824 | bytes 5242880 | tf_op jit(solution)/shard_map/dot_general | solution.py:178
  91.4 1.3 reshape.163
  92.7 3.5 %fusion.12 = bf16[512,16,32]{0,2,1:T(8,128)(2,1)S(1)} fusion(bf16[8,16,32,256]{3,2,1,0:T(8,128)(2,1)} %bitcast.5, bf16[512,8,256,1]{2,1,0,3:T(8,128)(2,1)} %bitcast.60, pred[512,16]{0,1:T(8,128)(4,1)S(1)} %iota_compare_fusion.1), kind=kOutput, calls=%fused_computation.14 | convolution fusion | flops 1074266112 | bytes 4726784 | tf_op jit(solution)/shard_map/tsf,sorf->tor/dot_general | solution.py:160
  96.2 0.0 copy-start.9
  96.2 1.1 fusion.8
  97.4 0.0 copy-done.9
  97.4 1.3 copy.39.dv_ref
  98.6 6.9 %all-to-all-done.2 = bf16[128,16,256]{2,1,0:T(8,128)(2,1)} async-done(((bf16[128,16,256]{2,1,0:T(8,128)(2,1)}), bf16[128,16,256]{2,1,0:T(8,128)(2,1)}, u32[]{:S(2)}, u32[]{:S(2)}) %all-to-all-start.2) | async-done | bytes 1048608 | tf_op jit(solution)/shard_map/all_to_all | solution.py:141
  105.6 3.4 %bitcast_convert_fusion = bf16[512,8,256]{0,2,1:T(8,128)(2,1)} fusion(bf16[8,16,16,256]{3,2,1,0:T(8,128)(2,1)} %bitcast.10, bf16[512,16,32]{0,2,1:T(8,128)(2,1)} %copy-done.9), kind=kOutput, calls=%fused_computation.3 | convolution fusion | flops 537919488 | bytes 3407872 | tf_op jit(solution)/shard_map/tor,sorf->tsf/dot_general | solution.py:165
  109.0 3.9 %copy.45.dq_ref = bf16[512,2048]{1,0:T(8,128)(2,1)} copy(bf16[512,2048]{0,1:T(8,128)(2,1)} %bitcast.58) | data formatting | bytes 4194304 | tf_op jit(solution)/shard_map/reshape | solution.py:167
  112.9 0.0 copy-start.1
  112.9 1.6 %copy-done.1 = bf16[512,2048]{1,0:T(8,128)(2,1)S(1)} copy-done((bf16[512,2048]{1,0:T(8,128)(2,1)S(1)}, bf16[512,2048]{1,0:T(8,128)(2,1)}, u32[]{:S(2)}) %copy-start.1) | copy-done | bytes 2097176
  114.5 0.0 copy-start.2
  114.5 1.2 copy-done.2
  115.7 0.0 copy-start.3
  115.7 1.2 copy-done.3
  117.0 25.2 %shard_map.100 = bf16[512,2048]{1,0:T(8,128)(2,1)} custom-call(f32[512,2048]{1,0:T(8,128)} %fusion.23.qb_ref, bf16[512,2048]{1,0:T(8,128)(2,1)S(1)} %copy-done.1, f32[512,512]{1,0:T(8,128)S(1)} %copy-done.2, f32[512,512]{1,0:T(8,128)S(1)} %copy-done.3, bf16[512,512]{1,0:T(8,128)(2,1)S(1)} %copy.39.dv_ref, f32[512,128]{1,0:T(8,128)S(1)} %get-tuple-element.10.cos_ref, ...), custom_call_target="tpu_custom_call" | custom-call | flops 2147483648 | bytes 9961472 | tf_op jit(solution)/shard_map/pallas_call | solution.py:285
  (9 shorter events, 0.1 us)
Async XLA Ops:
  0.0 57.6 %copy-start = (bf16[2048,512]{1,0:T(8,128)(2,1)S(1)}, bf16[2048,512]{1,0:T(8,128)(2,1)}, u32[]{:S(2)}) copy-start(bf16[2048,512]{1,0:T(8,128)(2,1)} %param.12) | copy-start | bytes 6291460
  1.5 21.2 %all-to-all-start = ((s32[128,1,16]{2,1,0:T(1,128)}), s32[128,1,16]{2,1,0:T(1,128)S(1)}, u32[]{:S(2)}, u32[]{:S(2)}) async-start(s32[128,1,16]{2,1,0:T(1,128)} %broadcast_in_dim.103), calls=%async_computation | async-start | bytes 131072 | tf_op jit(solution)/shard_map/all_to_all | solution.py:132
  15.6 19.8 %copy-start.4 = (bf16[32,32,256]{2,1,0:T(8,128)(2,1)S(1)}, bf16[32,32,256]{2,1,0:T(8,128)(2,1)}, u32[]{:S(2)}) copy-start(bf16[32,32,256]{2,1,0:T(8,128)(2,1)} %param.14) | copy-start | bytes 1572868
  30.8 16.0 %all-to-all-start.3 = ((bf16[128,2,512]{2,1,0:T(2,128)(2,1)}), bf16[128,2,512]{2,1,0:T(2,128)(2,1)S(1)}, u32[]{:S(2)}, u32[]{:S(2)}) async-start(bf16[128,2,512]{2,1,0:T(2,128)(2,1)} %reshape.162), calls=%async_computation.3 | async-start | bytes 524288 | tf_op jit(solution)/shard_map/all_to_all | solution.py:144
  40.6 11.3 %copy-start.8 = (f32[512,32]{1,0:T(8,128)S(1)}, f32[512,32]{1,0:T(8,128)}, u32[]{:S(2)}) copy-start(f32[512,32]{1,0:T(8,128)} %get-tuple-element.8) | copy-start | bytes 196612
  46.8 5.0 %copy-start.7 = (bf16[128,2,512]{2,1,0:T(2,128)(2,1)}, bf16[128,2,512]{2,1,0:T(2,128)(2,1)S(1)}, u32[]{:S(2)}) copy-start(bf16[128,2,512]{2,1,0:T(2,128)(2,1)S(1)} %all-to-all-done.3) | copy-start | bytes 786436
  46.8 34.1 %all-to-all-start.1 = ((bf16[128,32,256]{2,1,0:T(8,128)(2,1)}), bf16[128,32,256]{2,1,0:T(8,128)(2,1)}, u32[]{:S(2)}, u32[]{:S(2)}) async-start(bf16[128,32,256]{2,1,0:T(8,128)(2,1)} %broadcast_select_fusion), calls=%async_computation.1 | async-start | bytes 4194304 | tf_op jit(solution)/shard_map/all_to_all | solution.py:138
  53.8 3.8 %copy-start.6 = (bf16[512,2048]{1,0:T(8,128)(2,1)S(1)}, bf16[512,2048]{1,0:T(8,128)(2,1)}, u32[]{:S(2)}) copy-start(bf16[512,2048]{1,0:T(8,128)(2,1)} %param.10) | copy-start | bytes 6291460
  60.0 9.4 %copy-start.5 = (bf16[32,16,256]{2,1,0:T(8,128)(2,1)S(1)}, bf16[32,16,256]{2,1,0:T(8,128)(2,1)}, u32[]{:S(2)}) copy-start(bf16[32,16,256]{2,1,0:T(8,128)(2,1)} %param.15) | copy-start | bytes 786436
  80.9 24.7 %all-to-all-start.2 = ((bf16[128,16,256]{2,1,0:T(8,128)(2,1)}), bf16[128,16,256]{2,1,0:T(8,128)(2,1)}, u32[]{:S(2)}, u32[]{:S(2)}) async-start(bf16[128,16,256]{2,1,0:T(8,128)(2,1)} %broadcast_select_fusion.1), calls=%async_computation.2 | async-start | bytes 2097152 | tf_op jit(solution)/shard_map/all_to_all | solution.py:141
  96.2 1.2 copy-start.9
  112.9 1.6 %copy-start.1 = (bf16[512,2048]{1,0:T(8,128)(2,1)S(1)}, bf16[512,2048]{1,0:T(8,128)(2,1)}, u32[]{:S(2)}) copy-start(bf16[512,2048]{1,0:T(8,128)(2,1)} %copy.45.dq_ref) | copy-start | bytes 6291460
  114.5 1.2 copy-start.2
  115.7 1.2 copy-start.3

commit v5 on v4

--- a/solution.py
+++ b/solution.py
@@ -135,15 +135,18 @@
     all_slots = table_lookup(adapter_panel_slot, all_lists)
     mine = all_slots // ADP_DEV == my_store
     local_pick = jnp.sum(jnp.where(mine, all_slots % ADP_DEV, 0), axis=1)
-    down = lax.all_to_all(
-        jnp.take(adapter_down_weight, local_pick, axis=0), axes, 0, 0, tiled=True
-    ).reshape(serve_count, store_count, rank2, cols)
-    upq = lax.all_to_all(
-        jnp.take(adapter_up_query_weight, local_pick, axis=0), axes, 0, 0, tiled=True
-    ).reshape(serve_count, store_count, ADAPTER_RANK, cols)
-    upv = lax.all_to_all(
-        jnp.take(adapter_up_value_weight, local_pick, axis=0), axes, 0, 0, tiled=True
-    ).reshape(serve_count, store_count, ADAPTER_RANK, vcols)
+    picked = [jnp.take(panel, local_pick, axis=0, mode="clip")
+              for panel in (adapter_down_weight, adapter_up_query_weight, adapter_up_value_weight)]
+    send = jnp.concatenate(
+        [picked[0][:, :ADAPTER_RANK], picked[0][:, ADAPTER_RANK:], picked[1], picked[2]], axis=2
+    )
+    got = lax.all_to_all(send, axes, 0, 0, tiled=True).reshape(
+        serve_count, store_count, ADAPTER_RANK, send.shape[2]
+    )
+    down_q = got[..., :cols]
+    down_v = got[..., cols : 2 * cols]
+    upq = got[..., 2 * cols : 3 * cols]
+    upv = got[..., 3 * cols : 3 * cols + vcols]
 
     lengths = request_token_length[0]
     adapters = adapter_per_request[0]
@@ -157,16 +160,19 @@
     owner_token = jnp.sum(jnp.where(member, owners[None, :], 0), axis=1)
 
     states3 = normalized_hidden_states.reshape(tok_rows, serve_count, cols)
-    low = jnp.einsum(
-        "tsf,sorf->tor", states3, down, preferred_element_type=jnp.float32
-    ).astype(jnp.bfloat16)
     owner_mask = owner_token[:, None, None] == jnp.arange(store_count, dtype=jnp.int32)[None, :, None]
-    low = jnp.where(owner_mask, low, jnp.zeros((), jnp.bfloat16))
+
+    def low_part(down_half):
+        low = jnp.einsum(
+            "tsf,sorf->tor", states3, down_half, preferred_element_type=jnp.float32
+        ).astype(jnp.bfloat16)
+        return jnp.where(owner_mask, low, jnp.zeros((), jnp.bfloat16))
+
     delta_query = jnp.einsum(
-        "tor,sorf->tsf", low[..., :ADAPTER_RANK], upq, preferred_element_type=jnp.float32
+        "tor,sorf->tsf", low_part(down_q), upq, preferred_element_type=jnp.float32
     ).astype(jnp.bfloat16).reshape(tok_rows, serve_count * cols)
     delta_value = jnp.einsum(
-        "tor,sorf->tsf", low[..., ADAPTER_RANK:], upv, preferred_element_type=jnp.float32
+        "tor,sorf->tsf", low_part(down_v), upv, preferred_element_type=jnp.float32
     ).astype(jnp.bfloat16).reshape(tok_rows, serve_count * vcols)
 
     q_base = jnp.dot(

time: 143 us -> 131 us (0.916)
  waiting for transfers between devices: 25.9 us -> 37.1 us
  starting transfers between devices: 27.1 us -> 16.7 us
  other arithmetic: 15.9 us -> 8.92 us
  matrix products: 24.2 us -> 19.5 us
    all_to_all x3 -> x1, starting transfers between devices: 15.6 us -> 5.25 us  [local(): lax.all_to_all(send, axes, 0, 0, tiled=True)]
    all_to_all x3 -> x1, waiting for transfers between devices: 20.7 us -> 29.8 us  [local(): lax.all_to_all(send, axes, 0, 0, tiled=True)]
    select_n x4 -> x0, other arithmetic: 6.82 us -> none  [the longest x2 3.18 us: local(): jnp.take(adapter_down_weight, local_pick, axis=0)]
    dot_general x1, matrix products: 9.39 us -> 6.02 us  [local(): jnp.dot(normalized_hidden_states, query_weight_matrix, preferred_element_...]
    unnamed x23, local copies, waits for them, and re-layouts: 10.2 us -> 7.76 us
    dot_general x1, matrix products: 4.45 us -> 2.3 us  [local(): jnp.dot(normalized_hidden_states, value_weight_matrix, preferred_element_...]
    all_to_all x1, waiting for transfers between devices: 5.24 us -> 7.32 us  [local(): lax.all_to_all(jnp.broadcast_to(adapter_per_request, (device_total, reque...]
    concatenate x0 -> x1, other arithmetic: none -> 2.08 us  [local(): jnp.concatenate([picked[0][:, :ADAPTER_RANK], picked[0][:, ADAPTER_RANK:]...]
  transfers between devices with their start and end apart: 4 -> 2, of which waited for: 4 -> 2; matrix products, arithmetic and copies ran while one was open for 30% -> 14% of each run, Pallas kernels for 0% -> 0%
where the time goes in v5:
time: 131 us; the launch traced here: 130 us
  waiting for transfers between devices  37.1 us (28%)
  Pallas kernels  25.4 us (19%)
  local copies, waits for them, and re-layouts  22.3 us (17%)
  matrix products  19.5 us (15%)
  starting transfers between devices  16.7 us (13%)
  other arithmetic  8.92 us (7%)
    all_to_all x1, waiting for transfers between devices, local(): lax.all_to_all(send, axes, 0, 0, tiled=True)  29.8 us
    pallas_call x1, Pallas kernels, fused_attention(): pl.pallas_call(_attend_kernel, out_shape=jax.ShapeDtypeStruct((rows, HEAD...  25.4 us
    all_to_all x1, starting transfers between devices, local(): lax.all_to_all(jnp.broadcast_to(adapter_per_request, (device_total, reque...  11.5 us
    unnamed x23, local copies, waits for them, and re-layouts  7.76 us
    all_to_all x1, waiting for transfers between devices, local(): lax.all_to_all(jnp.broadcast_to(adapter_per_request, (device_total, reque...  7.32 us
    dot_general x1, matrix products, local(): jnp.dot(normalized_hidden_states, query_weight_matrix, preferred_element_...  6.02 us
    all_to_all x1, starting transfers between devices, local(): lax.all_to_all(send, axes, 0, 0, tiled=True)  5.25 us
    gather x3, local copies, waits for them, and re-layouts, local(): jnp.take(panel, local_pick, axis=0, mode='clip')  5.24 us
  transfers between devices with their start and end apart: 2, of which 2 were waited for; matrix products, arithmetic and copies ran while one was open for 14% of the time, Pallas kernels for 0%

profile of v5, /device:TPU:1, one launch (start us, length us, event | category | flops | bytes accessed | tf_op | source)
XLA Modules:
  0.0 130.2 jit_solution(767209298025684100)
XLA Ops:
  0.0 0.0 copy-start
  0.0 0.0 copy-start.6
  0.0 0.0 copy-start.4
  0.0 1.5 %broadcast_in_dim.85 = s32[128,1,16]{2,1,0:T(1,128)} broadcast(s32[16]{0:T(128)} %bitcast.87), dimensions={2} | broadcast | bytes 8256 | tf_op jit(solution)/shard_map/broadcast_in_dim | solution.py:133
  1.5 11.5 %all-to-all-start = ((s32[128,1,16]{2,1,0:T(1,128)}), s32[128,1,16]{2,1,0:T(1,128)S(1)}, u32[]{:S(2)}, u32[]{:S(2)}) async-start(s32[128,1,16]{2,1,0:T(1,128)} %broadcast_in_dim.85), calls=%async_computation | async-start | bytes 131072 | tf_op jit(solution)/shard_map/all_to_all | solution.py:132
  13.0 0.7 copy.32
  13.7 0.1 reduce
  13.9 0.7 fusion.55
  14.5 0.9 select_reduce_fusion.3
  15.4 7.3 %all-to-all-done = s32[128,1,16]{2,1,0:T(1,128)S(1)} async-done(((s32[128,1,16]{2,1,0:T(1,128)}), s32[128,1,16]{2,1,0:T(1,128)S(1)}, u32[]{:S(2)}, u32[]{:S(2)}) %all-to-all-start) | async-done | bytes 8224 | tf_op jit(solution)/shard_map/all_to_all | solution.py:132
  22.7 3.3 %select_reduce_fusion = s32[128,16]{1,0:T(8,128)S(1)} fusion(s32[512]{0:T(512)} %param.17, s32[128,16]{1,0:T(8,128)S(1)} %bitcast.85), kind=kLoop, calls=%fused_computation.4 | loop fusion | flops 3143680 | bytes 18432 | tf_op jit(solution)/shard_map/reduce_sum | solution.py:35
  26.0 0.1 fusion.52
  26.2 1.6 %gather_fusion.2 = bf16[128,16,64]{2,1,0:T(8,128)(2,1)S(1)} fusion(bf16[32,16,64]{2,1,0:T(8,128)(2,1)} %param.16, s32[1024]{0:T(1024)S(1)} %pad_clamp_fusion), kind=kCustom, calls=%fused_computation.2 | custom fusion | bytes 524800 | tf_op jit(solution)/shard_map/jit(_take)/gather | solution.py:138
  27.8 0.0 copy-done.6
  27.8 1.6 %gather_fusion.1 = bf16[128,16,256]{2,1,0:T(8,128)(2,1)} fusion(bf16[32,16,256]{2,1,0:T(8,128)(2,1)S(1)} %copy-done.6, s32[1024]{0:T(1024)S(1)} %pad_clamp_fusion), kind=kCustom, calls=%fused_computation.1 | custom fusion | bytes 2097664 | tf_op jit(solution)/shard_map/jit(_take)/gather | solution.py:138
  29.4 0.0 copy-done.4
  29.4 2.0 %gather_fusion = bf16[128,32,256]{2,1,0:T(8,128)(2,1)} fusion(bf16[32,32,256]{2,1,0:T(8,128)(2,1)S(1)} %copy-done.4, s32[1024]{0:T(1024)S(1)} %pad_clamp_fusion), kind=kCustom, calls=%fused_computation | custom fusion | bytes 4194816 | tf_op jit(solution)/shard_map/jit(_take)/gather | solution.py:138
  31.4 0.0 copy-start.5
  31.4 1.8 %fusion.58 = (bf16[128,16,256]{2,1,0:T(8,128)(2,1)S(1)}, bf16[128,16,256]{2,1,0:T(8,128)(2,1)S(1)}) fusion(bf16[128,32,256]{2,1,0:T(8,128)(2,1)} %gather_fusion), kind=kLoop, calls=%fused_computation.67 | loop fusion | bytes 4194304 | tf_op jit(solution)/shard_map/slice | solution.py:141
  33.2 0.1 copy-done.5
  33.3 2.1 %pad_maximum_fusion = bf16[128,16,832]{2,1,0:T(8,128)(2,1)} fusion(bf16[128,16,64]{2,1,0:T(8,128)(2,1)S(1)} %gather_fusion.2, bf16[128,16,256]{2,1,0:T(8,128)(2,1)S(1)} %copy-done.5, bf16[128,16,256]{2,1,0:T(8,128)(2,1)S(1)} %get-tuple-element.8, bf16[128,16,256]{2,1,0:T(8,128)(2,1)S(1)} %get-tuple-element.7), kind=kLoop, calls=%fused_computation.6 | loop fusion | flops 13631488 | bytes 6815744 | tf_op jit(solution)/shard_map/concatenate | solution.py:140
  35.4 5.3 %all-to-all-start.1 = ((bf16[128,16,832]{2,1,0:T(8,128)(2,1)}), bf16[128,16,832]{2,1,0:T(8,128)(2,1)}, u32[]{:S(2)}, u32[]{:S(2)}) async-start(bf16[128,16,832]{2,1,0:T(8,128)(2,1)} %pad_maximum_fusion), calls=%async_computation.1 | async-start | bytes 7340032 | tf_op jit(solution)/shard_map/all_to_all | solution.py:143
  40.7 0.1 convert_reduce_fusion
  40.8 0.1 select_reduce_fusion.1
  40.8 0.1 copy.38
  41.0 3.6 %copy.50 = bf16[64,8,8,256]{3,2,1,0:T(8,128)(2,1)} copy(bf16[64,8,8,256]{3,1,2,0:T(8,128)(2,1)} %bitcast.80) | data formatting | bytes 4194304
  44.6 0.0 copy-start.7
  44.6 1.0 fusion.49
  45.6 0.5 pad_maximum_fusion.1
  46.1 0.0 copy-start.8
  46.1 0.0 slice-start
  46.2 0.0 copy-done
  46.2 0.0 copy-done.7
  46.2 0.0 slice-start.1
  46.2 2.2 %fusion.60.kb_ref = f32[512,512]{1,0:T(8,128)} fusion(bf16[512,2048]{1,0:T(8,128)(2,1)S(1)} %copy-done.7, bf16[2048,512]{1,0:T(8,128)(2,1)S(1)} %copy-done), kind=kOutput, calls=%fused_computation.69 | convolution fusion | flops 1073741824 | bytes 5242880 | tf_op jit(solution)/shard_map/dot_general | solution.py:181
  48.4 0.0 copy-done.8
  48.4 2.3 %fusion.61.vb_ref = f32[512,512]{1,0:T(8,128)} fusion(bf16[512,2048]{1,0:T(8,128)(2,1)S(1)} %copy-done.7, bf16[2048,512]{1,0:T(8,128)(2,1)S(1)} %copy-done.8), kind=kOutput, calls=%fused_computation.70 | convolution fusion | flops 1073741824 | bytes 5242880 | tf_op jit(solution)/shard_map/dot_general | solution.py:184
  50.7 0.0 slice-done
  50.7 0.0 slice-done.1
  50.7 6.0 %fusion.59.qb_ref = f32[512,2048]{1,0:T(8,128)} fusion(bf16[512,2048]{1,0:T(8,128)(2,1)S(1)} %copy-done.7, bf16[2048,2048]{1,0:T(8,128)(2,1)S(1)} %bitcast.91), kind=kOutput, calls=%fused_computation.68 | convolution fusion | flops 4294967296 | bytes 14680064 | tf_op jit(solution)/shard_map/dot_general | solution.py:178
  56.8 29.8 %all-to-all-done.1 = bf16[128,16,832]{2,1,0:T(8,128)(2,1)} async-done(((bf16[128,16,832]{2,1,0:T(8,128)(2,1)}), bf16[128,16,832]{2,1,0:T(8,128)(2,1)}, u32[]{:S(2)}, u32[]{:S(2)}) %all-to-all-start.1) | async-done | bytes 3407904 | tf_op jit(solution)/shard_map/all_to_all | solution.py:143
  86.6 3.9 %fusion.4 = bf16[512,8,64]{0,2,1:T(8,128)(2,1)} fusion(bf16[512,8,256,1]{2,1,0,3:T(8,128)(2,1)} %bitcast.81, bf16[8,16,16,832]{3,2,1,0:T(8,128)(2,1)} %bitcast.3, pred[512,16]{0,1:T(8,128)(4,1)S(1)} %iota_compare_fusion.1), kind=kOutput, calls=%fused_computation.12 | convolution fusion | flops 671612928 | bytes 4202496 | tf_op jit(solution)/shard_map/tor,sorf->tsf/dot_general | solution.py:174
  90.5 5.1 %bitcast_convert_fusion = bf16[512,8,256]{0,2,1:T(8,128)(2,1)} fusion(bf16[512,8,256,1]{2,1,0,3:T(8,128)(2,1)} %bitcast.82, bf16[8,16,16,832]{3,2,1,0:T(8,128)(2,1)} %bitcast.3, pred[512,16]{0,1:T(8,128)(4,1)S(1)} %iota_compare_fusion.1), kind=kOutput, calls=%fused_computation.3 | convolution fusion | flops 1075052544 | bytes 6299648 | tf_op jit(solution)/shard_map/tor,sorf->tsf/dot_general | solution.py:171
  95.5 3.9 %copy.46.dq_ref = bf16[512,2048]{1,0:T(8,128)(2,1)} copy(bf16[512,2048]{0,1:T(8,128)(2,1)} %bitcast.83) | data formatting | bytes 4194304 | tf_op jit(solution)/shard_map/reshape | solution.py:173
  99.5 1.3 copy.39.dv_ref
  100.7 0.0 copy-start.1
  100.7 1.6 %copy-done.1 = bf16[512,2048]{1,0:T(8,128)(2,1)S(1)} copy-done((bf16[512,2048]{1,0:T(8,128)(2,1)S(1)}, bf16[512,2048]{1,0:T(8,128)(2,1)}, u32[]{:S(2)}) %copy-start.1) | copy-done | bytes 2097176
  102.3 0.0 copy-start.2
  102.3 1.2 copy-done.2
  103.5 0.0 copy-start.3
  103.5 1.2 copy-done.3
  104.8 25.4 %shard_map.100 = bf16[512,2048]{1,0:T(8,128)(2,1)} custom-call(f32[512,2048]{1,0:T(8,128)} %fusion.59.qb_ref, bf16[512,2048]{1,0:T(8,128)(2,1)S(1)} %copy-done.1, f32[512,512]{1,0:T(8,128)S(1)} %copy-done.2, f32[512,512]{1,0:T(8,128)S(1)} %copy-done.3, bf16[512,512]{1,0:T(8,128)(2,1)S(1)} %copy.39.dv_ref, f32[512,128]{1,0:T(8,128)S(1)} %get-tuple-element.12.cos_ref, ...), custom_call_target="tpu_custom_call" | custom-call | flops 2147483648 | bytes 9961472 | tf_op jit(solution)/shard_map/pallas_call | solution.py:291
  (8 shorter events, 0.1 us)
Async XLA Ops:
  0.0 46.2 %copy-start = (bf16[2048,512]{1,0:T(8,128)(2,1)S(1)}, bf16[2048,512]{1,0:T(8,128)(2,1)}, u32[]{:S(2)}) copy-start(bf16[2048,512]{1,0:T(8,128)(2,1)} %param.12) | copy-start | bytes 6291460
  0.0 27.8 %copy-start.6 = (bf16[32,16,256]{2,1,0:T(8,128)(2,1)S(1)}, bf16[32,16,256]{2,1,0:T(8,128)(2,1)}, u32[]{:S(2)}) copy-start(bf16[32,16,256]{2,1,0:T(8,128)(2,1)} %param.15) | copy-start | bytes 786436
  0.0 29.4 %copy-start.4 = (bf16[32,32,256]{2,1,0:T(8,128)(2,1)S(1)}, bf16[32,32,256]{2,1,0:T(8,128)(2,1)}, u32[]{:S(2)}) copy-start(bf16[32,32,256]{2,1,0:T(8,128)(2,1)} %param.14) | copy-start | bytes 1572868
  1.5 21.2 %all-to-all-start = ((s32[128,1,16]{2,1,0:T(1,128)}), s32[128,1,16]{2,1,0:T(1,128)S(1)}, u32[]{:S(2)}, u32[]{:S(2)}) async-start(s32[128,1,16]{2,1,0:T(1,128)} %broadcast_in_dim.85), calls=%async_computation | async-start | bytes 131072 | tf_op jit(solution)/shard_map/all_to_all | solution.py:132
  31.4 1.9 %copy-start.5 = (bf16[128,16,256]{2,1,0:T(8,128)(2,1)S(1)}, bf16[128,16,256]{2,1,0:T(8,128)(2,1)}, u32[]{:S(2)}) copy-start(bf16[128,16,256]{2,1,0:T(8,128)(2,1)} %gather_fusion.1) | copy-start | bytes 3145732
  35.4 51.2 %all-to-all-start.1 = ((bf16[128,16,832]{2,1,0:T(8,128)(2,1)}), bf16[128,16,832]{2,1,0:T(8,128)(2,1)}, u32[]{:S(2)}, u32[]{:S(2)}) async-start(bf16[128,16,832]{2,1,0:T(8,128)(2,1)} %pad_maximum_fusion), calls=%async_computation.1 | async-start | bytes 7340032 | tf_op jit(solution)/shard_map/all_to_all | solution.py:143
  44.6 1.6 %copy-start.7 = (bf16[512,2048]{1,0:T(8,128)(2,1)S(1)}, bf16[512,2048]{1,0:T(8,128)(2,1)}, u32[]{:S(2)}) copy-start(bf16[512,2048]{1,0:T(8,128)(2,1)} %param.10) | copy-start | bytes 6291460
  46.1 2.3 %copy-start.8 = (bf16[2048,512]{1,0:T(8,128)(2,1)S(1)}, bf16[2048,512]{1,0:T(8,128)(2,1)}, u32[]{:S(2)}) copy-start(bf16[2048,512]{1,0:T(8,128)(2,1)} %param.13) | copy-start | bytes 6291460
  46.1 4.6 %slice-start = ((s8[8388608]{0:T(1024)(128)(4,1)}), s8[4194304]{0:T(1024)(128)(4,1)S(1)}, s32[]{:S(2)}) async-start(s8[8388608]{0:T(1024)(128)(4,1)} %bitcast.90), calls=%async_computation.2 | async-start | bytes 8388608
  46.2 4.5 %slice-start.1 = ((s8[8388608]{0:T(1024)(128)(4,1)}), s8[4194304]{0:T(1024)(128)(4,1)S(1)}, s32[]{:S(2)}) async-start(s8[8388608]{0:T(1024)(128)(4,1)} %bitcast.90), calls=%async_computation.3 | async-start | bytes 8388608
  100.7 1.6 %copy-start.1 = (bf16[512,2048]{1,0:T(8,128)(2,1)S(1)}, bf16[512,2048]{1,0:T(8,128)(2,1)}, u32[]{:S(2)}) copy-start(bf16[512,2048]{1,0:T(8,128)(2,1)} %copy.46.dq_ref) | copy-start | bytes 6291460
  102.3 1.2 copy-start.2
  103.5 1.2 copy-start.3

commit v6 on v5

--- a/solution.py
+++ b/solution.py
@@ -140,13 +140,7 @@
     send = jnp.concatenate(
         [picked[0][:, :ADAPTER_RANK], picked[0][:, ADAPTER_RANK:], picked[1], picked[2]], axis=2
     )
-    got = lax.all_to_all(send, axes, 0, 0, tiled=True).reshape(
-        serve_count, store_count, ADAPTER_RANK, send.shape[2]
-    )
-    down_q = got[..., :cols]
-    down_v = got[..., cols : 2 * cols]
-    upq = got[..., 2 * cols : 3 * cols]
-    upv = got[..., 3 * cols : 3 * cols + vcols]
+    got = lax.all_to_all(send, axes, 0, 0, tiled=True)
 
     lengths = request_token_length[0]
     adapters = adapter_per_request[0]
@@ -159,22 +153,6 @@
     owners = table_lookup(adapter_panel_slot, adapters) // ADP_DEV
     owner_token = jnp.sum(jnp.where(member, owners[None, :], 0), axis=1)
 
-    states3 = normalized_hidden_states.reshape(tok_rows, serve_count, cols)
-    owner_mask = owner_token[:, None, None] == jnp.arange(store_count, dtype=jnp.int32)[None, :, None]
-
-    def low_part(down_half):
-        low = jnp.einsum(
-            "tsf,sorf->tor", states3, down_half, preferred_element_type=jnp.float32
-        ).astype(jnp.bfloat16)
-        return jnp.where(owner_mask, low, jnp.zeros((), jnp.bfloat16))
-
-    delta_query = jnp.einsum(
-        "tor,sorf->tsf", low_part(down_q), upq, preferred_element_type=jnp.float32
-    ).astype(jnp.bfloat16).reshape(tok_rows, serve_count * cols)
-    delta_value = jnp.einsum(
-        "tor,sorf->tsf", low_part(down_v), upv, preferred_element_type=jnp.float32
-    ).astype(jnp.bfloat16).reshape(tok_rows, serve_count * vcols)
-
     q_base = jnp.dot(
         normalized_hidden_states, query_weight_matrix, preferred_element_type=jnp.float32
     )
@@ -184,18 +162,51 @@
     v_base = jnp.dot(
         normalized_hidden_states, value_weight_matrix, preferred_element_type=jnp.float32
     )
-    return fused_attention(q_base, delta_query, k_base, v_base, delta_value, positions)
+    return fused_attention(
+        q_base, k_base, v_base, normalized_hidden_states,
+        got.reshape(-1, got.shape[-1]), owner_token, positions,
+    )
 
 
 def _swap_halves(x):
     return jnp.concatenate([x[:, 32:64], x[:, 0:32], x[:, 96:128], x[:, 64:96]], axis=1)
 
 
-def _attend_kernel(qb_ref, dq_ref, kb_ref, vb_ref, dv_ref, cos_ref, sin_ref, pos_ref, out_ref,
-                   q_s, kd_s, vd_s):
+def _attend_kernel(qb_ref, kb_ref, vb_ref, x_ref, got_ref, own_ref, cos_ref, sin_ref, pos_ref,
+                   out_ref, q_s, kd_s, vd_s, dq_ref, dv_ref):
     rows = qb_ref.shape[0]
     blk = 128
     n_blk = rows // blk
+    cols = 256
+    slices = x_ref.shape[1] // cols
+    owner_lane = lax.broadcasted_iota(jnp.int32, (1, cols), 1) // 16
+
+    def low_rank_rows(r, carry):
+        r0 = pl.multiple_of(r * blk, blk)
+        low_q = jnp.zeros((blk, cols), jnp.float32)
+        low_v = jnp.zeros((blk, cols), jnp.float32)
+        for sl in range(slices):
+            xs = x_ref[pl.ds(r0, blk), sl * cols:(sl + 1) * cols]
+            panel = got_ref[sl * cols:(sl + 1) * cols, 0:2 * cols]
+            nt = (((1,), (1,)), ((), ()))
+            low_q += lax.dot_general(xs, panel[:, 0:cols], nt, preferred_element_type=jnp.float32)
+            low_v += lax.dot_general(xs, panel[:, cols:2 * cols], nt, preferred_element_type=jnp.float32)
+        mine = owner_lane == own_ref[pl.ds(r0, blk), :]
+        low_q = jnp.where(mine, low_q.astype(jnp.bfloat16), jnp.zeros((), jnp.bfloat16))
+        low_v = jnp.where(mine, low_v.astype(jnp.bfloat16), jnp.zeros((), jnp.bfloat16))
+        pieces = []
+        for sl in range(slices):
+            upq = got_ref[sl * cols:(sl + 1) * cols, 2 * cols:3 * cols]
+            dq_ref[pl.ds(r0, blk), sl * cols:(sl + 1) * cols] = jnp.dot(
+                low_q, upq, preferred_element_type=jnp.float32).astype(jnp.bfloat16)
+            upv = got_ref[sl * cols:(sl + 1) * cols, 3 * cols:3 * cols + 64]
+            pieces.append(jnp.dot(low_v, upv, preferred_element_type=jnp.float32))
+        for c in range(slices // 2):
+            dv_ref[pl.ds(r0, blk), c * 128:(c + 1) * 128] = jnp.concatenate(
+                [pieces[2 * c], pieces[2 * c + 1]], axis=1).astype(jnp.bfloat16)
+        return carry
+
+    lax.fori_loop(0, n_blk, low_rank_rows, 0)
     q_chunks = qb_ref.shape[1] // 128
     k_chunks = kb_ref.shape[1] // 128
     lane = lax.broadcasted_iota(jnp.int32, (1, 128), 1)
@@ -282,26 +293,29 @@
     return cos_t, sin_t
 
 
-def fused_attention(q_base, delta_q, k_base, v_base, delta_v, positions):
+def fused_attention(q_base, k_base, v_base, states, got, owner_token, positions):
     rows = q_base.shape[0]
     cos_t, sin_t = rope_tables(positions)
     pos_col = positions.astype(jnp.int32).reshape(rows, 1)
+    own_col = owner_token.astype(jnp.int32).reshape(rows, 1)
     vmem = pl.BlockSpec(memory_space=pltpu.VMEM)
-    flops = 2 * rows * 256 * 64 * 2 * HEADS * 2
+    flops = 2 * rows * 256 * 64 * 2 * HEADS * 2 + 2 * rows * 256 * (2 * 2048 + 2048 + 512)
     return pl.pallas_call(
         _attend_kernel,
         out_shape=jax.ShapeDtypeStruct((rows, HEADS * HEAD_DIM), jnp.bfloat16),
-        in_specs=[vmem] * 8,
+        in_specs=[vmem] * 9,
         out_specs=vmem,
         scratch_shapes=[
             pltpu.VMEM((rows, HEADS * HEAD_DIM), jnp.bfloat16),
             pltpu.VMEM((KV_HEADS, rows, 128), jnp.bfloat16),
             pltpu.VMEM((KV_HEADS, rows, 256), jnp.bfloat16),
+            pltpu.VMEM((rows, HEADS * HEAD_DIM), jnp.bfloat16),
+            pltpu.VMEM((rows, KV_HEADS * HEAD_DIM), jnp.bfloat16),
         ],
         compiler_params=pltpu.CompilerParams(vmem_limit_bytes=48 * 1024 * 1024),
         cost_estimate=pl.CostEstimate(flops=flops, transcendentals=rows * 256 * HEADS,
-                                      bytes_accessed=rows * (2048 * 6 + 512 * 12 + 256 * 4)),
-    )(q_base, delta_q, k_base, v_base, delta_v, cos_t, sin_t, pos_col)
+                                      bytes_accessed=rows * (2048 * 8 + 512 * 8 + 256 * 4) + got.size * 2),
+    )(q_base, k_base, v_base, states, got, own_col, cos_t, sin_t, pos_col)
 
 
 def solution(mesh):

time: 131 us -> 125 us (0.954)
  matrix products: 19.5 us -> 11.2 us
  local copies, waits for them, and re-layouts: 22.3 us -> 16.3 us
  Pallas kernels: 25.4 us -> 31.3 us
  waiting for transfers between devices: 37.1 us -> 39.1 us
    dot_general x2 -> x0, matrix products: 8.98 us -> none  [the longest x1 5.09 us: local(): jnp.einsum('tor,sorf->tsf', low_part(down_q), upq, preferred_element_type...]
    pallas_call x1, Pallas kernels: 25.4 us -> 31.3 us  [fused_attention(): pl.pallas_call(_attend_kernel, out_shape=jax.ShapeDtypeStruct((rows, HEAD...]
    reshape x3 -> x2, local copies, waits for them, and re-layouts: 5.89 us -> 0.95 us  [the longest x1 0.86 us: fused_attention(): own_col = owner_token.astype(jnp.int32).reshape(rows, 1)]
    unnamed x23 -> x26, local copies, waits for them, and re-layouts: 7.76 us -> 5.77 us
    all_to_all x1, waiting for transfers between devices: 7.32 us -> 8.86 us  [local(): lax.all_to_all(jnp.broadcast_to(adapter_per_request, (device_total, reque...]
  transfers between devices with their start and end apart: 2 -> 2, of which waited for: 2 -> 2; matrix products, arithmetic and copies ran while one was open for 14% -> 13% of each run, Pallas kernels for 0% -> 0%
where the time goes in v6:
time: 125 us
  waiting for transfers between devices  39.1 us (31%)
  Pallas kernels  31.3 us (25%)
  starting transfers between devices  16.9 us (14%)
  local copies, waits for them, and re-layouts  16.3 us (13%)
  matrix products  11.2 us (9%)
  other arithmetic  9.64 us (8%)
    pallas_call x1, Pallas kernels, fused_attention(): pl.pallas_call(_attend_kernel, out_shape=jax.ShapeDtypeStruct((rows, HEAD...  31.3 us
    all_to_all x1, waiting for transfers between devices, local(): got = lax.all_to_all(send, axes, 0, 0, tiled=True)  30.3 us
    all_to_all x1, starting transfers between devices, local(): lax.all_to_all(jnp.broadcast_to(adapter_per_request, (device_total, reque...  11.5 us
    all_to_all x1, waiting for transfers between devices, local(): lax.all_to_all(jnp.broadcast_to(adapter_per_request, (device_total, reque...  8.86 us
    gather x3, local copies, waits for them, and re-layouts, local(): jnp.take(panel, local_pick, axis=0, mode='clip')  6.19 us
    dot_general x1, matrix products, local(): jnp.dot(normalized_hidden_states, query_weight_matrix, preferred_element_...  6.02 us
    unnamed x26, local copies, waits for them, and re-layouts  5.77 us
    all_to_all x1, starting transfers between devices, local(): got = lax.all_to_all(send, axes, 0, 0, tiled=True)  5.39 us
  transfers between devices with their start and end apart: 2, of which 2 were waited for; matrix products, arithmetic and copies ran while one was open for 13% of the time, Pallas kernels for 0%

profile of v6, /device:TPU:1, one launch (start us, length us, event | category | flops | bytes accessed | tf_op | source)
XLA Modules:
  0.0 124.6 jit_solution(8442883845134912281)
XLA Ops:
  0.0 0.0 copy-start
  0.0 0.0 copy-start.7
  0.0 1.5 %broadcast_in_dim.62 = s32[128,1,16]{2,1,0:T(1,128)} broadcast(s32[16]{0:T(128)} %bitcast.21), dimensions={2} | broadcast | bytes 8256 | tf_op jit(solution)/shard_map/broadcast_in_dim | solution.py:133
  1.5 11.5 %all-to-all-start = ((s32[128,1,16]{2,1,0:T(1,128)}), s32[128,1,16]{2,1,0:T(1,128)S(1)}, u32[]{:S(2)}, u32[]{:S(2)}) async-start(s32[128,1,16]{2,1,0:T(1,128)} %broadcast_in_dim.62), calls=%async_computation | async-start | bytes 131072 | tf_op jit(solution)/shard_map/all_to_all | solution.py:132
  13.0 0.9 select_reduce_fusion.3
  13.8 8.9 %all-to-all-done = s32[128,1,16]{2,1,0:T(1,128)S(1)} async-done(((s32[128,1,16]{2,1,0:T(1,128)}), s32[128,1,16]{2,1,0:T(1,128)S(1)}, u32[]{:S(2)}, u32[]{:S(2)}) %all-to-all-start) | async-done | bytes 8224 | tf_op jit(solution)/shard_map/all_to_all | solution.py:132
  22.7 3.3 %select_reduce_fusion = s32[128,16]{1,0:T(8,128)S(1)} fusion(s32[512]{0:T(512)} %param.17, s32[128,16]{1,0:T(8,128)S(1)} %bitcast.18), kind=kLoop, calls=%fused_computation.3 | loop fusion | flops 3143680 | bytes 18432 | tf_op jit(solution)/shard_map/reduce_sum | solution.py:35
  26.0 0.1 fusion.3
  26.2 1.6 %gather_fusion.2 = bf16[128,16,64]{2,1,0:T(8,128)(2,1)S(1)} fusion(bf16[32,16,64]{2,1,0:T(8,128)(2,1)} %param.16, s32[1024]{0:T(1024)S(1)} %pad_clamp_fusion), kind=kCustom, calls=%fused_computation.2 | custom fusion | bytes 524800 | tf_op jit(solution)/shard_map/jit(_take)/gather | solution.py:138
  27.8 2.6 %gather_fusion.1 = bf16[128,16,256]{2,1,0:T(8,128)(2,1)} fusion(bf16[32,16,256]{2,1,0:T(8,128)(2,1)} %param.15, s32[1024]{0:T(1024)S(1)} %pad_clamp_fusion), kind=kCustom, calls=%fused_computation.1 | custom fusion | bytes 2097664 | tf_op jit(solution)/shard_map/jit(_take)/gather | solution.py:138
  30.4 0.0 copy-done.7
  30.4 2.0 %gather_fusion = bf16[128,32,256]{2,1,0:T(8,128)(2,1)} fusion(bf16[32,32,256]{2,1,0:T(8,128)(2,1)S(1)} %copy-done.7, s32[1024]{0:T(1024)S(1)} %pad_clamp_fusion), kind=kCustom, calls=%fused_computation | custom fusion | bytes 4194816 | tf_op jit(solution)/shard_map/jit(_take)/gather | solution.py:138
  32.4 0.0 copy-start.8
  32.4 1.8 %fusion.7 = (bf16[128,16,256]{2,1,0:T(8,128)(2,1)S(1)}, bf16[128,16,256]{2,1,0:T(8,128)(2,1)S(1)}) fusion(bf16[128,32,256]{2,1,0:T(8,128)(2,1)} %gather_fusion), kind=kLoop, calls=%fused_computation.39 | loop fusion | bytes 4194304 | tf_op jit(solution)/shard_map/slice | solution.py:141
  34.2 0.1 copy-done.8
  34.2 2.1 %pad_maximum_fusion = bf16[128,16,832]{2,1,0:T(8,128)(2,1)} fusion(bf16[128,16,64]{2,1,0:T(8,128)(2,1)S(1)} %gather_fusion.2, bf16[128,16,256]{2,1,0:T(8,128)(2,1)S(1)} %copy-done.8, bf16[128,16,256]{2,1,0:T(8,128)(2,1)S(1)} %get-tuple-element.8, bf16[128,16,256]{2,1,0:T(8,128)(2,1)S(1)} %get-tuple-element.7), kind=kLoop, calls=%fused_computation.5 | loop fusion | flops 13631488 | bytes 6815744 | tf_op jit(solution)/shard_map/concatenate | solution.py:140
  36.3 0.0 copy-start.9
  36.3 5.4 %all-to-all-start.1 = ((bf16[128,16,832]{2,1,0:T(8,128)(2,1)}), bf16[128,16,832]{2,1,0:T(8,128)(2,1)}, u32[]{:S(2)}, u32[]{:S(2)}) async-start(bf16[128,16,832]{2,1,0:T(8,128)(2,1)} %pad_maximum_fusion), calls=%async_computation.1 | async-start | bytes 7340032 | tf_op jit(solution)/shard_map/all_to_all | solution.py:143
  41.7 0.0 copy-done.9
  41.7 0.1 copy.24
  41.9 0.1 reduce
  42.0 0.1 convert_reduce_fusion
  42.1 0.1 select_reduce_fusion.1
  42.2 0.9 copy.27.own_ref
  43.0 0.1 copy.26
  43.2 0.0 slice-start
  43.2 1.0 fusion
  44.2 1.2 pad_maximum_fusion.1
  45.4 0.0 copy-start.10
  45.4 0.7 iota_subtract_fusion.pos_ref
  46.1 0.0 copy-done
  46.1 0.0 copy-start.1
  46.1 0.0 slice-start.1
  46.1 3.0 %fusion.9.kb_ref = f32[512,512]{1,0:T(8,128)S(1)} fusion(bf16[512,2048]{1,0:T(8,128)(2,1)} %x_ref.1, bf16[2048,512]{1,0:T(8,128)(2,1)S(1)} %copy-done), kind=kOutput, calls=%fused_computation.41 | convolution fusion | flops 1073741824 | bytes 5242880 | tf_op jit(solution)/shard_map/dot_general | solution.py:159
  49.1 0.0 copy-done.10
  49.1 0.0 copy-done.1
  49.1 2.2 %fusion.10.vb_ref = f32[512,512]{1,0:T(8,128)} fusion(bf16[512,2048]{1,0:T(8,128)(2,1)S(1)} %copy-done.1, bf16[2048,512]{1,0:T(8,128)(2,1)S(1)} %copy-done.10), kind=kOutput, calls=%fused_computation.42 | convolution fusion | flops 1073741824 | bytes 5242880 | tf_op jit(solution)/shard_map/dot_general | solution.py:162
  51.4 0.0 slice-done
  51.4 0.0 slice-done.1
  51.4 6.0 %fusion.8.qb_ref = f32[512,2048]{1,0:T(8,128)} fusion(bf16[512,2048]{1,0:T(8,128)(2,1)S(1)} %copy-done.1, bf16[2048,2048]{1,0:T(8,128)(2,1)S(1)} %bitcast.25), kind=kOutput, calls=%fused_computation.40 | convolution fusion | flops 4294967296 | bytes 14680064 | tf_op jit(solution)/shard_map/dot_general | solution.py:156
  57.4 30.3 %all-to-all-done.1 = bf16[128,16,832]{2,1,0:T(8,128)(2,1)} async-done(((bf16[128,16,832]{2,1,0:T(8,128)(2,1)}), bf16[128,16,832]{2,1,0:T(8,128)(2,1)}, u32[]{:S(2)}, u32[]{:S(2)}) %all-to-all-start.1) | async-done | bytes 3407904 | tf_op jit(solution)/shard_map/all_to_all | solution.py:143
  87.6 0.0 copy-start.2
  87.6 1.6 %copy-done.2 = bf16[512,2048]{1,0:T(8,128)(2,1)S(1)} copy-done((bf16[512,2048]{1,0:T(8,128)(2,1)S(1)}, bf16[512,2048]{1,0:T(8,128)(2,1)}, u32[]{:S(2)}) %copy-start.2) | copy-done | bytes 2097176
  89.2 0.0 copy-start.3
  89.2 1.2 copy-done.3
  90.5 0.0 copy-start.4
  90.5 0.9 copy-done.4
  91.4 0.0 copy-start.5
  91.4 0.9 copy-done.5
  92.4 0.0 copy-start.6
  92.4 0.9 copy-done.6
  93.3 31.3 %shard_map.103 = bf16[512,2048]{1,0:T(8,128)(2,1)} custom-call(f32[512,2048]{1,0:T(8,128)} %fusion.8.qb_ref, f32[512,512]{1,0:T(8,128)S(1)} %fusion.9.kb_ref, f32[512,512]{1,0:T(8,128)S(1)} %copy-done.3, bf16[512,2048]{1,0:T(8,128)(2,1)S(1)} %copy-done.2, bf16[2048,832]{1,0:T(8,128)(2,1)} %bitcast.2.got_ref, s32[512,1]{1,0:T(8,128)S(1)} %copy-done.5, ...), custom_call_target="tpu_custom_call" | custom-call | flops 3892314112 | bytes 14417920 | tf_op jit(solution)/shard_map/pallas_call | solution.py:303
  (7 shorter events, 0.1 us)
Async XLA Ops:
  0.0 46.1 %copy-start = (bf16[2048,512]{1,0:T(8,128)(2,1)S(1)}, bf16[2048,512]{1,0:T(8,128)(2,1)}, u32[]{:S(2)}) copy-start(bf16[2048,512]{1,0:T(8,128)(2,1)} %param.12) | copy-start | bytes 6291460
  0.0 30.4 %copy-start.7 = (bf16[32,32,256]{2,1,0:T(8,128)(2,1)S(1)}, bf16[32,32,256]{2,1,0:T(8,128)(2,1)}, u32[]{:S(2)}) copy-start(bf16[32,32,256]{2,1,0:T(8,128)(2,1)} %param.14) | copy-start | bytes 1572868
  1.5 21.2 %all-to-all-start = ((s32[128,1,16]{2,1,0:T(1,128)}), s32[128,1,16]{2,1,0:T(1,128)S(1)}, u32[]{:S(2)}, u32[]{:S(2)}) async-start(s32[128,1,16]{2,1,0:T(1,128)} %broadcast_in_dim.62), calls=%async_computation | async-start | bytes 131072 | tf_op jit(solution)/shard_map/all_to_all | solution.py:132
  32.4 1.9 %copy-start.8 = (bf16[128,16,256]{2,1,0:T(8,128)(2,1)S(1)}, bf16[128,16,256]{2,1,0:T(8,128)(2,1)}, u32[]{:S(2)}) copy-start(bf16[128,16,256]{2,1,0:T(8,128)(2,1)} %gather_fusion.1) | copy-start | bytes 3145732
  36.3 5.4 %copy-start.9 = (s32[1,16]{1,0:T(1,128)S(1)}, s32[1,16]{1,0:T(1,128)}, u32[]{:S(2)}) copy-start(s32[1,16]{1,0:T(1,128)} %param.19) | copy-start | bytes 196
  36.3 51.3 %all-to-all-start.1 = ((bf16[128,16,832]{2,1,0:T(8,128)(2,1)}), bf16[128,16,832]{2,1,0:T(8,128)(2,1)}, u32[]{:S(2)}, u32[]{:S(2)}) async-start(bf16[128,16,832]{2,1,0:T(8,128)(2,1)} %pad_maximum_fusion), calls=%async_computation.1 | async-start | bytes 7340032 | tf_op jit(solution)/shard_map/all_to_all | solution.py:143
  43.2 8.1 %slice-start = ((s8[8388608]{0:T(1024)(128)(4,1)}), s8[4194304]{0:T(1024)(128)(4,1)S(1)}, s32[]{:S(2)}) async-start(s8[8388608]{0:T(1024)(128)(4,1)} %bitcast.24), calls=%async_computation.2 | async-start | bytes 8388608
  45.4 3.7 %copy-start.10 = (bf16[2048,512]{1,0:T(8,128)(2,1)S(1)}, bf16[2048,512]{1,0:T(8,128)(2,1)}, u32[]{:S(2)}) copy-start(bf16[2048,512]{1,0:T(8,128)(2,1)} %param.13) | copy-start | bytes 6291460
  46.1 3.0 %copy-start.1 = (bf16[512,2048]{1,0:T(8,128)(2,1)S(1)}, bf16[512,2048]{1,0:T(8,128)(2,1)}, u32[]{:S(2)}) copy-start(bf16[512,2048]{1,0:T(8,128)(2,1)} %x_ref.1) | copy-start | bytes 6291460
  46.1 5.2 %slice-start.1 = ((s8[8388608]{0:T(1024)(128)(4,1)}), s8[4194304]{0:T(1024)(128)(4,1)S(1)}, s32[]{:S(2)}) async-start(s8[8388608]{0:T(1024)(128)(4,1)} %bitcast.24), calls=%async_computation.3 | async-start | bytes 8388608
  87.6 1.6 %copy-start.2 = (bf16[512,2048]{1,0:T(8,128)(2,1)S(1)}, bf16[512,2048]{1,0:T(8,128)(2,1)}, u32[]{:S(2)}) copy-start(bf16[512,2048]{1,0:T(8,128)(2,1)} %x_ref.1) | copy-start | bytes 6291460
  89.2 1.2 copy-start.3
  90.5 0.9 copy-start.4
  91.4 0.9 copy-start.5
  92.4 0.9 copy-start.6

commit v7 on v6

--- a/solution.py
+++ b/solution.py
@@ -129,17 +129,22 @@
     adp_dev, rank2, cols = adapter_down_weight.shape
     vcols = adapter_up_value_weight.shape[2]
     device_total = serve_count * store_count
+    panel_table = jnp.concatenate(
+        [
+            adapter_down_weight[:, :ADAPTER_RANK],
+            adapter_down_weight[:, ADAPTER_RANK:],
+            adapter_up_query_weight,
+            adapter_up_value_weight,
+        ],
+        axis=2,
+    )
     all_lists = lax.all_to_all(
         jnp.broadcast_to(adapter_per_request, (device_total, request_count)), axes, 0, 0, tiled=True
     )
-    all_slots = table_lookup(adapter_panel_slot, all_lists)
+    all_slots = jnp.take(adapter_panel_slot, all_lists.reshape(-1), mode="clip").reshape(all_lists.shape)
     mine = all_slots // ADP_DEV == my_store
     local_pick = jnp.sum(jnp.where(mine, all_slots % ADP_DEV, 0), axis=1)
-    picked = [jnp.take(panel, local_pick, axis=0, mode="clip")
-              for panel in (adapter_down_weight, adapter_up_query_weight, adapter_up_value_weight)]
-    send = jnp.concatenate(
-        [picked[0][:, :ADAPTER_RANK], picked[0][:, ADAPTER_RANK:], picked[1], picked[2]], axis=2
-    )
+    send = jnp.take(panel_table, local_pick, axis=0, mode="clip")
     got = lax.all_to_all(send, axes, 0, 0, tiled=True)
 
     lengths = request_token_length[0]

time: 125 us -> 129 us (1.032)
  local copies, waits for them, and re-layouts: 16.3 us -> 26.1 us
  other arithmetic: 9.64 us -> 5.49 us
  matrix products: 11.2 us -> 9.5 us
    gather x3 -> x2, local copies, waits for them, and re-layouts: 6.19 us -> 16.1 us  [the longest x1 13.2 us: local(): jnp.take(adapter_panel_slot, all_lists.reshape(-1), mode='clip')]
    reduce_sum x2 -> x1, other arithmetic: 4.18 us -> 0.18 us  [table_lookup(): return jnp.sum(jnp.where(wanted[..., None] == entries, table, 0), axis=-1)]
    dot_general x1, matrix products: 2.98 us -> 1.25 us  [local(): jnp.dot(normalized_hidden_states, key_weight_matrix, preferred_element_ty...]
    all_to_all x1, waiting for transfers between devices: 30.3 us -> 31.9 us  [local(): got = lax.all_to_all(send, axes, 0, 0, tiled=True)]
    all_to_all x1, waiting for transfers between devices: 8.86 us -> 7.35 us  [local(): lax.all_to_all(jnp.broadcast_to(adapter_per_request, (device_total, reque...]
where the time goes in v7:
time: 129 us
  waiting for transfers between devices  39.3 us (30%)
  Pallas kernels  31.3 us (24%)
  local copies, waits for them, and re-layouts  26.1 us (20%)
  starting transfers between devices  16.9 us (13%)
  matrix products  9.5 us (7%)
  other arithmetic  5.49 us (4%)
    all_to_all x1, waiting for transfers between devices, local(): got = lax.all_to_all(send, axes, 0, 0, tiled=True)  31.9 us
    pallas_call x1, Pallas kernels, fused_attention(): pl.pallas_call(_attend_kernel, out_shape=jax.ShapeDtypeStruct((rows, HEAD...  31.3 us
    gather x1, local copies, waits for them, and re-layouts, local(): jnp.take(adapter_panel_slot, all_lists.reshape(-1), mode='clip')  13.2 us
    all_to_all x1, starting transfers between devices, local(): lax.all_to_all(jnp.broadcast_to(adapter_per_request, (device_total, reque...  11.5 us
    all_to_all x1, waiting for transfers between devices, local(): lax.all_to_all(jnp.broadcast_to(adapter_per_request, (device_total, reque...  7.35 us
    dot_general x1, matrix products, local(): jnp.dot(normalized_hidden_states, query_weight_matrix, preferred_element_...  6.02 us
    unnamed x26, local copies, waits for them, and re-layouts  5.76 us
    all_to_all x1, starting transfers between devices, local(): got = lax.all_to_all(send, axes, 0, 0, tiled=True)  5.39 us
  transfers between devices with their start and end apart: 2, of which 2 were waited for; matrix products, arithmetic and copies ran while one was open for 13% of the time, Pallas kernels for 0%

profile of v7, /device:TPU:1, one launch (start us, length us, event | category | flops | bytes accessed | tf_op | source)
XLA Modules:
  0.0 128.8 jit_solution(12186151602444723530)
XLA Ops:
  0.0 0.0 copy-start
  0.0 0.0 copy-start.8
  0.0 0.0 copy-start.7
  0.0 1.5 %broadcast_in_dim.52 = s32[128,1,16]{2,1,0:T(1,128)} broadcast(s32[16]{0:T(128)} %bitcast.19), dimensions={2} | broadcast | bytes 8256 | tf_op jit(solution)/shard_map/broadcast_in_dim | solution.py:142
  1.5 11.5 %all-to-all-start = ((s32[128,1,16]{2,1,0:T(1,128)}), s32[128,1,16]{2,1,0:T(1,128)S(1)}, u32[]{:S(2)}, u32[]{:S(2)}) async-start(s32[128,1,16]{2,1,0:T(1,128)} %broadcast_in_dim.52), calls=%async_computation | async-start | bytes 131072 | tf_op jit(solution)/shard_map/all_to_all | solution.py:141
  13.0 1.1 fusion.7
  14.1 1.1 pad_maximum_fusion
  15.2 0.0 copy-done.8
  15.2 0.0 copy-done.7
  15.2 0.2 select_reduce_fusion.2
  15.4 7.3 %all-to-all-done = s32[128,1,16]{2,1,0:T(1,128)S(1)} async-done(((s32[128,1,16]{2,1,0:T(1,128)}), s32[128,1,16]{2,1,0:T(1,128)S(1)}, u32[]{:S(2)}, u32[]{:S(2)}) %all-to-all-start) | async-done | bytes 8224 | tf_op jit(solution)/shard_map/all_to_all | solution.py:141
  22.7 0.5 broadcast.80
  23.2 0.8 reduce.5
  24.0 0.1 reshape.78
  24.1 13.2 %gather_fusion = s32[2048]{0:T(1024)S(1)} fusion(s32[512]{0:T(512)S(1)} %copy-done.7, s32[2048]{0:T(1024)S(1)} %broadcast_clamp_fusion), kind=kCustom, calls=%fused_computation | custom fusion | bytes 24576 | tf_op jit(solution)/shard_map/jit(_take)/gather | solution.py:144
  37.3 0.1 reshape.71
  37.4 0.1 fusion.3
  37.6 2.9 %gather_fusion.1 = bf16[128,16,832]{2,1,0:T(8,128)(2,1)} fusion(bf16[32,16,832]{2,1,0:T(8,128)(2,1)S(1)} %pad_maximum_fusion, s32[1024]{0:T(1024)S(1)} %pad_clamp_fusion), kind=kCustom, calls=%fused_computation.1 | custom fusion | bytes 6816256 | tf_op jit(solution)/shard_map/jit(_take)/gather | solution.py:147
  40.5 0.0 copy-start.9
  40.5 5.4 %all-to-all-start.1 = ((bf16[128,16,832]{2,1,0:T(8,128)(2,1)}), bf16[128,16,832]{2,1,0:T(8,128)(2,1)}, u32[]{:S(2)}, u32[]{:S(2)}) async-start(bf16[128,16,832]{2,1,0:T(8,128)(2,1)} %gather_fusion.1), calls=%async_computation.1 | async-start | bytes 7340032 | tf_op jit(solution)/shard_map/all_to_all | solution.py:148
  45.9 0.0 copy-done.9
  45.9 0.1 copy.21
  46.0 0.1 reduce.1
  46.1 0.1 convert_reduce_fusion
  46.2 0.1 select_reduce_fusion
  46.3 0.9 copy.24.own_ref
  47.2 0.1 copy.23
  47.3 0.0 copy-start.1
  47.4 1.0 fusion
  48.4 1.2 pad_maximum_fusion.1
  49.5 0.0 copy-start.10
  49.5 0.0 slice-start
  49.5 0.7 iota_subtract_fusion.pos_ref
  50.2 0.0 copy-done
  50.2 0.0 copy-done.1
  50.2 0.0 slice-start.1
  50.2 1.2 fusion.9.kb_ref
  51.5 0.0 copy-done.10
  51.5 2.2 %fusion.10.vb_ref = f32[512,512]{1,0:T(8,128)} fusion(bf16[512,2048]{1,0:T(8,128)(2,1)S(1)} %copy-done.1, bf16[2048,512]{1,0:T(8,128)(2,1)S(1)} %copy-done.10), kind=kOutput, calls=%fused_computation.40 | convolution fusion | flops 1073741824 | bytes 5242880 | tf_op jit(solution)/shard_map/dot_general | solution.py:167
  53.7 0.0 slice-done
  53.7 0.1 slice-done.1
  53.8 6.0 %fusion.8.qb_ref = f32[512,2048]{1,0:T(8,128)} fusion(bf16[512,2048]{1,0:T(8,128)(2,1)S(1)} %copy-done.1, bf16[2048,2048]{1,0:T(8,128)(2,1)S(1)} %bitcast.23), kind=kOutput, calls=%fused_computation.38 | convolution fusion | flops 4294967296 | bytes 14680064 | tf_op jit(solution)/shard_map/dot_general | solution.py:161
  59.8 31.9 %all-to-all-done.1 = bf16[128,16,832]{2,1,0:T(8,128)(2,1)} async-done(((bf16[128,16,832]{2,1,0:T(8,128)(2,1)}), bf16[128,16,832]{2,1,0:T(8,128)(2,1)}, u32[]{:S(2)}, u32[]{:S(2)}) %all-to-all-start.1) | async-done | bytes 3407904 | tf_op jit(solution)/shard_map/all_to_all | solution.py:148
  91.8 0.0 copy-start.2
  91.8 1.6 %copy-done.2 = bf16[512,2048]{1,0:T(8,128)(2,1)S(1)} copy-done((bf16[512,2048]{1,0:T(8,128)(2,1)S(1)}, bf16[512,2048]{1,0:T(8,128)(2,1)}, u32[]{:S(2)}) %copy-start.2) | copy-done | bytes 2097176
  93.4 0.0 copy-start.3
  93.4 1.2 copy-done.3
  94.6 0.0 copy-start.4
  94.6 0.9 copy-done.4
  95.5 0.0 copy-start.5
  95.5 0.9 copy-done.5
  96.5 0.0 copy-start.6
  96.5 0.9 copy-done.6
  97.4 31.3 %shard_map.103 = bf16[512,2048]{1,0:T(8,128)(2,1)} custom-call(f32[512,2048]{1,0:T(8,128)} %fusion.8.qb_ref, f32[512,512]{1,0:T(8,128)S(1)} %fusion.9.kb_ref, f32[512,512]{1,0:T(8,128)S(1)} %copy-done.3, bf16[512,2048]{1,0:T(8,128)(2,1)S(1)} %copy-done.2, bf16[2048,832]{1,0:T(8,128)(2,1)} %bitcast.1.got_ref, s32[512,1]{1,0:T(8,128)S(1)} %copy-done.5, ...), custom_call_target="tpu_custom_call" | custom-call | flops 3892314112 | bytes 14417920 | tf_op jit(solution)/shard_map/pallas_call | solution.py:308
  (8 shorter events, 0.1 us)
Async XLA Ops:
  0.0 50.2 %copy-start = (bf16[2048,512]{1,0:T(8,128)(2,1)S(1)}, bf16[2048,512]{1,0:T(8,128)(2,1)}, u32[]{:S(2)}) copy-start(bf16[2048,512]{1,0:T(8,128)(2,1)} %param.12) | copy-start | bytes 6291460
  0.0 15.2 %copy-start.8 = (s32[1,16]{1,0:T(1,128)S(1)}, s32[1,16]{1,0:T(1,128)}, u32[]{:S(2)}) copy-start(s32[1,16]{1,0:T(1,128)} %param.18) | copy-start | bytes 196
  0.0 15.2 %copy-start.7 = (s32[512]{0:T(512)S(1)}, s32[512]{0:T(512)}, u32[]{:S(2)}) copy-start(s32[512]{0:T(512)} %param.17) | copy-start | bytes 6148
  1.5 21.2 %all-to-all-start = ((s32[128,1,16]{2,1,0:T(1,128)}), s32[128,1,16]{2,1,0:T(1,128)S(1)}, u32[]{:S(2)}, u32[]{:S(2)}) async-start(s32[128,1,16]{2,1,0:T(1,128)} %broadcast_in_dim.52), calls=%async_computation | async-start | bytes 131072 | tf_op jit(solution)/shard_map/all_to_all | solution.py:141
  40.5 5.4 %copy-start.9 = (s32[1,16]{1,0:T(1,128)S(1)}, s32[1,16]{1,0:T(1,128)}, u32[]{:S(2)}) copy-start(s32[1,16]{1,0:T(1,128)} %param.19) | copy-start | bytes 196
  40.5 51.3 %all-to-all-start.1 = ((bf16[128,16,832]{2,1,0:T(8,128)(2,1)}), bf16[128,16,832]{2,1,0:T(8,128)(2,1)}, u32[]{:S(2)}, u32[]{:S(2)}) async-start(bf16[128,16,832]{2,1,0:T(8,128)(2,1)} %gather_fusion.1), calls=%async_computation.1 | async-start | bytes 7340032 | tf_op jit(solution)/shard_map/all_to_all | solution.py:148
  47.3 2.9 %copy-start.1 = (bf16[512,2048]{1,0:T(8,128)(2,1)S(1)}, bf16[512,2048]{1,0:T(8,128)(2,1)}, u32[]{:S(2)}) copy-start(bf16[512,2048]{1,0:T(8,128)(2,1)} %x_ref.1) | copy-start | bytes 6291460
  49.5 2.0 %copy-start.10 = (bf16[2048,512]{1,0:T(8,128)(2,1)S(1)}, bf16[2048,512]{1,0:T(8,128)(2,1)}, u32[]{:S(2)}) copy-start(bf16[2048,512]{1,0:T(8,128)(2,1)} %param.13) | copy-start | bytes 6291460
  49.5 4.2 %slice-start = ((s8[8388608]{0:T(1024)(128)(4,1)}), s8[4194304]{0:T(1024)(128)(4,1)S(1)}, s32[]{:S(2)}) async-start(s8[8388608]{0:T(1024)(128)(4,1)} %bitcast.22), calls=%async_computation.2 | async-start | bytes 8388608
  50.2 3.6 %slice-start.1 = ((s8[8388608]{0:T(1024)(128)(4,1)}), s8[4194304]{0:T(1024)(128)(4,1)S(1)}, s32[]{:S(2)}) async-start(s8[8388608]{0:T(1024)(128)(4,1)} %bitcast.22), calls=%async_computation.3 | async-start | bytes 8388608
  91.8 1.6 %copy-start.2 = (bf16[512,2048]{1,0:T(8,128)(2,1)S(1)}, bf16[512,2048]{1,0:T(8,128)(2,1)}, u32[]{:S(2)}) copy-start(bf16[512,2048]{1,0:T(8,128)(2,1)} %x_ref.1) | copy-start | bytes 6291460
  93.4 1.2 copy-start.3
  94.6 0.9 copy-start.4
  95.5 0.9 copy-start.5
  96.5 0.9 copy-start.6

commit v8 on v7

--- a/solution.py
+++ b/solution.py
@@ -141,7 +141,7 @@
     all_lists = lax.all_to_all(
         jnp.broadcast_to(adapter_per_request, (device_total, request_count)), axes, 0, 0, tiled=True
     )
-    all_slots = jnp.take(adapter_panel_slot, all_lists.reshape(-1), mode="clip").reshape(all_lists.shape)
+    all_slots = table_lookup(adapter_panel_slot, all_lists)
     mine = all_slots // ADP_DEV == my_store
     local_pick = jnp.sum(jnp.where(mine, all_slots % ADP_DEV, 0), axis=1)
     send = jnp.take(panel_table, local_pick, axis=0, mode="clip")

time: 129 us -> 117 us (0.907)
  local copies, waits for them, and re-layouts: 26.1 us -> 12.3 us
  other arithmetic: 5.49 us -> 7.3 us
    gather x1 -> x0, local copies, waits for them, and re-layouts: 13.2 us -> none  [local(): jnp.take(adapter_panel_slot, all_lists.reshape(-1), mode='clip')]
    reduce_sum x1 -> x2, other arithmetic: 0.18 us -> 2.81 us  [table_lookup(): return jnp.sum(jnp.where(wanted[..., None] == entries, table, 0), axis=-1)]
  transfers between devices with their start and end apart: 2 -> 2, of which waited for: 2 -> 2; matrix products, arithmetic and copies ran while one was open for 13% -> 14% of each run, Pallas kernels for 0% -> 0%
where the time goes in v8:
time: 117 us
  waiting for transfers between devices  39.3 us (34%)
  Pallas kernels  31.3 us (27%)
  starting transfers between devices  16.9 us (14%)
  local copies, waits for them, and re-layouts  12.3 us (11%)
  matrix products  9.48 us (8%)
  other arithmetic  7.3 us (6%)
    all_to_all x1, waiting for transfers between devices, local(): got = lax.all_to_all(send, axes, 0, 0, tiled=True)  31.9 us
    pallas_call x1, Pallas kernels, fused_attention(): pl.pallas_call(_attend_kernel, out_shape=jax.ShapeDtypeStruct((rows, HEAD...  31.3 us
    all_to_all x1, starting transfers between devices, local(): lax.all_to_all(jnp.broadcast_to(adapter_per_request, (device_total, reque...  11.5 us
    all_to_all x1, waiting for transfers between devices, local(): lax.all_to_all(jnp.broadcast_to(adapter_per_request, (device_total, reque...  7.35 us
    dot_general x1, matrix products, local(): jnp.dot(normalized_hidden_states, query_weight_matrix, preferred_element_...  6.02 us
    unnamed x26, local copies, waits for them, and re-layouts  5.77 us
    all_to_all x1, starting transfers between devices, local(): got = lax.all_to_all(send, axes, 0, 0, tiled=True)  5.39 us
    gather x1, local copies, waits for them, and re-layouts, local(): send = jnp.take(panel_table, local_pick, axis=0, mode='clip')  2.88 us
  transfers between devices with their start and end apart: 2, of which 2 were waited for; matrix products, arithmetic and copies ran while one was open for 14% of the time, Pallas kernels for 0%

profile of v8, /device:TPU:1, one launch (start us, length us, event | category | flops | bytes accessed | tf_op | source)
XLA Modules:
  0.0 116.7 jit_solution(13461976791833509231)
XLA Ops:
  0.0 0.0 copy-start
  0.0 0.0 copy-start.8
  0.0 0.0 copy-start.7
  0.0 1.5 %broadcast_in_dim.58 = s32[128,1,16]{2,1,0:T(1,128)} broadcast(s32[16]{0:T(128)} %bitcast.21), dimensions={2} | broadcast | bytes 8256 | tf_op jit(solution)/shard_map/broadcast_in_dim | solution.py:142
  1.5 11.5 %all-to-all-start = ((s32[128,1,16]{2,1,0:T(1,128)}), s32[128,1,16]{2,1,0:T(1,128)S(1)}, u32[]{:S(2)}, u32[]{:S(2)}) async-start(s32[128,1,16]{2,1,0:T(1,128)} %broadcast_in_dim.58), calls=%async_computation | async-start | bytes 131072 | tf_op jit(solution)/shard_map/all_to_all | solution.py:141
  13.0 1.1 fusion.7
  14.1 1.1 pad_maximum_fusion
  15.2 0.0 copy-done.8
  15.2 0.0 copy-done.7
  15.2 0.2 select_reduce_fusion.3
  15.4 7.3 %all-to-all-done = s32[128,1,16]{2,1,0:T(1,128)S(1)} async-done(((s32[128,1,16]{2,1,0:T(1,128)}), s32[128,1,16]{2,1,0:T(1,128)S(1)}, u32[]{:S(2)}, u32[]{:S(2)}) %all-to-all-start) | async-done | bytes 8224 | tf_op jit(solution)/shard_map/all_to_all | solution.py:141
  22.7 2.6 %select_reduce_fusion = s32[128,16]{1,0:T(8,128)S(1)} fusion(s32[512]{0:T(512)S(1)} %copy-done.7, s32[128,16]{1,0:T(8,128)S(1)} %bitcast.18), kind=kLoop, calls=%fused_computation.1 | loop fusion | flops 3143680 | bytes 18432 | tf_op jit(solution)/shard_map/reduce_sum | solution.py:35
  25.3 0.1 fusion.3
  25.5 2.9 %gather_fusion = bf16[128,16,832]{2,1,0:T(8,128)(2,1)} fusion(bf16[32,16,832]{2,1,0:T(8,128)(2,1)S(1)} %pad_maximum_fusion, s32[1024]{0:T(1024)S(1)} %pad_clamp_fusion), kind=kCustom, calls=%fused_computation | custom fusion | bytes 6816256 | tf_op jit(solution)/shard_map/jit(_take)/gather | solution.py:147
  28.4 0.0 copy-start.9
  28.4 5.4 %all-to-all-start.1 = ((bf16[128,16,832]{2,1,0:T(8,128)(2,1)}), bf16[128,16,832]{2,1,0:T(8,128)(2,1)}, u32[]{:S(2)}, u32[]{:S(2)}) async-start(bf16[128,16,832]{2,1,0:T(8,128)(2,1)} %gather_fusion), calls=%async_computation.1 | async-start | bytes 7340032 | tf_op jit(solution)/shard_map/all_to_all | solution.py:148
  33.8 0.0 copy-done.9
  33.8 0.1 copy.24
  33.9 0.1 reduce
  34.0 0.1 convert_reduce_fusion
  34.1 0.1 select_reduce_fusion.1
  34.2 0.9 copy.27.own_ref
  35.1 0.1 copy.26
  35.2 0.0 copy-start.1
  35.3 1.0 fusion
  36.3 1.2 %pad_maximum_fusion.1 = (f32[512,128]{1,0:T(8,128)S(1)}, f32[512,128]{1,0:T(8,128)}) fusion(f32[512,32]{1,0:T(8,128)S(1)} %get-tuple-element.11, f32[512,32]{1,0:T(8,128)S(1)} %get-tuple-element.10, f32[512,32]{1,0:T(8,128)S(1)} %get-tuple-element.9), kind=kLoop, calls=%fused_computation.6 | loop fusion | flops 393216 | bytes 720896 | tf_op jit(solution)/shard_map/concatenate | solution.py:296
  37.4 0.0 copy-start.10
  37.4 0.0 slice-start
  37.5 0.7 iota_subtract_fusion.pos_ref
  38.2 0.0 copy-done
  38.2 0.0 copy-done.1
  38.2 0.0 slice-start.1
  38.2 1.2 %fusion.9.kb_ref = f32[512,512]{1,0:T(8,128)S(1)} fusion(bf16[512,2048]{1,0:T(8,128)(2,1)S(1)} %copy-done.1, bf16[2048,512]{1,0:T(8,128)(2,1)S(1)} %copy-done), kind=kOutput, calls=%fused_computation.39 | convolution fusion | flops 1073741824 | bytes 5242880 | tf_op jit(solution)/shard_map/dot_general | solution.py:164
  39.4 0.0 copy-done.10
  39.4 2.2 %fusion.10.vb_ref = f32[512,512]{1,0:T(8,128)} fusion(bf16[512,2048]{1,0:T(8,128)(2,1)S(1)} %copy-done.1, bf16[2048,512]{1,0:T(8,128)(2,1)S(1)} %copy-done.10), kind=kOutput, calls=%fused_computation.40 | convolution fusion | flops 1073741824 | bytes 5242880 | tf_op jit(solution)/shard_map/dot_general | solution.py:167
  41.6 0.0 slice-done
  41.6 0.1 slice-done.1
  41.7 6.0 %fusion.8.qb_ref = f32[512,2048]{1,0:T(8,128)} fusion(bf16[512,2048]{1,0:T(8,128)(2,1)S(1)} %copy-done.1, bf16[2048,2048]{1,0:T(8,128)(2,1)S(1)} %bitcast.25), kind=kOutput, calls=%fused_computation.38 | convolution fusion | flops 4294967296 | bytes 14680064 | tf_op jit(solution)/shard_map/dot_general | solution.py:161
  47.8 31.9 %all-to-all-done.1 = bf16[128,16,832]{2,1,0:T(8,128)(2,1)} async-done(((bf16[128,16,832]{2,1,0:T(8,128)(2,1)}), bf16[128,16,832]{2,1,0:T(8,128)(2,1)}, u32[]{:S(2)}, u32[]{:S(2)}) %all-to-all-start.1) | async-done | bytes 3407904 | tf_op jit(solution)/shard_map/all_to_all | solution.py:148
  79.7 0.0 copy-start.2
  79.7 1.6 %copy-done.2 = bf16[512,2048]{1,0:T(8,128)(2,1)S(1)} copy-done((bf16[512,2048]{1,0:T(8,128)(2,1)S(1)}, bf16[512,2048]{1,0:T(8,128)(2,1)}, u32[]{:S(2)}) %copy-start.2) | copy-done | bytes 2097176
  81.3 0.0 copy-start.3
  81.3 1.2 %copy-done.3 = f32[512,512]{1,0:T(8,128)S(1)} copy-done((f32[512,512]{1,0:T(8,128)S(1)}, f32[512,512]{1,0:T(8,128)}, u32[]{:S(2)}) %copy-start.3) | copy-done | bytes 1048600
  82.5 0.0 copy-start.4
  82.5 0.9 copy-done.4
  83.5 0.0 copy-start.5
  83.5 0.9 copy-done.5
  84.4 0.0 copy-start.6
  84.4 0.9 copy-done.6
  85.4 31.3 %shard_map.103 = bf16[512,2048]{1,0:T(8,128)(2,1)} custom-call(f32[512,2048]{1,0:T(8,128)} %fusion.8.qb_ref, f32[512,512]{1,0:T(8,128)S(1)} %fusion.9.kb_ref, f32[512,512]{1,0:T(8,128)S(1)} %copy-done.3, bf16[512,2048]{1,0:T(8,128)(2,1)S(1)} %copy-done.2, bf16[2048,832]{1,0:T(8,128)(2,1)} %bitcast.2.got_ref, s32[512,1]{1,0:T(8,128)S(1)} %copy-done.5, ...), custom_call_target="tpu_custom_call" | custom-call | flops 3892314112 | bytes 14417920 | tf_op jit(solution)/shard_map/pallas_call | solution.py:308
  (7 shorter events, 0.1 us)
Async XLA Ops:
  0.0 38.2 %copy-start = (bf16[2048,512]{1,0:T(8,128)(2,1)S(1)}, bf16[2048,512]{1,0:T(8,128)(2,1)}, u32[]{:S(2)}) copy-start(bf16[2048,512]{1,0:T(8,128)(2,1)} %param.12) | copy-start | bytes 6291460
  0.0 15.2 %copy-start.8 = (s32[1,16]{1,0:T(1,128)S(1)}, s32[1,16]{1,0:T(1,128)}, u32[]{:S(2)}) copy-start(s32[1,16]{1,0:T(1,128)} %param.18) | copy-start | bytes 196
  0.0 15.2 %copy-start.7 = (s32[512]{0:T(512)S(1)}, s32[512]{0:T(512)}, u32[]{:S(2)}) copy-start(s32[512]{0:T(512)} %param.17) | copy-start | bytes 6148
  1.5 21.2 %all-to-all-start = ((s32[128,1,16]{2,1,0:T(1,128)}), s32[128,1,16]{2,1,0:T(1,128)S(1)}, u32[]{:S(2)}, u32[]{:S(2)}) async-start(s32[128,1,16]{2,1,0:T(1,128)} %broadcast_in_dim.58), calls=%async_computation | async-start | bytes 131072 | tf_op jit(solution)/shard_map/all_to_all | solution.py:141
  28.4 5.4 %copy-start.9 = (s32[1,16]{1,0:T(1,128)S(1)}, s32[1,16]{1,0:T(1,128)}, u32[]{:S(2)}) copy-start(s32[1,16]{1,0:T(1,128)} %param.19) | copy-start | bytes 196
  28.4 51.3 %all-to-all-start.1 = ((bf16[128,16,832]{2,1,0:T(8,128)(2,1)}), bf16[128,16,832]{2,1,0:T(8,128)(2,1)}, u32[]{:S(2)}, u32[]{:S(2)}) async-start(bf16[128,16,832]{2,1,0:T(8,128)(2,1)} %gather_fusion), calls=%async_computation.1 | async-start | bytes 7340032 | tf_op jit(solution)/shard_map/all_to_all | solution.py:148
  35.2 2.9 %copy-start.1 = (bf16[512,2048]{1,0:T(8,128)(2,1)S(1)}, bf16[512,2048]{1,0:T(8,128)(2,1)}, u32[]{:S(2)}) copy-start(bf16[512,2048]{1,0:T(8,128)(2,1)} %x_ref.1) | copy-start | bytes 6291460
  37.4 2.0 %copy-start.10 = (bf16[2048,512]{1,0:T(8,128)(2,1)S(1)}, bf16[2048,512]{1,0:T(8,128)(2,1)}, u32[]{:S(2)}) copy-start(bf16[2048,512]{1,0:T(8,128)(2,1)} %param.13) | copy-start | bytes 6291460
  37.4 4.2 %slice-start = ((s8[8388608]{0:T(1024)(128)(4,1)}), s8[4194304]{0:T(1024)(128)(4,1)S(1)}, s32[]{:S(2)}) async-start(s8[8388608]{0:T(1024)(128)(4,1)} %bitcast.24), calls=%async_computation.2 | async-start | bytes 8388608
  38.2 3.6 %slice-start.1 = ((s8[8388608]{0:T(1024)(128)(4,1)}), s8[4194304]{0:T(1024)(128)(4,1)S(1)}, s32[]{:S(2)}) async-start(s8[8388608]{0:T(1024)(128)(4,1)} %bitcast.24), calls=%async_computation.3 | async-start | bytes 8388608
  79.7 1.6 %copy-start.2 = (bf16[512,2048]{1,0:T(8,128)(2,1)S(1)}, bf16[512,2048]{1,0:T(8,128)(2,1)}, u32[]{:S(2)}) copy-start(bf16[512,2048]{1,0:T(8,128)(2,1)} %x_ref.1) | copy-start | bytes 6291460
  81.3 1.2 %copy-start.3 = (f32[512,512]{1,0:T(8,128)S(1)}, f32[512,512]{1,0:T(8,128)}, u32[]{:S(2)}) copy-start(f32[512,512]{1,0:T(8,128)} %fusion.10.vb_ref) | copy-start | bytes 3145732
  82.5 0.9 copy-start.4
  83.5 0.9 copy-start.5
  84.4 0.9 copy-start.6

commit v9 on v2

--- a/solution.py
+++ b/solution.py
@@ -1,6 +1,8 @@
 import jax
 import jax.numpy as jnp
 from jax import lax
+from jax.experimental import pallas as pl
+from jax.experimental.pallas import tpu as pltpu
 from jax.sharding import PartitionSpec as P
 
 HEADS = 32
@@ -127,21 +129,23 @@
     adp_dev, rank2, cols = adapter_down_weight.shape
     vcols = adapter_up_value_weight.shape[2]
     device_total = serve_count * store_count
+    panel_table = jnp.concatenate(
+        [
+            adapter_down_weight[:, :ADAPTER_RANK],
+            adapter_down_weight[:, ADAPTER_RANK:],
+            adapter_up_query_weight,
+            adapter_up_value_weight,
+        ],
+        axis=2,
+    )
     all_lists = lax.all_to_all(
         jnp.broadcast_to(adapter_per_request, (device_total, request_count)), axes, 0, 0, tiled=True
     )
     all_slots = table_lookup(adapter_panel_slot, all_lists)
     mine = all_slots // ADP_DEV == my_store
     local_pick = jnp.sum(jnp.where(mine, all_slots % ADP_DEV, 0), axis=1)
-    down = lax.all_to_all(
-        jnp.take(adapter_down_weight, local_pick, axis=0), axes, 0, 0, tiled=True
-    ).reshape(serve_count, store_count, rank2, cols)
-    upq = lax.all_to_all(
-        jnp.take(adapter_up_query_weight, local_pick, axis=0), axes, 0, 0, tiled=True
-    ).reshape(serve_count, store_count, ADAPTER_RANK, cols)
-    upv = lax.all_to_all(
-        jnp.take(adapter_up_value_weight, local_pick, axis=0), axes, 0, 0, tiled=True
-    ).reshape(serve_count, store_count, ADAPTER_RANK, vcols)
+    send = jnp.take(panel_table, local_pick, axis=0, mode="clip")
+    got = lax.all_to_all(send, axes, 0, 0, tiled=True)
 
     lengths = request_token_length[0]
     adapters = adapter_per_request[0]
@@ -154,35 +158,171 @@
     owners = table_lookup(adapter_panel_slot, adapters) // ADP_DEV
     owner_token = jnp.sum(jnp.where(member, owners[None, :], 0), axis=1)
 
-    states3 = normalized_hidden_states.reshape(tok_rows, serve_count, cols)
-    low = jnp.einsum(
-        "tsf,sorf->tor", states3, down, preferred_element_type=jnp.float32
-    ).astype(jnp.bfloat16)
-    owner_mask = owner_token[:, None, None] == jnp.arange(store_count, dtype=jnp.int32)[None, :, None]
-    low = jnp.where(owner_mask, low, jnp.zeros((), jnp.bfloat16))
-    delta_query = jnp.einsum(
-        "tor,sorf->tsf", low[..., :ADAPTER_RANK], upq, preferred_element_type=jnp.float32
-    ).astype(jnp.bfloat16).reshape(tok_rows, serve_count * cols)
-    delta_value = jnp.einsum(
-        "tor,sorf->tsf", low[..., ADAPTER_RANK:], upv, preferred_element_type=jnp.float32
-    ).astype(jnp.bfloat16).reshape(tok_rows, serve_count * vcols)
-
-    base_query = jnp.dot(
+    q_base = jnp.dot(
         normalized_hidden_states, query_weight_matrix, preferred_element_type=jnp.float32
-    ) + delta_query.astype(jnp.float32)
-    query_rot = rotary(base_query.reshape(tok_rows, HEADS, HEAD_DIM), positions).astype(
-        jnp.bfloat16
-    )
-    base_key = jnp.dot(
+    )
+    k_base = jnp.dot(
         normalized_hidden_states, key_weight_matrix, preferred_element_type=jnp.float32
     )
-    key_rot = rotary(base_key.reshape(tok_rows, KV_HEADS, HEAD_DIM), positions).astype(jnp.bfloat16)
-    value_rows = (
-        jnp.dot(normalized_hidden_states, value_weight_matrix, preferred_element_type=jnp.float32)
-        + delta_value.astype(jnp.float32)
-    ).astype(jnp.bfloat16)
-    value_rows = value_rows.reshape(tok_rows, KV_HEADS, HEAD_DIM)
-    return attention(query_rot, key_rot, value_rows, request_ids)
+    v_base = jnp.dot(
+        normalized_hidden_states, value_weight_matrix, preferred_element_type=jnp.float32
+    )
+    return fused_attention(
+        q_base, k_base, v_base, normalized_hidden_states,
+        got.reshape(-1, got.shape[-1]), owner_token, positions,
+    )
+
+
+def _swap_halves(x):
+    return jnp.concatenate([x[:, 32:64], x[:, 0:32], x[:, 96:128], x[:, 64:96]], axis=1)
+
+
+def _attend_kernel(qb_ref, kb_ref, vb_ref, x_ref, got_ref, own_ref, cos_ref, sin_ref, pos_ref,
+                   out_ref, q_s, kd_s, vd_s, dq_ref, dv_ref):
+    blk = qb_ref.shape[0]
+    rows = kd_s.shape[1]
+    b = pl.program_id(0)
+    g0 = pl.multiple_of(b * blk, blk)
+    cols = 256
+    slices = x_ref.shape[1] // cols
+    q_chunks = qb_ref.shape[1] // 128
+    k_chunks = kb_ref.shape[1] // 128
+    lane = lax.broadcasted_iota(jnp.int32, (1, 128), 1)
+    owner_lane = lax.broadcasted_iota(jnp.int32, (1, cols), 1) // 16
+
+    @pl.when(b == 0)
+    def _():
+        kd_s[:, blk:2 * blk, :] = jnp.zeros((kd_s.shape[0], blk, kd_s.shape[2]), kd_s.dtype)
+        vd_s[:, blk:2 * blk, :] = jnp.zeros((vd_s.shape[0], blk, vd_s.shape[2]), vd_s.dtype)
+
+    low_q = jnp.zeros((blk, cols), jnp.float32)
+    low_v = jnp.zeros((blk, cols), jnp.float32)
+    nt = (((1,), (1,)), ((), ()))
+    for sl in range(slices):
+        xs = x_ref[:, sl * cols:(sl + 1) * cols]
+        panel = got_ref[sl * cols:(sl + 1) * cols, 0:2 * cols]
+        low_q += lax.dot_general(xs, panel[:, 0:cols], nt, preferred_element_type=jnp.float32)
+        low_v += lax.dot_general(xs, panel[:, cols:2 * cols], nt, preferred_element_type=jnp.float32)
+    mine = owner_lane == own_ref[...]
+    low_q = jnp.where(mine, low_q.astype(jnp.bfloat16), jnp.zeros((), jnp.bfloat16))
+    low_v = jnp.where(mine, low_v.astype(jnp.bfloat16), jnp.zeros((), jnp.bfloat16))
+    pieces = []
+    for sl in range(slices):
+        upq = got_ref[sl * cols:(sl + 1) * cols, 2 * cols:3 * cols]
+        dq_ref[:, sl * cols:(sl + 1) * cols] = jnp.dot(
+            low_q, upq, preferred_element_type=jnp.float32).astype(jnp.bfloat16)
+        upv = got_ref[sl * cols:(sl + 1) * cols, 3 * cols:3 * cols + 64]
+        pieces.append(jnp.dot(low_v, upv, preferred_element_type=jnp.float32))
+    for c in range(slices // 2):
+        dv_ref[:, c * 128:(c + 1) * 128] = jnp.concatenate(
+            [pieces[2 * c], pieces[2 * c + 1]], axis=1).astype(jnp.bfloat16)
+
+    cos = cos_ref[...]
+    sin = sin_ref[...]
+
+    def q_col(c, carry2):
+        c0 = pl.multiple_of(c * 128, 128)
+        x = qb_ref[:, pl.ds(c0, 128)] + dq_ref[:, pl.ds(c0, 128)].astype(jnp.float32)
+        q_s[:, pl.ds(c0, 128)] = (x * cos + _swap_halves(x) * sin).astype(jnp.bfloat16)
+        return carry2
+
+    lax.fori_loop(0, q_chunks, q_col, 0, unroll=True)
+    zeros = jnp.zeros((blk, 64), jnp.float32)
+    for c in range(k_chunks):
+        x = kb_ref[:, c * 128:(c + 1) * 128]
+        k = (x * cos + _swap_halves(x) * sin).astype(jnp.bfloat16).astype(jnp.float32)
+        v = vb_ref[:, c * 128:(c + 1) * 128] + dv_ref[:, c * 128:(c + 1) * 128].astype(jnp.float32)
+        v = v.astype(jnp.bfloat16).astype(jnp.float32)
+        for half in range(2):
+            g = 2 * c + half
+            kg = k[:, half * 64:(half + 1) * 64]
+            vg = v[:, half * 64:(half + 1) * 64]
+            kd_s[g, pl.ds(g0, blk), :] = jnp.concatenate([kg, kg], axis=1).astype(jnp.bfloat16)
+            vd_s[g, pl.ds(g0, blk), 0:128] = jnp.concatenate([vg, zeros], axis=1).astype(jnp.bfloat16)
+            vd_s[g, pl.ds(g0, blk), 128:256] = jnp.concatenate([zeros, vg], axis=1).astype(jnp.bfloat16)
+
+    window = 2 * blk
+    per_group = HEADS // KV_HEADS
+    ws = pl.multiple_of(jnp.clip(g0 - blk, 0, rows - window), blk)
+    qpos = pos_ref[...]
+    qidx = g0 + lax.broadcasted_iota(jnp.int32, (blk, 1), 0)
+    kidx = ws + lax.broadcasted_iota(jnp.int32, (1, window), 1)
+    allowed = (kidx >= qidx - qpos) & (kidx <= qidx)
+
+    def head_pair(j, carry2):
+        g = j // (per_group // 2)
+        c0 = pl.multiple_of(j * 128, 128)
+        qc = q_s[:, pl.ds(c0, 128)]
+        kd = kd_s[g, pl.ds(ws, window), :]
+        vd = vd_s[g, pl.ds(ws, window), :]
+        zero = jnp.zeros_like(qc)
+        probs, totals = [], []
+        for half in range(2):
+            keep = (lane < 64) if half == 0 else (lane >= 64)
+            qh = jnp.where(keep, qc, zero)
+            s = lax.dot_general(qh, kd, nt, preferred_element_type=jnp.float32) * (HEAD_DIM ** -0.5)
+            s = jnp.where(allowed, s, -jnp.inf)
+            m = jnp.max(s, axis=1, keepdims=True)
+            p = jnp.exp(s - m)
+            totals.append(jnp.sum(p, axis=1, keepdims=True))
+            probs.append(p.astype(jnp.bfloat16))
+        o = (jnp.dot(probs[0], vd[:, 0:128], preferred_element_type=jnp.float32)
+             + jnp.dot(probs[1], vd[:, 128:256], preferred_element_type=jnp.float32))
+        o = jnp.where(lane < 64, o / totals[0], o / totals[1])
+        out_ref[:, pl.ds(c0, 128)] = o.astype(out_ref.dtype)
+        return carry2
+
+    lax.fori_loop(0, HEADS // 2, head_pair, 0, unroll=True)
+
+
+def rope_tables(positions):
+    half_dim = HEAD_DIM // 2
+    frequency = 500000.0 ** (-(jnp.arange(half_dim).astype(jnp.float32) * 2.0 / HEAD_DIM))
+    angles = positions.astype(jnp.float32)[:, None] * frequency[None, :]
+    cos = jnp.cos(angles)
+    sin = jnp.sin(angles)
+    cos_t = jnp.concatenate([cos, cos, cos, cos], axis=1)
+    sin_t = jnp.concatenate([-sin, sin, -sin, sin], axis=1)
+    return cos_t, sin_t
+
+
+def fused_attention(q_base, k_base, v_base, states, got, owner_token, positions):
+    rows = q_base.shape[0]
+    cos_t, sin_t = rope_tables(positions)
+    pos_col = positions.astype(jnp.int32).reshape(rows, 1)
+    own_col = owner_token.astype(jnp.int32).reshape(rows, 1)
+    flops = 2 * rows * 256 * 64 * 2 * HEADS * 2 + 2 * rows * 256 * (2 * 2048 + 2048 + 512)
+    blk = 128
+    row_block = lambda width: pl.BlockSpec((blk, width), lambda b: (b, 0))
+    return pl.pallas_call(
+        _attend_kernel,
+        out_shape=jax.ShapeDtypeStruct((rows, HEADS * HEAD_DIM), jnp.bfloat16),
+        grid=(rows // blk,),
+        in_specs=[
+            row_block(q_base.shape[1]),
+            row_block(k_base.shape[1]),
+            row_block(v_base.shape[1]),
+            row_block(states.shape[1]),
+            pl.BlockSpec(got.shape, lambda b: (0, 0)),
+            row_block(1),
+            row_block(128),
+            row_block(128),
+            row_block(1),
+        ],
+        out_specs=row_block(HEADS * HEAD_DIM),
+        scratch_shapes=[
+            pltpu.VMEM((blk, HEADS * HEAD_DIM), jnp.bfloat16),
+            pltpu.VMEM((KV_HEADS, rows, 128), jnp.bfloat16),
+            pltpu.VMEM((KV_HEADS, rows, 256), jnp.bfloat16),
+            pltpu.VMEM((blk, HEADS * HEAD_DIM), jnp.bfloat16),
+            pltpu.VMEM((blk, KV_HEADS * HEAD_DIM), jnp.bfloat16),
+        ],
+        compiler_params=pltpu.CompilerParams(
+            dimension_semantics=("arbitrary",), vmem_limit_bytes=48 * 1024 * 1024
+        ),
+        cost_estimate=pl.CostEstimate(flops=flops, transcendentals=rows * 256 * HEADS,
+                                      bytes_accessed=rows * (2048 * 8 + 512 * 8 + 256 * 4) + got.size * 2),
+    )(q_base, k_base, v_base, states, got, own_col, cos_t, sin_t, pos_col)
 
 
 def solution(mesh):

time: 240 us -> 112 us (0.47)
  matrix products: 89.4 us -> 9.48 us
  local copies, waits for them, and re-layouts: 42.9 us -> 12.3 us
  Pallas kernels: 0 us -> 26.1 us
  other arithmetic: 31 us -> 7.3 us
  waiting for transfers between devices: 48.3 us -> 39.3 us
  starting transfers between devices: 25.8 us -> 16.9 us
    dot_general x67 -> x0, matrix products: 71.2 us -> none  [the longest x32 50.1 us: attention(): jnp.einsum('qhd,kd->hqk', query_part, key_part, preferred_element_type=jn...]
    pallas_call x0 -> x1, Pallas kernels: none -> 26.1 us  [fused_attention(): pl.pallas_call(_attend_kernel, out_shape=jax.ShapeDtypeStruct((rows, HEAD...]
    convert_element_type x7 -> x0, local copies, waits for them, and re-layouts: 15.1 us -> none  [the longest x4 5.8 us: attention(): outputs.append(jnp.concatenate(pieces, axis=1).reshape(block_rows, HEADS...]
    reduce_sum x32 -> x0, other arithmetic: 10.8 us -> none  [attention(): row_total = jnp.sum(raised, axis=-1)]
    all_to_all x3 -> x1, waiting for transfers between devices: 41 us -> 31.9 us  [local(): got = lax.all_to_all(send, axes, 0, 0, tiled=True)]
    all_to_all x3 -> x1, starting transfers between devices: 14.3 us -> 5.39 us  [local(): got = lax.all_to_all(send, axes, 0, 0, tiled=True)]
    dot_general x1, matrix products: 11.6 us -> 6.02 us  [local(): jnp.dot(normalized_hidden_states, query_weight_matrix, preferred_element_...]
    add x1 -> x0, local copies, waits for them, and re-layouts: 5.35 us -> none  [local(): jnp.dot(normalized_hidden_states, query_weight_matrix, preferred_element_...]
  transfers between devices with their start and end apart: 4 -> 2, of which waited for: 4 -> 2; matrix products, arithmetic and copies ran while one was open for 8% -> 15% of each run, Pallas kernels for 0% -> 0%
where the time goes in v9:
time: 112 us; the launch traced here: 111 us
  waiting for transfers between devices  39.3 us (35%)
  Pallas kernels  26.1 us (23%)
  starting transfers between devices  16.9 us (15%)
  local copies, waits for them, and re-layouts  12.3 us (11%)
  matrix products  9.48 us (8%)
  other arithmetic  7.3 us (7%)
    all_to_all x1, waiting for transfers between devices, local(): got = lax.all_to_all(send, axes, 0, 0, tiled=True)  31.9 us
    pallas_call x1, Pallas kernels, fused_attention(): pl.pallas_call(_attend_kernel, out_shape=jax.ShapeDtypeStruct((rows, HEAD...  26.1 us
    all_to_all x1, starting transfers between devices, local(): lax.all_to_all(jnp.broadcast_to(adapter_per_request, (device_total, reque...  11.5 us
    all_to_all x1, waiting for transfers between devices, local(): lax.all_to_all(jnp.broadcast_to(adapter_per_request, (device_total, reque...  7.35 us
    dot_general x1, matrix products, local(): jnp.dot(normalized_hidden_states, query_weight_matrix, preferred_element_...  6.02 us
    unnamed x26, local copies, waits for them, and re-layouts  5.77 us
    all_to_all x1, starting transfers between devices, local(): got = lax.all_to_all(send, axes, 0, 0, tiled=True)  5.39 us
    gather x1, local copies, waits for them, and re-layouts, local(): send = jnp.take(panel_table, local_pick, axis=0, mode='clip')  2.88 us
  transfers between devices with their start and end apart: 2, of which 2 were waited for; matrix products, arithmetic and copies ran while one was open for 15% of the time, Pallas kernels for 0%

profile of v9, /device:TPU:1, one launch (start us, length us, event | category | flops | bytes accessed | tf_op | source)
XLA Modules:
  0.0 111.4 jit_solution(3159956904478150545)
XLA Ops:
  0.0 0.0 copy-start
  0.0 0.0 copy-start.8
  0.0 0.0 copy-start.7
  0.0 1.5 %broadcast_in_dim.58 = s32[128,1,16]{2,1,0:T(1,128)} broadcast(s32[16]{0:T(128)} %bitcast.21), dimensions={2} | broadcast | bytes 8256 | tf_op jit(solution)/shard_map/broadcast_in_dim | solution.py:142
  1.5 11.5 %all-to-all-start = ((s32[128,1,16]{2,1,0:T(1,128)}), s32[128,1,16]{2,1,0:T(1,128)S(1)}, u32[]{:S(2)}, u32[]{:S(2)}) async-start(s32[128,1,16]{2,1,0:T(1,128)} %broadcast_in_dim.58), calls=%async_computation | async-start | bytes 131072 | tf_op jit(solution)/shard_map/all_to_all | solution.py:141
  13.0 1.1 fusion.7
  14.1 1.1 pad_maximum_fusion
  15.2 0.0 copy-done.8
  15.2 0.0 copy-done.7
  15.2 0.2 select_reduce_fusion.3
  15.4 7.3 %all-to-all-done = s32[128,1,16]{2,1,0:T(1,128)S(1)} async-done(((s32[128,1,16]{2,1,0:T(1,128)}), s32[128,1,16]{2,1,0:T(1,128)S(1)}, u32[]{:S(2)}, u32[]{:S(2)}) %all-to-all-start) | async-done | bytes 8224 | tf_op jit(solution)/shard_map/all_to_all | solution.py:141
  22.7 2.6 %select_reduce_fusion = s32[128,16]{1,0:T(8,128)S(1)} fusion(s32[512]{0:T(512)S(1)} %copy-done.7, s32[128,16]{1,0:T(8,128)S(1)} %bitcast.18), kind=kLoop, calls=%fused_computation.1 | loop fusion | flops 3143680 | bytes 18432 | tf_op jit(solution)/shard_map/reduce_sum | solution.py:35
  25.3 0.1 fusion.3
  25.5 2.9 %gather_fusion = bf16[128,16,832]{2,1,0:T(8,128)(2,1)} fusion(bf16[32,16,832]{2,1,0:T(8,128)(2,1)S(1)} %pad_maximum_fusion, s32[1024]{0:T(1024)S(1)} %pad_clamp_fusion), kind=kCustom, calls=%fused_computation | custom fusion | bytes 6816256 | tf_op jit(solution)/shard_map/jit(_take)/gather | solution.py:147
  28.4 0.0 copy-start.9
  28.4 5.4 %all-to-all-start.1 = ((bf16[128,16,832]{2,1,0:T(8,128)(2,1)}), bf16[128,16,832]{2,1,0:T(8,128)(2,1)}, u32[]{:S(2)}, u32[]{:S(2)}) async-start(bf16[128,16,832]{2,1,0:T(8,128)(2,1)} %gather_fusion), calls=%async_computation.1 | async-start | bytes 7340032 | tf_op jit(solution)/shard_map/all_to_all | solution.py:148
  33.8 0.0 copy-done.9
  33.8 0.1 copy.24
  33.9 0.1 reduce
  34.0 0.1 convert_reduce_fusion
  34.1 0.1 select_reduce_fusion.1
  34.2 0.9 copy.27.own_ref
  35.1 0.1 copy.26
  35.2 0.0 copy-start.1
  35.3 1.0 fusion
  36.3 1.2 %pad_maximum_fusion.1 = (f32[512,128]{1,0:T(8,128)S(1)}, f32[512,128]{1,0:T(8,128)}) fusion(f32[512,32]{1,0:T(8,128)S(1)} %get-tuple-element.11, f32[512,32]{1,0:T(8,128)S(1)} %get-tuple-element.10, f32[512,32]{1,0:T(8,128)S(1)} %get-tuple-element.9), kind=kLoop, calls=%fused_computation.6 | loop fusion | flops 393216 | bytes 720896 | tf_op jit(solution)/shard_map/concatenate | solution.py:284
  37.4 0.0 copy-start.10
  37.4 0.0 slice-start
  37.5 0.7 iota_subtract_fusion.pos_ref
  38.2 0.0 copy-done
  38.2 0.0 copy-done.1
  38.2 0.0 slice-start.1
  38.2 1.2 %fusion.9.kb_ref = f32[512,512]{1,0:T(8,128)S(1)} fusion(bf16[512,2048]{1,0:T(8,128)(2,1)S(1)} %copy-done.1, bf16[2048,512]{1,0:T(8,128)(2,1)S(1)} %copy-done), kind=kOutput, calls=%fused_computation.39 | convolution fusion | flops 1073741824 | bytes 5242880 | tf_op jit(solution)/shard_map/dot_general | solution.py:164
  39.4 0.0 copy-done.10
  39.4 2.2 %fusion.10.vb_ref = f32[512,512]{1,0:T(8,128)} fusion(bf16[512,2048]{1,0:T(8,128)(2,1)S(1)} %copy-done.1, bf16[2048,512]{1,0:T(8,128)(2,1)S(1)} %copy-done.10), kind=kOutput, calls=%fused_computation.40 | convolution fusion | flops 1073741824 | bytes 5242880 | tf_op jit(solution)/shard_map/dot_general | solution.py:167
  41.6 0.0 slice-done
  41.6 0.1 slice-done.1
  41.7 6.0 %fusion.8.qb_ref = f32[512,2048]{1,0:T(8,128)} fusion(bf16[512,2048]{1,0:T(8,128)(2,1)S(1)} %copy-done.1, bf16[2048,2048]{1,0:T(8,128)(2,1)S(1)} %bitcast.25), kind=kOutput, calls=%fused_computation.38 | convolution fusion | flops 4294967296 | bytes 14680064 | tf_op jit(solution)/shard_map/dot_general | solution.py:161
  47.8 31.9 %all-to-all-done.1 = bf16[128,16,832]{2,1,0:T(8,128)(2,1)} async-done(((bf16[128,16,832]{2,1,0:T(8,128)(2,1)}), bf16[128,16,832]{2,1,0:T(8,128)(2,1)}, u32[]{:S(2)}, u32[]{:S(2)}) %all-to-all-start.1) | async-done | bytes 3407904 | tf_op jit(solution)/shard_map/all_to_all | solution.py:148
  79.7 0.0 copy-start.2
  79.7 1.6 %copy-done.2 = bf16[512,2048]{1,0:T(8,128)(2,1)S(1)} copy-done((bf16[512,2048]{1,0:T(8,128)(2,1)S(1)}, bf16[512,2048]{1,0:T(8,128)(2,1)}, u32[]{:S(2)}) %copy-start.2) | copy-done | bytes 2097176
  81.3 0.0 copy-start.3
  81.3 1.2 %copy-done.3 = f32[512,512]{1,0:T(8,128)S(1)} copy-done((f32[512,512]{1,0:T(8,128)S(1)}, f32[512,512]{1,0:T(8,128)}, u32[]{:S(2)}) %copy-start.3) | copy-done | bytes 1048600
  82.5 0.0 copy-start.4
  82.5 0.9 copy-done.4
  83.5 0.0 copy-start.5
  83.5 0.9 copy-done.5
  84.4 0.0 copy-start.6
  84.4 0.9 copy-done.6
  85.4 26.1 %shard_map.103 = bf16[512,2048]{1,0:T(8,128)(2,1)} custom-call(f32[512,2048]{1,0:T(8,128)} %fusion.8.qb_ref, f32[512,512]{1,0:T(8,128)S(1)} %fusion.9.kb_ref, f32[512,512]{1,0:T(8,128)S(1)} %copy-done.3, bf16[512,2048]{1,0:T(8,128)(2,1)S(1)} %copy-done.2, bf16[2048,832]{1,0:T(8,128)(2,1)} %bitcast.2.got_ref, s32[512,1]{1,0:T(8,128)S(1)} %copy-done.5, ...), custom_call_target="tpu_custom_call" | custom-call | flops 3892314112 | bytes 14417920 | tf_op jit(solution)/shard_map/pallas_call | solution.py:297
  (7 shorter events, 0.1 us)
Async XLA Ops:
  0.0 38.2 %copy-start = (bf16[2048,512]{1,0:T(8,128)(2,1)S(1)}, bf16[2048,512]{1,0:T(8,128)(2,1)}, u32[]{:S(2)}) copy-start(bf16[2048,512]{1,0:T(8,128)(2,1)} %param.12) | copy-start | bytes 6291460
  0.0 15.2 %copy-start.8 = (s32[1,16]{1,0:T(1,128)S(1)}, s32[1,16]{1,0:T(1,128)}, u32[]{:S(2)}) copy-start(s32[1,16]{1,0:T(1,128)} %param.18) | copy-start | bytes 196
  0.0 15.2 %copy-start.7 = (s32[512]{0:T(512)S(1)}, s32[512]{0:T(512)}, u32[]{:S(2)}) copy-start(s32[512]{0:T(512)} %param.17) | copy-start | bytes 6148
  1.5 21.2 %all-to-all-start = ((s32[128,1,16]{2,1,0:T(1,128)}), s32[128,1,16]{2,1,0:T(1,128)S(1)}, u32[]{:S(2)}, u32[]{:S(2)}) async-start(s32[128,1,16]{2,1,0:T(1,128)} %broadcast_in_dim.58), calls=%async_computation | async-start | bytes 131072 | tf_op jit(solution)/shard_map/all_to_all | solution.py:141
  28.4 5.4 %copy-start.9 = (s32[1,16]{1,0:T(1,128)S(1)}, s32[1,16]{1,0:T(1,128)}, u32[]{:S(2)}) copy-start(s32[1,16]{1,0:T(1,128)} %param.19) | copy-start | bytes 196
  28.4 51.3 %all-to-all-start.1 = ((bf16[128,16,832]{2,1,0:T(8,128)(2,1)}), bf16[128,16,832]{2,1,0:T(8,128)(2,1)}, u32[]{:S(2)}, u32[]{:S(2)}) async-start(bf16[128,16,832]{2,1,0:T(8,128)(2,1)} %gather_fusion), calls=%async_computation.1 | async-start | bytes 7340032 | tf_op jit(solution)/shard_map/all_to_all | solution.py:148
  35.2 2.9 %copy-start.1 = (bf16[512,2048]{1,0:T(8,128)(2,1)S(1)}, bf16[512,2048]{1,0:T(8,128)(2,1)}, u32[]{:S(2)}) copy-start(bf16[512,2048]{1,0:T(8,128)(2,1)} %x_ref.1) | copy-start | bytes 6291460
  37.4 2.0 %copy-start.10 = (bf16[2048,512]{1,0:T(8,128)(2,1)S(1)}, bf16[2048,512]{1,0:T(8,128)(2,1)}, u32[]{:S(2)}) copy-start(bf16[2048,512]{1,0:T(8,128)(2,1)} %param.13) | copy-start | bytes 6291460
  37.4 4.2 %slice-start = ((s8[8388608]{0:T(1024)(128)(4,1)}), s8[4194304]{0:T(1024)(128)(4,1)S(1)}, s32[]{:S(2)}) async-start(s8[8388608]{0:T(1024)(128)(4,1)} %bitcast.24), calls=%async_computation.2 | async-start | bytes 8388608
  38.2 3.6 %slice-start.1 = ((s8[8388608]{0:T(1024)(128)(4,1)}), s8[4194304]{0:T(1024)(128)(4,1)S(1)}, s32[]{:S(2)}) async-start(s8[8388608]{0:T(1024)(128)(4,1)} %bitcast.24), calls=%async_computation.3 | async-start | bytes 8388608
  79.7 1.6 %copy-start.2 = (bf16[512,2048]{1,0:T(8,128)(2,1)S(1)}, bf16[512,2048]{1,0:T(8,128)(2,1)}, u32[]{:S(2)}) copy-start(bf16[512,2048]{1,0:T(8,128)(2,1)} %x_ref.1) | copy-start | bytes 6291460
  81.3 1.2 %copy-start.3 = (f32[512,512]{1,0:T(8,128)S(1)}, f32[512,512]{1,0:T(8,128)}, u32[]{:S(2)}) copy-start(f32[512,512]{1,0:T(8,128)} %fusion.10.vb_ref) | copy-start | bytes 3145732
  82.5 0.9 copy-start.4
  83.5 0.9 copy-start.5
  84.4 0.9 copy-start.6

commit v10 on v9

--- a/solution.py
+++ b/solution.py
@@ -177,8 +177,12 @@
     return jnp.concatenate([x[:, 32:64], x[:, 0:32], x[:, 96:128], x[:, 64:96]], axis=1)
 
 
-def _attend_kernel(qb_ref, kb_ref, vb_ref, x_ref, got_ref, own_ref, cos_ref, sin_ref, pos_ref,
-                   out_ref, q_s, kd_s, vd_s, dq_ref, dv_ref):
+def _attend_kernel(qkv_ref, x_ref, got_ref, aux_ref, out_ref, q_s, kd_s, vd_s, dq_ref, dv_ref):
+    q_width = dq_ref.shape[1]
+    kv_width = dv_ref.shape[1]
+    qb_ref = qkv_ref.at[:, 0:q_width]
+    kb_ref = qkv_ref.at[:, q_width:q_width + kv_width]
+    vb_ref = qkv_ref.at[:, q_width + kv_width:q_width + 2 * kv_width]
     blk = qb_ref.shape[0]
     rows = kd_s.shape[1]
     b = pl.program_id(0)
@@ -203,7 +207,7 @@
         panel = got_ref[sl * cols:(sl + 1) * cols, 0:2 * cols]
         low_q += lax.dot_general(xs, panel[:, 0:cols], nt, preferred_element_type=jnp.float32)
         low_v += lax.dot_general(xs, panel[:, cols:2 * cols], nt, preferred_element_type=jnp.float32)
-    mine = owner_lane == own_ref[...]
+    mine = owner_lane == aux_ref[:, 257:258].astype(jnp.int32)
     low_q = jnp.where(mine, low_q.astype(jnp.bfloat16), jnp.zeros((), jnp.bfloat16))
     low_v = jnp.where(mine, low_v.astype(jnp.bfloat16), jnp.zeros((), jnp.bfloat16))
     pieces = []
@@ -217,8 +221,8 @@
         dv_ref[:, c * 128:(c + 1) * 128] = jnp.concatenate(
             [pieces[2 * c], pieces[2 * c + 1]], axis=1).astype(jnp.bfloat16)
 
-    cos = cos_ref[...]
-    sin = sin_ref[...]
+    cos = aux_ref[:, 0:128]
+    sin = aux_ref[:, 128:256]
 
     def q_col(c, carry2):
         c0 = pl.multiple_of(c * 128, 128)
@@ -244,7 +248,7 @@
     window = 2 * blk
     per_group = HEADS // KV_HEADS
     ws = pl.multiple_of(jnp.clip(g0 - blk, 0, rows - window), blk)
-    qpos = pos_ref[...]
+    qpos = aux_ref[:, 256:257].astype(jnp.int32)
     qidx = g0 + lax.broadcasted_iota(jnp.int32, (blk, 1), 0)
     kidx = ws + lax.broadcasted_iota(jnp.int32, (1, window), 1)
     allowed = (kidx >= qidx - qpos) & (kidx <= qidx)
@@ -289,8 +293,10 @@
 def fused_attention(q_base, k_base, v_base, states, got, owner_token, positions):
     rows = q_base.shape[0]
     cos_t, sin_t = rope_tables(positions)
-    pos_col = positions.astype(jnp.int32).reshape(rows, 1)
-    own_col = owner_token.astype(jnp.int32).reshape(rows, 1)
+    side = jnp.zeros((rows, 128), jnp.float32)
+    side = side.at[:, 0].set(positions.astype(jnp.float32)).at[:, 1].set(owner_token.astype(jnp.float32))
+    aux = jnp.concatenate([cos_t, sin_t, side], axis=1)
+    qkv = jnp.concatenate([q_base, k_base, v_base], axis=1)
     flops = 2 * rows * 256 * 64 * 2 * HEADS * 2 + 2 * rows * 256 * (2 * 2048 + 2048 + 512)
     blk = 128
     row_block = lambda width: pl.BlockSpec((blk, width), lambda b: (b, 0))
@@ -299,15 +305,10 @@
         out_shape=jax.ShapeDtypeStruct((rows, HEADS * HEAD_DIM), jnp.bfloat16),
         grid=(rows // blk,),
         in_specs=[
-            row_block(q_base.shape[1]),
-            row_block(k_base.shape[1]),
-            row_block(v_base.shape[1]),
+            row_block(qkv.shape[1]),
             row_block(states.shape[1]),
             pl.BlockSpec(got.shape, lambda b: (0, 0)),
-            row_block(1),
-            row_block(128),
-            row_block(128),
-            row_block(1),
+            row_block(aux.shape[1]),
         ],
         out_specs=row_block(HEADS * HEAD_DIM),
         scratch_shapes=[
@@ -322,7 +323,7 @@
         ),
         cost_estimate=pl.CostEstimate(flops=flops, transcendentals=rows * 256 * HEADS,
                                       bytes_accessed=rows * (2048 * 8 + 512 * 8 + 256 * 4) + got.size * 2),
-    )(q_base, k_base, v_base, states, got, own_col, cos_t, sin_t, pos_col)
+    )(qkv, states, got, aux)
 
 
 def solution(mesh):

time: 112 us -> 109 us (0.973)
  waiting for transfers between devices: 39.3 us -> 28.3 us
  other arithmetic: 7.3 us -> 13.6 us
  matrix products: 9.48 us -> 11.1 us
  local copies, waits for them, and re-layouts: 12.3 us -> 11 us
    all_to_all x1, waiting for transfers between devices: 31.9 us -> 24.3 us  [local(): got = lax.all_to_all(send, axes, 0, 0, tiled=True)]
    unnamed x26 -> x12, local copies, waits for them, and re-layouts: 5.77 us -> 1.62 us
    all_to_all x1, waiting for transfers between devices: 7.35 us -> 4.06 us  [local(): lax.all_to_all(jnp.broadcast_to(adapter_per_request, (device_total, reque...]
    another operation x2 -> x6, other arithmetic: 0.16 us -> 2.9 us
    concatenate x1, other arithmetic: 1.17 us -> 3.35 us  [fused_attention(): qkv = jnp.concatenate([q_base, k_base, v_base], axis=1)]
    sin x0 -> x1, other arithmetic: none -> 1.78 us  [rope_tables(): sin = jnp.sin(angles)]
    concatenate x0 -> x1, local copies, waits for them, and re-layouts: none -> 1.67 us  [fused_attention(): aux = jnp.concatenate([cos_t, sin_t, side], axis=1)]
    scatter x0 -> x2, local copies, waits for them, and re-layouts: none -> 1.31 us  [fused_attention(): side.at[:, 0].set(positions.astype(jnp.float32)).at[:, 1]]
  transfers between devices with their start and end apart: 2 -> 2, of which waited for: 2 -> 2; matrix products, arithmetic and copies ran while one was open for 15% -> 25% of each run, Pallas kernels for 0% -> 0%
where the time goes in v10:
time: 109 us
  waiting for transfers between devices  28.3 us (26%)
  Pallas kernels  27.2 us (25%)
  starting transfers between devices  17.6 us (16%)
  other arithmetic  13.6 us (12%)
  matrix products  11.1 us (10%)
  local copies, waits for them, and re-layouts  11 us (10%)
    pallas_call x1, Pallas kernels, fused_attention(): pl.pallas_call(_attend_kernel, out_shape=jax.ShapeDtypeStruct((rows, HEAD...  27.2 us
    all_to_all x1, waiting for transfers between devices, local(): got = lax.all_to_all(send, axes, 0, 0, tiled=True)  24.3 us
    all_to_all x1, starting transfers between devices, local(): lax.all_to_all(jnp.broadcast_to(adapter_per_request, (device_total, reque...  11.5 us
    dot_general x1, matrix products, local(): jnp.dot(normalized_hidden_states, query_weight_matrix, preferred_element_...  6.89 us
    all_to_all x1, starting transfers between devices, local(): got = lax.all_to_all(send, axes, 0, 0, tiled=True)  6.1 us
    all_to_all x1, waiting for transfers between devices, local(): lax.all_to_all(jnp.broadcast_to(adapter_per_request, (device_total, reque...  4.06 us
    reduce_sum x2, other arithmetic, table_lookup(): return jnp.sum(jnp.where(wanted[..., None] == entries, table, 0), axis=-1)  3.51 us
    concatenate x1, other arithmetic, fused_attention(): qkv = jnp.concatenate([q_base, k_base, v_base], axis=1)  3.35 us
  transfers between devices with their start and end apart: 2, of which 2 were waited for; matrix products, arithmetic and copies ran while one was open for 25% of the time, Pallas kernels for 0%

profile of v10, /device:TPU:1, one launch (start us, length us, event | category | flops | bytes accessed | tf_op | source)
XLA Modules:
  0.0 109.0 jit_solution(3178545947862882289)
XLA Ops:
  0.0 0.0 copy-start
  0.0 0.0 copy-start.4
  0.0 1.5 %broadcast_in_dim.59 = s32[128,1,16]{2,1,0:T(1,128)} broadcast(s32[16]{0:T(128)} %bitcast.21), dimensions={2} | broadcast | bytes 8256 | tf_op jit(solution)/shard_map/broadcast_in_dim | solution.py:142
  1.5 11.5 %all-to-all-start = ((s32[128,1,16]{2,1,0:T(1,128)}), s32[128,1,16]{2,1,0:T(1,128)S(1)}, u32[]{:S(2)}, u32[]{:S(2)}) async-start(s32[128,1,16]{2,1,0:T(1,128)} %broadcast_in_dim.59), calls=%async_computation | async-start | bytes 131072 | tf_op jit(solution)/shard_map/all_to_all | solution.py:141
  13.0 0.7 copy.34
  13.7 0.1 reduce.14
  13.9 0.1 convert_reduce_fusion
  14.0 0.7 fusion.6
  14.6 1.1 fusion.7
  15.7 0.9 select_reduce_fusion.2
  16.6 1.1 %pad_maximum_fusion.1 = bf16[32,16,832]{2,1,0:T(8,128)(2,1)S(1)} fusion(bf16[32,16,64]{2,1,0:T(8,128)(2,1)} %param.20, bf16[32,16,256]{2,1,0:T(8,128)(2,1)} %param.19, bf16[32,16,256]{2,1,0:T(8,128)(2,1)S(1)} %get-tuple-element.32, bf16[32,16,256]{2,1,0:T(8,128)(2,1)S(1)} %get-tuple-element.31), kind=kLoop, calls=%fused_computation.4 | loop fusion | flops 3407872 | bytes 1703936 | tf_op jit(solution)/shard_map/concatenate | solution.py:132
  17.7 0.1 select_reduce_fusion.1
  17.8 0.1 copy.36
  17.9 0.7 compare_reduce_fusion
  18.6 4.1 %all-to-all-done = s32[128,1,16]{2,1,0:T(1,128)S(1)} async-done(((s32[128,1,16]{2,1,0:T(1,128)}), s32[128,1,16]{2,1,0:T(1,128)S(1)}, u32[]{:S(2)}, u32[]{:S(2)}) %all-to-all-start) | async-done | bytes 8224 | tf_op jit(solution)/shard_map/all_to_all | solution.py:141
  22.7 0.0 copy-done.4
  22.7 2.6 %select_reduce_fusion = s32[128,16]{1,0:T(8,128)S(1)} fusion(s32[512]{0:T(512)S(1)} %copy-done.4, s32[128,16]{1,0:T(8,128)S(1)} %bitcast.18), kind=kLoop, calls=%fused_computation.2 | loop fusion | flops 3143680 | bytes 18432 | tf_op jit(solution)/shard_map/reduce_sum | solution.py:35
  25.4 0.1 fusion.3
  25.5 2.9 %gather_fusion = bf16[128,16,832]{2,1,0:T(8,128)(2,1)} fusion(bf16[32,16,832]{2,1,0:T(8,128)(2,1)S(1)} %pad_maximum_fusion.1, s32[1024]{0:T(1024)S(1)} %pad_clamp_fusion), kind=kCustom, calls=%fused_computation | custom fusion | bytes 6816256 | tf_op jit(solution)/shard_map/jit(_take)/gather | solution.py:147
  28.4 6.1 %all-to-all-start.1 = ((bf16[128,16,832]{2,1,0:T(8,128)(2,1)}), bf16[128,16,832]{2,1,0:T(8,128)(2,1)}, u32[]{:S(2)}, u32[]{:S(2)}) async-start(bf16[128,16,832]{2,1,0:T(8,128)(2,1)} %gather_fusion), calls=%async_computation.1 | async-start | bytes 7340032 | tf_op jit(solution)/shard_map/all_to_all | solution.py:148
  34.5 0.7 convert_select_fusion.1
  35.2 0.1 copy.37
  35.3 0.6 compare_reduce_fusion.1
  36.0 0.7 convert_select_fusion
  36.7 1.3 %scatter.9 = f32[512,128]{1,0:T(8,128)S(1)} dynamic-update-slice(f32[512,128]{1,0:T(8,128)S(1)} %scatter.6, f32[512,1]{1,0:T(8,128)S(1)} %copy.37, s32[]{:T(128)} %constant.94.clone.1, s32[]{:T(128)} %constant.95.clone.1) | dynamic-update-slice | bytes 4100 | tf_op jit(solution)/shard_map/scatter | solution.py:297
  38.0 0.0 copy-start.3
  38.0 1.8 %multiply_sine_fusion = (f32[512,32]{1,0:T(8,128)S(1)}, f32[512,32]{1,0:T(8,128)}, f32[512,32]{1,0:T(8,128)S(1)}) fusion(f32[512]{0:T(512)S(1)} %subtract_convert_fusion, f32[32]{0:T(128)S(1)} %negate_power_fusion), kind=kLoop, calls=%fused_computation.5 | loop fusion | flops 32768 | bytes 198784 | tf_op jit(solution)/shard_map/sin | solution.py:287
  39.8 0.0 copy-done.3
  39.8 1.7 %concatenate.15.aux_ref = f32[512,384]{1,0:T(8,128)S(1)} concatenate(f32[512,32]{1,0:T(8,128)S(1)} %get-tuple-element.35, f32[512,32]{1,0:T(8,128)S(1)} %get-tuple-element.35, f32[512,32]{1,0:T(8,128)S(1)} %get-tuple-element.35, f32[512,32]{1,0:T(8,128)S(1)} %get-tuple-element.35, f32[512,32]{1,0:T(8,128)} %get-tuple-element.34, f32[512,32]{1,0:T(8,128)S(1)} %get-tuple-element.33, ...), dimensions={1} | concatenate | bytes 1572864 | tf_op jit(solution)/shard_map/concatenate | solution.py:298
  41.5 0.0 copy-done
  41.5 0.0 copy-start.1
  41.5 0.0 copy-start.5
  41.5 3.0 %fusion.10 = f32[512,512]{1,0:T(8,128)S(1)} fusion(bf16[512,2048]{1,0:T(8,128)(2,1)} %x_ref.1, bf16[2048,512]{1,0:T(8,128)(2,1)S(1)} %copy-done), kind=kOutput, calls=%fused_computation.43 | convolution fusion | flops 1073741824 | bytes 5242880 | tf_op jit(solution)/shard_map/dot_general | solution.py:167
  44.5 0.0 copy-done.1
  44.5 0.0 copy-done.5
  44.5 1.2 %fusion.9 = f32[512,512]{1,0:T(8,128)S(1)} fusion(bf16[512,2048]{1,0:T(8,128)(2,1)S(1)} %copy-done.1, bf16[2048,512]{1,0:T(8,128)(2,1)S(1)} %copy-done.5), kind=kOutput, calls=%fused_computation.42 | convolution fusion | flops 1073741824 | bytes 5242880 | tf_op jit(solution)/shard_map/dot_general | solution.py:164
  45.8 6.9 %fusion.8 = f32[512,2048]{1,0:T(8,128)S(1)} fusion(bf16[512,2048]{1,0:T(8,128)(2,1)S(1)} %copy-done.1, bf16[2048,2048]{1,0:T(8,128)(2,1)} %param.15), kind=kOutput, calls=%fused_computation.41 | convolution fusion | flops 4294967296 | bytes 14680064 | tf_op jit(solution)/shard_map/dot_general | solution.py:161
  52.7 3.3 %pad_maximum_fusion.qkv_ref = f32[512,3072]{1,0:T(8,128)} fusion(f32[512,512]{1,0:T(8,128)S(1)} %fusion.10, f32[512,512]{1,0:T(8,128)S(1)} %fusion.9, f32[512,2048]{1,0:T(8,128)S(1)} %fusion.8), kind=kLoop, calls=%fused_computation.1 | loop fusion | flops 3145728 | bytes 12582912 | tf_op jit(solution)/shard_map/concatenate | solution.py:299
  56.0 24.3 %all-to-all-done.1 = bf16[128,16,832]{2,1,0:T(8,128)(2,1)} async-done(((bf16[128,16,832]{2,1,0:T(8,128)(2,1)}), bf16[128,16,832]{2,1,0:T(8,128)(2,1)}, u32[]{:S(2)}, u32[]{:S(2)}) %all-to-all-start.1) | async-done | bytes 3407904 | tf_op jit(solution)/shard_map/all_to_all | solution.py:148
  80.3 0.0 copy-start.2
  80.3 1.6 %copy-done.2 = bf16[512,2048]{1,0:T(8,128)(2,1)S(1)} copy-done((bf16[512,2048]{1,0:T(8,128)(2,1)S(1)}, bf16[512,2048]{1,0:T(8,128)(2,1)}, u32[]{:S(2)}) %copy-start.2) | copy-done | bytes 2097176
  81.9 27.2 %shard_map.103 = bf16[512,2048]{1,0:T(8,128)(2,1)} custom-call(f32[512,3072]{1,0:T(8,128)} %pad_maximum_fusion.qkv_ref, bf16[512,2048]{1,0:T(8,128)(2,1)S(1)} %copy-done.2, bf16[2048,832]{1,0:T(8,128)(2,1)} %bitcast.2.got_ref, f32[512,384]{1,0:T(8,128)S(1)} %concatenate.15.aux_ref), custom_call_target="tpu_custom_call" | custom-call | flops 3892314112 | bytes 14417920 | tf_op jit(solution)/shard_map/pallas_call | solution.py:303
  (6 shorter events, 0.1 us)
Async XLA Ops:
  0.0 41.5 %copy-start = (bf16[2048,512]{1,0:T(8,128)(2,1)S(1)}, bf16[2048,512]{1,0:T(8,128)(2,1)}, u32[]{:S(2)}) copy-start(bf16[2048,512]{1,0:T(8,128)(2,1)} %param.17) | copy-start | bytes 6291460
  0.0 22.7 %copy-start.4 = (s32[512]{0:T(512)S(1)}, s32[512]{0:T(512)}, u32[]{:S(2)}) copy-start(s32[512]{0:T(512)} %param.21) | copy-start | bytes 6148
  1.5 21.2 %all-to-all-start = ((s32[128,1,16]{2,1,0:T(1,128)}), s32[128,1,16]{2,1,0:T(1,128)S(1)}, u32[]{:S(2)}, u32[]{:S(2)}) async-start(s32[128,1,16]{2,1,0:T(1,128)} %broadcast_in_dim.59), calls=%async_computation | async-start | bytes 131072 | tf_op jit(solution)/shard_map/all_to_all | solution.py:141
  28.4 51.9 %all-to-all-start.1 = ((bf16[128,16,832]{2,1,0:T(8,128)(2,1)}), bf16[128,16,832]{2,1,0:T(8,128)(2,1)}, u32[]{:S(2)}, u32[]{:S(2)}) async-start(bf16[128,16,832]{2,1,0:T(8,128)(2,1)} %gather_fusion), calls=%async_computation.1 | async-start | bytes 7340032 | tf_op jit(solution)/shard_map/all_to_all | solution.py:148
  38.0 1.8 %copy-start.3 = (f32[512,128]{1,0:T(8,128)}, f32[512,128]{1,0:T(8,128)S(1)}, u32[]{:S(2)}) copy-start(f32[512,128]{1,0:T(8,128)S(1)} %scatter.9) | copy-start | bytes 786436
  41.5 3.0 %copy-start.1 = (bf16[512,2048]{1,0:T(8,128)(2,1)S(1)}, bf16[512,2048]{1,0:T(8,128)(2,1)}, u32[]{:S(2)}) copy-start(bf16[512,2048]{1,0:T(8,128)(2,1)} %x_ref.1) | copy-start | bytes 6291460
  41.5 3.0 %copy-start.5 = (bf16[2048,512]{1,0:T(8,128)(2,1)S(1)}, bf16[2048,512]{1,0:T(8,128)(2,1)}, u32[]{:S(2)}) copy-start(bf16[2048,512]{1,0:T(8,128)(2,1)} %param.16) | copy-start | bytes 6291460
  80.3 1.6 %copy-start.2 = (bf16[512,2048]{1,0:T(8,128)(2,1)S(1)}, bf16[512,2048]{1,0:T(8,128)(2,1)}, u32[]{:S(2)}) copy-start(bf16[512,2048]{1,0:T(8,128)(2,1)} %x_ref.1) | copy-start | bytes 6291460

commit v11 on v10

--- a/solution.py
+++ b/solution.py
@@ -272,7 +272,7 @@
             probs.append(p.astype(jnp.bfloat16))
         o = (jnp.dot(probs[0], vd[:, 0:128], preferred_element_type=jnp.float32)
              + jnp.dot(probs[1], vd[:, 128:256], preferred_element_type=jnp.float32))
-        o = jnp.where(lane < 64, o / totals[0], o / totals[1])
+        o = o * jnp.where(lane < 64, 1.0 / totals[0], 1.0 / totals[1])
         out_ref[:, pl.ds(c0, 128)] = o.astype(out_ref.dtype)
         return carry2
 

time: 109 us -> 109 us (level)
  no operation moved by 1% of the time
where the time goes in v11:
time: 109 us
  waiting for transfers between devices  28.3 us (26%)
  Pallas kernels  27.2 us (25%)
  starting transfers between devices  17.6 us (16%)
  other arithmetic  13.6 us (12%)
  matrix products  11.1 us (10%)
  local copies, waits for them, and re-layouts  11 us (10%)
    pallas_call x1, Pallas kernels, fused_attention(): pl.pallas_call(_attend_kernel, out_shape=jax.ShapeDtypeStruct((rows, HEAD...  27.2 us
    all_to_all x1, waiting for transfers between devices, local(): got = lax.all_to_all(send, axes, 0, 0, tiled=True)  24.3 us
    all_to_all x1, starting transfers between devices, local(): lax.all_to_all(jnp.broadcast_to(adapter_per_request, (device_total, reque...  11.5 us
    dot_general x1, matrix products, local(): jnp.dot(normalized_hidden_states, query_weight_matrix, preferred_element_...  6.89 us
    all_to_all x1, starting transfers between devices, local(): got = lax.all_to_all(send, axes, 0, 0, tiled=True)  6.1 us
    all_to_all x1, waiting for transfers between devices, local(): lax.all_to_all(jnp.broadcast_to(adapter_per_request, (device_total, reque...  4.06 us
    reduce_sum x2, other arithmetic, table_lookup(): return jnp.sum(jnp.where(wanted[..., None] == entries, table, 0), axis=-1)  3.51 us
    concatenate x1, other arithmetic, fused_attention(): qkv = jnp.concatenate([q_base, k_base, v_base], axis=1)  3.35 us
  transfers between devices with their start and end apart: 2, of which 2 were waited for; matrix products, arithmetic and copies ran while one was open for 25% of the time, Pallas kernels for 0%

profile of v11, /device:TPU:1, one launch (start us, length us, event | category | flops | bytes accessed | tf_op | source)
XLA Modules:
  0.0 109.1 jit_solution(14005111562628437003)
XLA Ops:
  0.0 0.0 copy-start
  0.0 0.0 copy-start.4
  0.0 1.5 %broadcast_in_dim.59 = s32[128,1,16]{2,1,0:T(1,128)} broadcast(s32[16]{0:T(128)} %bitcast.21), dimensions={2} | broadcast | bytes 8256 | tf_op jit(solution)/shard_map/broadcast_in_dim | solution.py:142
  1.5 11.5 %all-to-all-start = ((s32[128,1,16]{2,1,0:T(1,128)}), s32[128,1,16]{2,1,0:T(1,128)S(1)}, u32[]{:S(2)}, u32[]{:S(2)}) async-start(s32[128,1,16]{2,1,0:T(1,128)} %broadcast_in_dim.59), calls=%async_computation | async-start | bytes 131072 | tf_op jit(solution)/shard_map/all_to_all | solution.py:141
  13.0 0.7 copy.34
  13.7 0.1 reduce.14
  13.9 0.1 convert_reduce_fusion
  14.0 0.7 fusion.6
  14.6 1.1 fusion.7
  15.7 0.9 select_reduce_fusion.2
  16.6 1.1 %pad_maximum_fusion.1 = bf16[32,16,832]{2,1,0:T(8,128)(2,1)S(1)} fusion(bf16[32,16,64]{2,1,0:T(8,128)(2,1)} %param.20, bf16[32,16,256]{2,1,0:T(8,128)(2,1)} %param.19, bf16[32,16,256]{2,1,0:T(8,128)(2,1)S(1)} %get-tuple-element.32, bf16[32,16,256]{2,1,0:T(8,128)(2,1)S(1)} %get-tuple-element.31), kind=kLoop, calls=%fused_computation.4 | loop fusion | flops 3407872 | bytes 1703936 | tf_op jit(solution)/shard_map/concatenate | solution.py:132
  17.7 0.1 select_reduce_fusion.1
  17.8 0.1 copy.36
  17.9 0.7 compare_reduce_fusion
  18.6 4.1 %all-to-all-done = s32[128,1,16]{2,1,0:T(1,128)S(1)} async-done(((s32[128,1,16]{2,1,0:T(1,128)}), s32[128,1,16]{2,1,0:T(1,128)S(1)}, u32[]{:S(2)}, u32[]{:S(2)}) %all-to-all-start) | async-done | bytes 8224 | tf_op jit(solution)/shard_map/all_to_all | solution.py:141
  22.7 0.0 copy-done.4
  22.7 2.6 %select_reduce_fusion = s32[128,16]{1,0:T(8,128)S(1)} fusion(s32[512]{0:T(512)S(1)} %copy-done.4, s32[128,16]{1,0:T(8,128)S(1)} %bitcast.18), kind=kLoop, calls=%fused_computation.2 | loop fusion | flops 3143680 | bytes 18432 | tf_op jit(solution)/shard_map/reduce_sum | solution.py:35
  25.4 0.1 fusion.3
  25.5 2.9 %gather_fusion = bf16[128,16,832]{2,1,0:T(8,128)(2,1)} fusion(bf16[32,16,832]{2,1,0:T(8,128)(2,1)S(1)} %pad_maximum_fusion.1, s32[1024]{0:T(1024)S(1)} %pad_clamp_fusion), kind=kCustom, calls=%fused_computation | custom fusion | bytes 6816256 | tf_op jit(solution)/shard_map/jit(_take)/gather | solution.py:147
  28.4 6.1 %all-to-all-start.1 = ((bf16[128,16,832]{2,1,0:T(8,128)(2,1)}), bf16[128,16,832]{2,1,0:T(8,128)(2,1)}, u32[]{:S(2)}, u32[]{:S(2)}) async-start(bf16[128,16,832]{2,1,0:T(8,128)(2,1)} %gather_fusion), calls=%async_computation.1 | async-start | bytes 7340032 | tf_op jit(solution)/shard_map/all_to_all | solution.py:148
  34.5 0.7 convert_select_fusion.1
  35.2 0.1 copy.37
  35.3 0.6 compare_reduce_fusion.1
  36.0 0.7 convert_select_fusion
  36.7 1.3 %scatter.9 = f32[512,128]{1,0:T(8,128)S(1)} dynamic-update-slice(f32[512,128]{1,0:T(8,128)S(1)} %scatter.6, f32[512,1]{1,0:T(8,128)S(1)} %copy.37, s32[]{:T(128)} %constant.94.clone.1, s32[]{:T(128)} %constant.95.clone.1) | dynamic-update-slice | bytes 4100 | tf_op jit(solution)/shard_map/scatter | solution.py:297
  38.0 0.0 copy-start.3
  38.0 1.8 %multiply_sine_fusion = (f32[512,32]{1,0:T(8,128)S(1)}, f32[512,32]{1,0:T(8,128)}, f32[512,32]{1,0:T(8,128)S(1)}) fusion(f32[512]{0:T(512)S(1)} %subtract_convert_fusion, f32[32]{0:T(128)S(1)} %negate_power_fusion), kind=kLoop, calls=%fused_computation.5 | loop fusion | flops 32768 | bytes 198784 | tf_op jit(solution)/shard_map/sin | solution.py:287
  39.8 0.0 copy-done.3
  39.8 1.7 %concatenate.15.aux_ref = f32[512,384]{1,0:T(8,128)S(1)} concatenate(f32[512,32]{1,0:T(8,128)S(1)} %get-tuple-element.35, f32[512,32]{1,0:T(8,128)S(1)} %get-tuple-element.35, f32[512,32]{1,0:T(8,128)S(1)} %get-tuple-element.35, f32[512,32]{1,0:T(8,128)S(1)} %get-tuple-element.35, f32[512,32]{1,0:T(8,128)} %get-tuple-element.34, f32[512,32]{1,0:T(8,128)S(1)} %get-tuple-element.33, ...), dimensions={1} | concatenate | bytes 1572864 | tf_op jit(solution)/shard_map/concatenate | solution.py:298
  41.5 0.0 copy-done
  41.5 0.0 copy-start.1
  41.5 0.0 copy-start.5
  41.5 3.0 %fusion.10 = f32[512,512]{1,0:T(8,128)S(1)} fusion(bf16[512,2048]{1,0:T(8,128)(2,1)} %x_ref.1, bf16[2048,512]{1,0:T(8,128)(2,1)S(1)} %copy-done), kind=kOutput, calls=%fused_computation.43 | convolution fusion | flops 1073741824 | bytes 5242880 | tf_op jit(solution)/shard_map/dot_general | solution.py:167
  44.5 0.0 copy-done.1
  44.5 0.0 copy-done.5
  44.5 1.2 %fusion.9 = f32[512,512]{1,0:T(8,128)S(1)} fusion(bf16[512,2048]{1,0:T(8,128)(2,1)S(1)} %copy-done.1, bf16[2048,512]{1,0:T(8,128)(2,1)S(1)} %copy-done.5), kind=kOutput, calls=%fused_computation.42 | convolution fusion | flops 1073741824 | bytes 5242880 | tf_op jit(solution)/shard_map/dot_general | solution.py:164
  45.8 6.9 %fusion.8 = f32[512,2048]{1,0:T(8,128)S(1)} fusion(bf16[512,2048]{1,0:T(8,128)(2,1)S(1)} %copy-done.1, bf16[2048,2048]{1,0:T(8,128)(2,1)} %param.15), kind=kOutput, calls=%fused_computation.41 | convolution fusion | flops 4294967296 | bytes 14680064 | tf_op jit(solution)/shard_map/dot_general | solution.py:161
  52.7 3.3 %pad_maximum_fusion.qkv_ref = f32[512,3072]{1,0:T(8,128)} fusion(f32[512,512]{1,0:T(8,128)S(1)} %fusion.10, f32[512,512]{1,0:T(8,128)S(1)} %fusion.9, f32[512,2048]{1,0:T(8,128)S(1)} %fusion.8), kind=kLoop, calls=%fused_computation.1 | loop fusion | flops 3145728 | bytes 12582912 | tf_op jit(solution)/shard_map/concatenate | solution.py:299
  56.0 24.3 %all-to-all-done.1 = bf16[128,16,832]{2,1,0:T(8,128)(2,1)} async-done(((bf16[128,16,832]{2,1,0:T(8,128)(2,1)}), bf16[128,16,832]{2,1,0:T(8,128)(2,1)}, u32[]{:S(2)}, u32[]{:S(2)}) %all-to-all-start.1) | async-done | bytes 3407904 | tf_op jit(solution)/shard_map/all_to_all | solution.py:148
  80.3 0.0 copy-start.2
  80.3 1.6 %copy-done.2 = bf16[512,2048]{1,0:T(8,128)(2,1)S(1)} copy-done((bf16[512,2048]{1,0:T(8,128)(2,1)S(1)}, bf16[512,2048]{1,0:T(8,128)(2,1)}, u32[]{:S(2)}) %copy-start.2) | copy-done | bytes 2097176
  81.9 27.2 %shard_map.103 = bf16[512,2048]{1,0:T(8,128)(2,1)} custom-call(f32[512,3072]{1,0:T(8,128)} %pad_maximum_fusion.qkv_ref, bf16[512,2048]{1,0:T(8,128)(2,1)S(1)} %copy-done.2, bf16[2048,832]{1,0:T(8,128)(2,1)} %bitcast.2.got_ref, f32[512,384]{1,0:T(8,128)S(1)} %concatenate.15.aux_ref), custom_call_target="tpu_custom_call" | custom-call | flops 3892314112 | bytes 14417920 | tf_op jit(solution)/shard_map/pallas_call | solution.py:303
  (6 shorter events, 0.1 us)
Async XLA Ops:
  0.0 41.5 %copy-start = (bf16[2048,512]{1,0:T(8,128)(2,1)S(1)}, bf16[2048,512]{1,0:T(8,128)(2,1)}, u32[]{:S(2)}) copy-start(bf16[2048,512]{1,0:T(8,128)(2,1)} %param.17) | copy-start | bytes 6291460
  0.0 22.7 %copy-start.4 = (s32[512]{0:T(512)S(1)}, s32[512]{0:T(512)}, u32[]{:S(2)}) copy-start(s32[512]{0:T(512)} %param.21) | copy-start | bytes 6148
  1.5 21.2 %all-to-all-start = ((s32[128,1,16]{2,1,0:T(1,128)}), s32[128,1,16]{2,1,0:T(1,128)S(1)}, u32[]{:S(2)}, u32[]{:S(2)}) async-start(s32[128,1,16]{2,1,0:T(1,128)} %broadcast_in_dim.59), calls=%async_computation | async-start | bytes 131072 | tf_op jit(solution)/shard_map/all_to_all | solution.py:141
  28.4 51.9 %all-to-all-start.1 = ((bf16[128,16,832]{2,1,0:T(8,128)(2,1)}), bf16[128,16,832]{2,1,0:T(8,128)(2,1)}, u32[]{:S(2)}, u32[]{:S(2)}) async-start(bf16[128,16,832]{2,1,0:T(8,128)(2,1)} %gather_fusion), calls=%async_computation.1 | async-start | bytes 7340032 | tf_op jit(solution)/shard_map/all_to_all | solution.py:148
  38.0 1.8 %copy-start.3 = (f32[512,128]{1,0:T(8,128)}, f32[512,128]{1,0:T(8,128)S(1)}, u32[]{:S(2)}) copy-start(f32[512,128]{1,0:T(8,128)S(1)} %scatter.9) | copy-start | bytes 786436
  41.5 3.0 %copy-start.1 = (bf16[512,2048]{1,0:T(8,128)(2,1)S(1)}, bf16[512,2048]{1,0:T(8,128)(2,1)}, u32[]{:S(2)}) copy-start(bf16[512,2048]{1,0:T(8,128)(2,1)} %x_ref.1) | copy-start | bytes 6291460
  41.5 3.0 %copy-start.5 = (bf16[2048,512]{1,0:T(8,128)(2,1)S(1)}, bf16[2048,512]{1,0:T(8,128)(2,1)}, u32[]{:S(2)}) copy-start(bf16[2048,512]{1,0:T(8,128)(2,1)} %param.16) | copy-start | bytes 6291460
  80.3 1.6 %copy-start.2 = (bf16[512,2048]{1,0:T(8,128)(2,1)S(1)}, bf16[512,2048]{1,0:T(8,128)(2,1)}, u32[]{:S(2)}) copy-start(bf16[512,2048]{1,0:T(8,128)(2,1)} %x_ref.1) | copy-start | bytes 6291460

commit v12 on v11

--- a/solution.py
+++ b/solution.py
@@ -184,7 +184,7 @@
     kb_ref = qkv_ref.at[:, q_width:q_width + kv_width]
     vb_ref = qkv_ref.at[:, q_width + kv_width:q_width + 2 * kv_width]
     blk = qb_ref.shape[0]
-    rows = kd_s.shape[1]
+    rows = kd_s.shape[2]
     b = pl.program_id(0)
     g0 = pl.multiple_of(b * blk, blk)
     cols = 256
@@ -196,7 +196,7 @@
 
     @pl.when(b == 0)
     def _():
-        kd_s[:, blk:2 * blk, :] = jnp.zeros((kd_s.shape[0], blk, kd_s.shape[2]), kd_s.dtype)
+        kd_s[:, :, blk:2 * blk] = jnp.zeros((kd_s.shape[0], kd_s.shape[1], blk), kd_s.dtype)
         vd_s[:, blk:2 * blk, :] = jnp.zeros((vd_s.shape[0], blk, vd_s.shape[2]), vd_s.dtype)
 
     low_q = jnp.zeros((blk, cols), jnp.float32)
@@ -241,7 +241,7 @@
             g = 2 * c + half
             kg = k[:, half * 64:(half + 1) * 64]
             vg = v[:, half * 64:(half + 1) * 64]
-            kd_s[g, pl.ds(g0, blk), :] = jnp.concatenate([kg, kg], axis=1).astype(jnp.bfloat16)
+            kd_s[g, :, pl.ds(g0, blk)] = jnp.transpose(jnp.concatenate([kg, kg], axis=1)).astype(jnp.bfloat16)
             vd_s[g, pl.ds(g0, blk), 0:128] = jnp.concatenate([vg, zeros], axis=1).astype(jnp.bfloat16)
             vd_s[g, pl.ds(g0, blk), 128:256] = jnp.concatenate([zeros, vg], axis=1).astype(jnp.bfloat16)
 
@@ -257,14 +257,14 @@
         g = j // (per_group // 2)
         c0 = pl.multiple_of(j * 128, 128)
         qc = q_s[:, pl.ds(c0, 128)]
-        kd = kd_s[g, pl.ds(ws, window), :]
+        kd = kd_s[g, :, pl.ds(ws, window)]
         vd = vd_s[g, pl.ds(ws, window), :]
         zero = jnp.zeros_like(qc)
         probs, totals = [], []
         for half in range(2):
             keep = (lane < 64) if half == 0 else (lane >= 64)
             qh = jnp.where(keep, qc, zero)
-            s = lax.dot_general(qh, kd, nt, preferred_element_type=jnp.float32) * (HEAD_DIM ** -0.5)
+            s = jnp.dot(qh, kd, preferred_element_type=jnp.float32) * (HEAD_DIM ** -0.5)
             s = jnp.where(allowed, s, -jnp.inf)
             m = jnp.max(s, axis=1, keepdims=True)
             p = jnp.exp(s - m)
@@ -313,7 +313,7 @@
         out_specs=row_block(HEADS * HEAD_DIM),
         scratch_shapes=[
             pltpu.VMEM((blk, HEADS * HEAD_DIM), jnp.bfloat16),
-            pltpu.VMEM((KV_HEADS, rows, 128), jnp.bfloat16),
+            pltpu.VMEM((KV_HEADS, 128, rows), jnp.bfloat16),
             pltpu.VMEM((KV_HEADS, rows, 256), jnp.bfloat16),
             pltpu.VMEM((blk, HEADS * HEAD_DIM), jnp.bfloat16),
             pltpu.VMEM((blk, KV_HEADS * HEAD_DIM), jnp.bfloat16),

time: 109 us -> 108 us (level)
  Pallas kernels: 27.2 us -> 25.8 us
    pallas_call x1, Pallas kernels: 27.2 us -> 25.8 us  [fused_attention(): pl.pallas_call(_attend_kernel, out_shape=jax.ShapeDtypeStruct((rows, HEAD...]
where the time goes in v12:
time: 108 us
  waiting for transfers between devices  28.3 us (26%)
  Pallas kernels  25.8 us (24%)
  starting transfers between devices  17.6 us (16%)
  other arithmetic  13.6 us (13%)
  matrix products  11.1 us (10%)
  local copies, waits for them, and re-layouts  11 us (10%)
    pallas_call x1, Pallas kernels, fused_attention(): pl.pallas_call(_attend_kernel, out_shape=jax.ShapeDtypeStruct((rows, HEAD...  25.8 us
    all_to_all x1, waiting for transfers between devices, local(): got = lax.all_to_all(send, axes, 0, 0, tiled=True)  24.3 us
    all_to_all x1, starting transfers between devices, local(): lax.all_to_all(jnp.broadcast_to(adapter_per_request, (device_total, reque...  11.5 us
    dot_general x1, matrix products, local(): jnp.dot(normalized_hidden_states, query_weight_matrix, preferred_element_...  6.89 us
    all_to_all x1, starting transfers between devices, local(): got = lax.all_to_all(send, axes, 0, 0, tiled=True)  6.1 us
    all_to_all x1, waiting for transfers between devices, local(): lax.all_to_all(jnp.broadcast_to(adapter_per_request, (device_total, reque...  4.06 us
    reduce_sum x2, other arithmetic, table_lookup(): return jnp.sum(jnp.where(wanted[..., None] == entries, table, 0), axis=-1)  3.51 us
    concatenate x1, other arithmetic, fused_attention(): qkv = jnp.concatenate([q_base, k_base, v_base], axis=1)  3.35 us
  transfers between devices with their start and end apart: 2, of which 2 were waited for; matrix products, arithmetic and copies ran while one was open for 25% of the time, Pallas kernels for 0%

profile of v12, /device:TPU:1, one launch (start us, length us, event | category | flops | bytes accessed | tf_op | source)
XLA Modules:
  0.0 107.6 jit_solution(12795956071798014086)
XLA Ops:
  0.0 0.0 copy-start
  0.0 0.0 copy-start.4
  0.0 1.5 %broadcast_in_dim.59 = s32[128,1,16]{2,1,0:T(1,128)} broadcast(s32[16]{0:T(128)} %bitcast.21), dimensions={2} | broadcast | bytes 8256 | tf_op jit(solution)/shard_map/broadcast_in_dim | solution.py:142
  1.5 11.5 %all-to-all-start = ((s32[128,1,16]{2,1,0:T(1,128)}), s32[128,1,16]{2,1,0:T(1,128)S(1)}, u32[]{:S(2)}, u32[]{:S(2)}) async-start(s32[128,1,16]{2,1,0:T(1,128)} %broadcast_in_dim.59), calls=%async_computation | async-start | bytes 131072 | tf_op jit(solution)/shard_map/all_to_all | solution.py:141
  13.0 0.7 copy.34
  13.7 0.1 reduce.14
  13.9 0.1 convert_reduce_fusion
  14.0 0.7 fusion.6
  14.6 1.1 fusion.7
  15.7 0.9 select_reduce_fusion.2
  16.6 1.1 %pad_maximum_fusion.1 = bf16[32,16,832]{2,1,0:T(8,128)(2,1)S(1)} fusion(bf16[32,16,64]{2,1,0:T(8,128)(2,1)} %param.20, bf16[32,16,256]{2,1,0:T(8,128)(2,1)} %param.19, bf16[32,16,256]{2,1,0:T(8,128)(2,1)S(1)} %get-tuple-element.32, bf16[32,16,256]{2,1,0:T(8,128)(2,1)S(1)} %get-tuple-element.31), kind=kLoop, calls=%fused_computation.4 | loop fusion | flops 3407872 | bytes 1703936 | tf_op jit(solution)/shard_map/concatenate | solution.py:132
  17.7 0.1 select_reduce_fusion.1
  17.8 0.1 copy.36
  17.9 0.7 compare_reduce_fusion
  18.6 4.1 %all-to-all-done = s32[128,1,16]{2,1,0:T(1,128)S(1)} async-done(((s32[128,1,16]{2,1,0:T(1,128)}), s32[128,1,16]{2,1,0:T(1,128)S(1)}, u32[]{:S(2)}, u32[]{:S(2)}) %all-to-all-start) | async-done | bytes 8224 | tf_op jit(solution)/shard_map/all_to_all | solution.py:141
  22.7 0.0 copy-done.4
  22.7 2.6 %select_reduce_fusion = s32[128,16]{1,0:T(8,128)S(1)} fusion(s32[512]{0:T(512)S(1)} %copy-done.4, s32[128,16]{1,0:T(8,128)S(1)} %bitcast.18), kind=kLoop, calls=%fused_computation.2 | loop fusion | flops 3143680 | bytes 18432 | tf_op jit(solution)/shard_map/reduce_sum | solution.py:35
  25.4 0.1 fusion.3
  25.5 2.9 %gather_fusion = bf16[128,16,832]{2,1,0:T(8,128)(2,1)} fusion(bf16[32,16,832]{2,1,0:T(8,128)(2,1)S(1)} %pad_maximum_fusion.1, s32[1024]{0:T(1024)S(1)} %pad_clamp_fusion), kind=kCustom, calls=%fused_computation | custom fusion | bytes 6816256 | tf_op jit(solution)/shard_map/jit(_take)/gather | solution.py:147
  28.4 6.1 %all-to-all-start.1 = ((bf16[128,16,832]{2,1,0:T(8,128)(2,1)}), bf16[128,16,832]{2,1,0:T(8,128)(2,1)}, u32[]{:S(2)}, u32[]{:S(2)}) async-start(bf16[128,16,832]{2,1,0:T(8,128)(2,1)} %gather_fusion), calls=%async_computation.1 | async-start | bytes 7340032 | tf_op jit(solution)/shard_map/all_to_all | solution.py:148
  34.5 0.7 convert_select_fusion.1
  35.2 0.1 copy.37
  35.3 0.6 compare_reduce_fusion.1
  36.0 0.7 convert_select_fusion
  36.7 1.3 %scatter.9 = f32[512,128]{1,0:T(8,128)S(1)} dynamic-update-slice(f32[512,128]{1,0:T(8,128)S(1)} %scatter.6, f32[512,1]{1,0:T(8,128)S(1)} %copy.37, s32[]{:T(128)} %constant.94.clone.1, s32[]{:T(128)} %constant.95.clone.1) | dynamic-update-slice | bytes 4100 | tf_op jit(solution)/shard_map/scatter | solution.py:297
  38.0 0.0 copy-start.3
  38.0 1.8 %multiply_sine_fusion = (f32[512,32]{1,0:T(8,128)S(1)}, f32[512,32]{1,0:T(8,128)}, f32[512,32]{1,0:T(8,128)S(1)}) fusion(f32[512]{0:T(512)S(1)} %subtract_convert_fusion, f32[32]{0:T(128)S(1)} %negate_power_fusion), kind=kLoop, calls=%fused_computation.5 | loop fusion | flops 32768 | bytes 198784 | tf_op jit(solution)/shard_map/sin | solution.py:287
  39.8 0.0 copy-done.3
  39.8 1.7 %concatenate.15.aux_ref = f32[512,384]{1,0:T(8,128)S(1)} concatenate(f32[512,32]{1,0:T(8,128)S(1)} %get-tuple-element.35, f32[512,32]{1,0:T(8,128)S(1)} %get-tuple-element.35, f32[512,32]{1,0:T(8,128)S(1)} %get-tuple-element.35, f32[512,32]{1,0:T(8,128)S(1)} %get-tuple-element.35, f32[512,32]{1,0:T(8,128)} %get-tuple-element.34, f32[512,32]{1,0:T(8,128)S(1)} %get-tuple-element.33, ...), dimensions={1} | concatenate | bytes 1572864 | tf_op jit(solution)/shard_map/concatenate | solution.py:298
  41.5 0.0 copy-done
  41.5 0.0 copy-start.1
  41.5 0.0 copy-start.5
  41.5 3.0 %fusion.10 = f32[512,512]{1,0:T(8,128)S(1)} fusion(bf16[512,2048]{1,0:T(8,128)(2,1)} %x_ref.1, bf16[2048,512]{1,0:T(8,128)(2,1)S(1)} %copy-done), kind=kOutput, calls=%fused_computation.43 | convolution fusion | flops 1073741824 | bytes 5242880 | tf_op jit(solution)/shard_map/dot_general | solution.py:167
  44.5 0.0 copy-done.1
  44.5 0.0 copy-done.5
  44.5 1.2 %fusion.9 = f32[512,512]{1,0:T(8,128)S(1)} fusion(bf16[512,2048]{1,0:T(8,128)(2,1)S(1)} %copy-done.1, bf16[2048,512]{1,0:T(8,128)(2,1)S(1)} %copy-done.5), kind=kOutput, calls=%fused_computation.42 | convolution fusion | flops 1073741824 | bytes 5242880 | tf_op jit(solution)/shard_map/dot_general | solution.py:164
  45.8 6.9 %fusion.8 = f32[512,2048]{1,0:T(8,128)S(1)} fusion(bf16[512,2048]{1,0:T(8,128)(2,1)S(1)} %copy-done.1, bf16[2048,2048]{1,0:T(8,128)(2,1)} %param.15), kind=kOutput, calls=%fused_computation.41 | convolution fusion | flops 4294967296 | bytes 14680064 | tf_op jit(solution)/shard_map/dot_general | solution.py:161
  52.7 3.3 %pad_maximum_fusion.qkv_ref = f32[512,3072]{1,0:T(8,128)} fusion(f32[512,512]{1,0:T(8,128)S(1)} %fusion.10, f32[512,512]{1,0:T(8,128)S(1)} %fusion.9, f32[512,2048]{1,0:T(8,128)S(1)} %fusion.8), kind=kLoop, calls=%fused_computation.1 | loop fusion | flops 3145728 | bytes 12582912 | tf_op jit(solution)/shard_map/concatenate | solution.py:299
  56.0 24.3 %all-to-all-done.1 = bf16[128,16,832]{2,1,0:T(8,128)(2,1)} async-done(((bf16[128,16,832]{2,1,0:T(8,128)(2,1)}), bf16[128,16,832]{2,1,0:T(8,128)(2,1)}, u32[]{:S(2)}, u32[]{:S(2)}) %all-to-all-start.1) | async-done | bytes 3407904 | tf_op jit(solution)/shard_map/all_to_all | solution.py:148
  80.3 0.0 copy-start.2
  80.3 1.6 %copy-done.2 = bf16[512,2048]{1,0:T(8,128)(2,1)S(1)} copy-done((bf16[512,2048]{1,0:T(8,128)(2,1)S(1)}, bf16[512,2048]{1,0:T(8,128)(2,1)}, u32[]{:S(2)}) %copy-start.2) | copy-done | bytes 2097176
  81.9 25.8 %shard_map.103 = bf16[512,2048]{1,0:T(8,128)(2,1)} custom-call(f32[512,3072]{1,0:T(8,128)} %pad_maximum_fusion.qkv_ref, bf16[512,2048]{1,0:T(8,128)(2,1)S(1)} %copy-done.2, bf16[2048,832]{1,0:T(8,128)(2,1)} %bitcast.2.got_ref, f32[512,384]{1,0:T(8,128)S(1)} %concatenate.15.aux_ref), custom_call_target="tpu_custom_call" | custom-call | flops 3892314112 | bytes 14417920 | tf_op jit(solution)/shard_map/pallas_call | solution.py:303
  (6 shorter events, 0.1 us)
Async XLA Ops:
  0.0 41.5 %copy-start = (bf16[2048,512]{1,0:T(8,128)(2,1)S(1)}, bf16[2048,512]{1,0:T(8,128)(2,1)}, u32[]{:S(2)}) copy-start(bf16[2048,512]{1,0:T(8,128)(2,1)} %param.17) | copy-start | bytes 6291460
  0.0 22.7 %copy-start.4 = (s32[512]{0:T(512)S(1)}, s32[512]{0:T(512)}, u32[]{:S(2)}) copy-start(s32[512]{0:T(512)} %param.21) | copy-start | bytes 6148
  1.5 21.2 %all-to-all-start = ((s32[128,1,16]{2,1,0:T(1,128)}), s32[128,1,16]{2,1,0:T(1,128)S(1)}, u32[]{:S(2)}, u32[]{:S(2)}) async-start(s32[128,1,16]{2,1,0:T(1,128)} %broadcast_in_dim.59), calls=%async_computation | async-start | bytes 131072 | tf_op jit(solution)/shard_map/all_to_all | solution.py:141
  28.4 51.9 %all-to-all-start.1 = ((bf16[128,16,832]{2,1,0:T(8,128)(2,1)}), bf16[128,16,832]{2,1,0:T(8,128)(2,1)}, u32[]{:S(2)}, u32[]{:S(2)}) async-start(bf16[128,16,832]{2,1,0:T(8,128)(2,1)} %gather_fusion), calls=%async_computation.1 | async-start | bytes 7340032 | tf_op jit(solution)/shard_map/all_to_all | solution.py:148
  38.0 1.8 %copy-start.3 = (f32[512,128]{1,0:T(8,128)}, f32[512,128]{1,0:T(8,128)S(1)}, u32[]{:S(2)}) copy-start(f32[512,128]{1,0:T(8,128)S(1)} %scatter.9) | copy-start | bytes 786436
  41.5 3.0 %copy-start.1 = (bf16[512,2048]{1,0:T(8,128)(2,1)S(1)}, bf16[512,2048]{1,0:T(8,128)(2,1)}, u32[]{:S(2)}) copy-start(bf16[512,2048]{1,0:T(8,128)(2,1)} %x_ref.1) | copy-start | bytes 6291460
  41.5 3.0 %copy-start.5 = (bf16[2048,512]{1,0:T(8,128)(2,1)S(1)}, bf16[2048,512]{1,0:T(8,128)(2,1)}, u32[]{:S(2)}) copy-start(bf16[2048,512]{1,0:T(8,128)(2,1)} %param.16) | copy-start | bytes 6291460
  80.3 1.6 %copy-start.2 = (bf16[512,2048]{1,0:T(8,128)(2,1)S(1)}, bf16[512,2048]{1,0:T(8,128)(2,1)}, u32[]{:S(2)}) copy-start(bf16[512,2048]{1,0:T(8,128)(2,1)} %x_ref.1) | copy-start | bytes 6291460

commit v13 on v12

--- a/solution.py
+++ b/solution.py
@@ -138,12 +138,18 @@
         ],
         axis=2,
     )
-    all_lists = lax.all_to_all(
-        jnp.broadcast_to(adapter_per_request, (device_total, request_count)), axes, 0, 0, tiled=True
-    )
-    all_slots = table_lookup(adapter_panel_slot, all_lists)
-    mine = all_slots // ADP_DEV == my_store
-    local_pick = jnp.sum(jnp.where(mine, all_slots % ADP_DEV, 0), axis=1)
+    my_slots = table_lookup(adapter_panel_slot, adapter_per_request[0])
+    slot_for_owner = jnp.sum(
+        jnp.where(
+            my_slots[None, :] // ADP_DEV == jnp.arange(store_count, dtype=jnp.int32)[:, None],
+            my_slots[None, :] % ADP_DEV,
+            0,
+        ),
+        axis=1,
+    )
+    local_pick = lax.all_to_all(
+        jnp.tile(slot_for_owner, serve_count).reshape(device_total, 1), axes, 0, 0, tiled=True
+    ).reshape(device_total)
     send = jnp.take(panel_table, local_pick, axis=0, mode="clip")
     got = lax.all_to_all(send, axes, 0, 0, tiled=True)
 

time: 108 us -> 107 us (level)
    reduce_sum x2 -> x1, other arithmetic: 3.51 us -> 1.02 us  [table_lookup(): return jnp.sum(jnp.where(wanted[..., None] == entries, table, 0), axis=-1)]
    all_to_all x0 -> x1, other arithmetic: none -> 2.35 us  [local(): lax.all_to_all(jnp.tile(slot_for_owner, serve_count).reshape(device_total...]
    broadcast_in_dim x1 -> x0, local copies, waits for them, and re-layouts: 1.48 us -> none  [local(): jnp.broadcast_to(adapter_per_request, (device_total, request_count))]
  transfers between devices with their start and end apart: 2 -> 2, of which waited for: 2 -> 2; matrix products, arithmetic and copies ran while one was open for 25% -> 24% of each run, Pallas kernels for 0% -> 0%
where the time goes in v13:
time: 107 us
  waiting for transfers between devices  29.3 us (27%)
  Pallas kernels  25.8 us (24%)
  starting transfers between devices  16.7 us (16%)
  other arithmetic  13.5 us (13%)
  matrix products  11.1 us (10%)
  local copies, waits for them, and re-layouts  10.3 us (10%)
    pallas_call x1, Pallas kernels, fused_attention(): pl.pallas_call(_attend_kernel, out_shape=jax.ShapeDtypeStruct((rows, HEAD...  25.8 us
    all_to_all x1, waiting for transfers between devices, local(): got = lax.all_to_all(send, axes, 0, 0, tiled=True)  24.4 us
    all_to_all x1, starting transfers between devices, local(): lax.all_to_all(jnp.tile(slot_for_owner, serve_count).reshape(device_total...  11.5 us
    dot_general x1, matrix products, local(): jnp.dot(normalized_hidden_states, query_weight_matrix, preferred_element_...  6.89 us
    all_to_all x1, starting transfers between devices, local(): got = lax.all_to_all(send, axes, 0, 0, tiled=True)  5.25 us
    all_to_all x1, waiting for transfers between devices, local(): lax.all_to_all(jnp.tile(slot_for_owner, serve_count).reshape(device_total...  4.95 us
    concatenate x1, other arithmetic, fused_attention(): qkv = jnp.concatenate([q_base, k_base, v_base], axis=1)  3.35 us
    dot_general x1, matrix products, local(): jnp.dot(normalized_hidden_states, value_weight_matrix, preferred_element_...  2.98 us
  transfers between devices with their start and end apart: 2, of which 2 were waited for; matrix products, arithmetic and copies ran while one was open for 24% of the time, Pallas kernels for 0%

profile of v13, /device:TPU:1, one launch (start us, length us, event | category | flops | bytes accessed | tf_op | source)
XLA Modules:
  0.0 106.9 jit_solution(15514969503393126174)
XLA Ops:
  0.0 0.0 copy-start
  0.0 1.0 select_reduce_fusion.2
  1.0 0.1 select_reduce_fusion.3
  1.2 0.8 all_to_all.15
  1.9 11.5 %all-to-all-start = ((s32[128,1,1]{2,1,0:T(1,128)}), s32[128,1,1]{2,1,0:T(1,128)S(1)}, u32[]{:S(2)}, u32[]{:S(2)}) async-start(s32[128,1,1]{2,1,0:T(1,128)} %all_to_all.15), calls=%async_computation | async-start | bytes 131072 | tf_op jit(solution)/shard_map/all_to_all | solution.py:150
  13.4 0.7 copy.40
  14.2 0.1 reduce.15
  14.3 0.1 convert_reduce_fusion
  14.4 0.7 fusion.1
  15.1 1.1 %fusion.2 = (bf16[32,16,256]{2,1,0:T(8,128)(2,1)S(1)}, bf16[32,16,256]{2,1,0:T(8,128)(2,1)S(1)}) fusion(bf16[32,32,256]{2,1,0:T(8,128)(2,1)} %param.18), kind=kLoop, calls=%fused_computation.30 | loop fusion | bytes 1048576 | tf_op jit(solution)/shard_map/slice | solution.py:134
  16.1 1.1 %pad_maximum_fusion.1 = bf16[32,16,832]{2,1,0:T(8,128)(2,1)S(1)} fusion(bf16[32,16,64]{2,1,0:T(8,128)(2,1)} %param.20, bf16[32,16,256]{2,1,0:T(8,128)(2,1)} %param.19, bf16[32,16,256]{2,1,0:T(8,128)(2,1)S(1)} %get-tuple-element.32, bf16[32,16,256]{2,1,0:T(8,128)(2,1)S(1)} %get-tuple-element.31), kind=kLoop, calls=%fused_computation.2 | loop fusion | flops 3407872 | bytes 1703936 | tf_op jit(solution)/shard_map/concatenate | solution.py:132
  17.2 0.1 select_reduce_fusion
  17.3 0.1 copy.42
  17.5 0.7 compare_reduce_fusion
  18.2 4.9 %all-to-all-done = s32[128,1,1]{2,1,0:T(1,128)S(1)} async-done(((s32[128,1,1]{2,1,0:T(1,128)}), s32[128,1,1]{2,1,0:T(1,128)S(1)}, u32[]{:S(2)}, u32[]{:S(2)}) %all-to-all-start) | async-done | bytes 544 | tf_op jit(solution)/shard_map/all_to_all | solution.py:150
  23.2 2.3 %reduce.14 = s32[128]{0:T(128)S(1)} reduce(s32[128,1,1]{2,1,0:T(1,128)S(1)} %all-to-all-done, s32[]{:T(128)} %constant.91.clone.1), dimensions={1,2}, to_apply=%all_to_all.12.reduce_sub_computation | reduce | bytes 1028 | tf_op jit(solution)/shard_map/all_to_all | solution.py:150
  25.5 2.9 %gather_fusion = bf16[128,16,832]{2,1,0:T(8,128)(2,1)} fusion(bf16[32,16,832]{2,1,0:T(8,128)(2,1)S(1)} %pad_maximum_fusion.1, s32[1024]{0:T(1024)S(1)} %pad_clamp_fusion), kind=kCustom, calls=%fused_computation | custom fusion | bytes 6816256 | tf_op jit(solution)/shard_map/jit(_take)/gather | solution.py:153
  28.4 5.2 %all-to-all-start.1 = ((bf16[128,16,832]{2,1,0:T(8,128)(2,1)}), bf16[128,16,832]{2,1,0:T(8,128)(2,1)}, u32[]{:S(2)}, u32[]{:S(2)}) async-start(bf16[128,16,832]{2,1,0:T(8,128)(2,1)} %gather_fusion), calls=%async_computation.1 | async-start | bytes 7340032 | tf_op jit(solution)/shard_map/all_to_all | solution.py:154
  33.7 0.7 convert_select_fusion.1
  34.4 0.1 copy.43
  34.5 0.6 compare_reduce_fusion.1
  35.1 0.7 convert_select_fusion
  35.9 1.3 %scatter.9 = f32[512,128]{1,0:T(8,128)S(1)} dynamic-update-slice(f32[512,128]{1,0:T(8,128)S(1)} %scatter.6, f32[512,1]{1,0:T(8,128)S(1)} %copy.43, s32[]{:T(128)} %constant.91.clone.1, s32[]{:T(128)} %constant.92.clone.1) | dynamic-update-slice | bytes 4100 | tf_op jit(solution)/shard_map/scatter | solution.py:303
  37.2 0.0 copy-start.3
  37.2 1.8 %multiply_sine_fusion = (f32[512,32]{1,0:T(8,128)S(1)}, f32[512,32]{1,0:T(8,128)}, f32[512,32]{1,0:T(8,128)S(1)}) fusion(f32[512]{0:T(512)S(1)} %subtract_convert_fusion, f32[32]{0:T(128)S(1)} %negate_power_fusion), kind=kLoop, calls=%fused_computation.3 | loop fusion | flops 32768 | bytes 198784 | tf_op jit(solution)/shard_map/sin | solution.py:293
  39.0 0.0 copy-done.3
  39.0 1.7 %concatenate.15.aux_ref = f32[512,384]{1,0:T(8,128)S(1)} concatenate(f32[512,32]{1,0:T(8,128)S(1)} %get-tuple-element.35, f32[512,32]{1,0:T(8,128)S(1)} %get-tuple-element.35, f32[512,32]{1,0:T(8,128)S(1)} %get-tuple-element.35, f32[512,32]{1,0:T(8,128)S(1)} %get-tuple-element.35, f32[512,32]{1,0:T(8,128)} %get-tuple-element.34, f32[512,32]{1,0:T(8,128)S(1)} %get-tuple-element.33, ...), dimensions={1} | concatenate | bytes 1572864 | tf_op jit(solution)/shard_map/concatenate | solution.py:304
  40.7 0.0 copy-done
  40.7 0.0 copy-start.1
  40.7 0.0 copy-start.4
  40.7 3.0 %fusion.5 = f32[512,512]{1,0:T(8,128)S(1)} fusion(bf16[512,2048]{1,0:T(8,128)(2,1)} %x_ref.1, bf16[2048,512]{1,0:T(8,128)(2,1)S(1)} %copy-done), kind=kOutput, calls=%fused_computation.33 | convolution fusion | flops 1073741824 | bytes 5242880 | tf_op jit(solution)/shard_map/dot_general | solution.py:173
  43.7 0.0 copy-done.1
  43.7 0.0 copy-done.4
  43.7 1.2 %fusion.4 = f32[512,512]{1,0:T(8,128)S(1)} fusion(bf16[512,2048]{1,0:T(8,128)(2,1)S(1)} %copy-done.1, bf16[2048,512]{1,0:T(8,128)(2,1)S(1)} %copy-done.4), kind=kOutput, calls=%fused_computation.32 | convolution fusion | flops 1073741824 | bytes 5242880 | tf_op jit(solution)/shard_map/dot_general | solution.py:170
  44.9 6.9 %fusion.3 = f32[512,2048]{1,0:T(8,128)S(1)} fusion(bf16[512,2048]{1,0:T(8,128)(2,1)S(1)} %copy-done.1, bf16[2048,2048]{1,0:T(8,128)(2,1)} %param.15), kind=kOutput, calls=%fused_computation.31 | convolution fusion | flops 4294967296 | bytes 14680064 | tf_op jit(solution)/shard_map/dot_general | solution.py:167
  51.8 3.3 %pad_maximum_fusion.qkv_ref = f32[512,3072]{1,0:T(8,128)} fusion(f32[512,512]{1,0:T(8,128)S(1)} %fusion.5, f32[512,512]{1,0:T(8,128)S(1)} %fusion.4, f32[512,2048]{1,0:T(8,128)S(1)} %fusion.3), kind=kLoop, calls=%fused_computation.1 | loop fusion | flops 3145728 | bytes 12582912 | tf_op jit(solution)/shard_map/concatenate | solution.py:305
  55.2 24.4 %all-to-all-done.1 = bf16[128,16,832]{2,1,0:T(8,128)(2,1)} async-done(((bf16[128,16,832]{2,1,0:T(8,128)(2,1)}), bf16[128,16,832]{2,1,0:T(8,128)(2,1)}, u32[]{:S(2)}, u32[]{:S(2)}) %all-to-all-start.1) | async-done | bytes 3407904 | tf_op jit(solution)/shard_map/all_to_all | solution.py:154
  79.6 0.0 copy-start.2
  79.6 1.6 %copy-done.2 = bf16[512,2048]{1,0:T(8,128)(2,1)S(1)} copy-done((bf16[512,2048]{1,0:T(8,128)(2,1)S(1)}, bf16[512,2048]{1,0:T(8,128)(2,1)}, u32[]{:S(2)}) %copy-start.2) | copy-done | bytes 2097176
  81.2 25.8 %shard_map.100 = bf16[512,2048]{1,0:T(8,128)(2,1)} custom-call(f32[512,3072]{1,0:T(8,128)} %pad_maximum_fusion.qkv_ref, bf16[512,2048]{1,0:T(8,128)(2,1)S(1)} %copy-done.2, bf16[2048,832]{1,0:T(8,128)(2,1)} %bitcast.1.got_ref, f32[512,384]{1,0:T(8,128)S(1)} %concatenate.15.aux_ref), custom_call_target="tpu_custom_call" | custom-call | flops 3892314112 | bytes 14417920 | tf_op jit(solution)/shard_map/pallas_call | solution.py:309
  (7 shorter events, 0.1 us)
Async XLA Ops:
  0.0 40.7 %copy-start = (bf16[2048,512]{1,0:T(8,128)(2,1)S(1)}, bf16[2048,512]{1,0:T(8,128)(2,1)}, u32[]{:S(2)}) copy-start(bf16[2048,512]{1,0:T(8,128)(2,1)} %param.17) | copy-start | bytes 6291460
  1.9 21.2 %all-to-all-start = ((s32[128,1,1]{2,1,0:T(1,128)}), s32[128,1,1]{2,1,0:T(1,128)S(1)}, u32[]{:S(2)}, u32[]{:S(2)}) async-start(s32[128,1,1]{2,1,0:T(1,128)} %all_to_all.15), calls=%async_computation | async-start | bytes 131072 | tf_op jit(solution)/shard_map/all_to_all | solution.py:150
  28.4 51.2 %all-to-all-start.1 = ((bf16[128,16,832]{2,1,0:T(8,128)(2,1)}), bf16[128,16,832]{2,1,0:T(8,128)(2,1)}, u32[]{:S(2)}, u32[]{:S(2)}) async-start(bf16[128,16,832]{2,1,0:T(8,128)(2,1)} %gather_fusion), calls=%async_computation.1 | async-start | bytes 7340032 | tf_op jit(solution)/shard_map/all_to_all | solution.py:154
  37.2 1.8 %copy-start.3 = (f32[512,128]{1,0:T(8,128)}, f32[512,128]{1,0:T(8,128)S(1)}, u32[]{:S(2)}) copy-start(f32[512,128]{1,0:T(8,128)S(1)} %scatter.9) | copy-start | bytes 786436
  40.7 3.0 %copy-start.1 = (bf16[512,2048]{1,0:T(8,128)(2,1)S(1)}, bf16[512,2048]{1,0:T(8,128)(2,1)}, u32[]{:S(2)}) copy-start(bf16[512,2048]{1,0:T(8,128)(2,1)} %x_ref.1) | copy-start | bytes 6291460
  40.7 3.0 %copy-start.4 = (bf16[2048,512]{1,0:T(8,128)(2,1)S(1)}, bf16[2048,512]{1,0:T(8,128)(2,1)}, u32[]{:S(2)}) copy-start(bf16[2048,512]{1,0:T(8,128)(2,1)} %param.16) | copy-start | bytes 6291460
  79.6 1.6 %copy-start.2 = (bf16[512,2048]{1,0:T(8,128)(2,1)S(1)}, bf16[512,2048]{1,0:T(8,128)(2,1)}, u32[]{:S(2)}) copy-start(bf16[512,2048]{1,0:T(8,128)(2,1)} %x_ref.1) | copy-start | bytes 6291460

commit v14 on v13

--- a/solution.py
+++ b/solution.py
@@ -183,7 +183,7 @@
     return jnp.concatenate([x[:, 32:64], x[:, 0:32], x[:, 96:128], x[:, 64:96]], axis=1)
 
 
-def _attend_kernel(qkv_ref, x_ref, got_ref, aux_ref, out_ref, q_s, kd_s, vd_s, dq_ref, dv_ref):
+def _attend_kernel(qkv_ref, x_ref, got_ref, aux_ref, out_ref, q_s, kd_s, vd_s, dq_ref, dv_ref, dt_s):
     q_width = dq_ref.shape[1]
     kv_width = dv_ref.shape[1]
     qb_ref = qkv_ref.at[:, 0:q_width]
@@ -202,17 +202,19 @@
 
     @pl.when(b == 0)
     def _():
+        for sl in range(slices):
+            panel = got_ref[sl * cols:(sl + 1) * cols, 0:2 * cols].astype(jnp.float32)
+            dt_s[sl, :, 0:cols] = jnp.transpose(panel[:, 0:cols]).astype(jnp.bfloat16)
+            dt_s[sl, :, cols:2 * cols] = jnp.transpose(panel[:, cols:2 * cols]).astype(jnp.bfloat16)
         kd_s[:, :, blk:2 * blk] = jnp.zeros((kd_s.shape[0], kd_s.shape[1], blk), kd_s.dtype)
         vd_s[:, blk:2 * blk, :] = jnp.zeros((vd_s.shape[0], blk, vd_s.shape[2]), vd_s.dtype)
 
-    low_q = jnp.zeros((blk, cols), jnp.float32)
-    low_v = jnp.zeros((blk, cols), jnp.float32)
+    low = jnp.zeros((blk, 2 * cols), jnp.float32)
     nt = (((1,), (1,)), ((), ()))
     for sl in range(slices):
-        xs = x_ref[:, sl * cols:(sl + 1) * cols]
-        panel = got_ref[sl * cols:(sl + 1) * cols, 0:2 * cols]
-        low_q += lax.dot_general(xs, panel[:, 0:cols], nt, preferred_element_type=jnp.float32)
-        low_v += lax.dot_general(xs, panel[:, cols:2 * cols], nt, preferred_element_type=jnp.float32)
+        low += jnp.dot(x_ref[:, sl * cols:(sl + 1) * cols], dt_s[sl], preferred_element_type=jnp.float32)
+    low_q = low[:, 0:cols]
+    low_v = low[:, cols:2 * cols]
     mine = owner_lane == aux_ref[:, 257:258].astype(jnp.int32)
     low_q = jnp.where(mine, low_q.astype(jnp.bfloat16), jnp.zeros((), jnp.bfloat16))
     low_v = jnp.where(mine, low_v.astype(jnp.bfloat16), jnp.zeros((), jnp.bfloat16))
@@ -323,6 +325,7 @@
             pltpu.VMEM((KV_HEADS, rows, 256), jnp.bfloat16),
             pltpu.VMEM((blk, HEADS * HEAD_DIM), jnp.bfloat16),
             pltpu.VMEM((blk, KV_HEADS * HEAD_DIM), jnp.bfloat16),
+            pltpu.VMEM((states.shape[1] // 256, 256, 512), jnp.bfloat16),
         ],
         compiler_params=pltpu.CompilerParams(
             dimension_semantics=("arbitrary",), vmem_limit_bytes=48 * 1024 * 1024

time: 107 us -> 106 us (level)
  transfers between devices with their start and end apart: 2 -> 2, of which waited for: 2 -> 2; matrix products, arithmetic and copies ran while one was open for 24% -> 25% of each run, Pallas kernels for 0% -> 0%
where the time goes in v14:
time: 106 us
  waiting for transfers between devices  29.3 us (28%)
  Pallas kernels  24.9 us (23%)
  starting transfers between devices  16.7 us (16%)
  other arithmetic  13.5 us (13%)
  matrix products  11.1 us (10%)
  local copies, waits for them, and re-layouts  10.3 us (10%)
    pallas_call x1, Pallas kernels, fused_attention(): pl.pallas_call(_attend_kernel, out_shape=jax.ShapeDtypeStruct((rows, HEAD...  24.9 us
    all_to_all x1, waiting for transfers between devices, local(): got = lax.all_to_all(send, axes, 0, 0, tiled=True)  24.4 us
    all_to_all x1, starting transfers between devices, local(): lax.all_to_all(jnp.tile(slot_for_owner, serve_count).reshape(device_total...  11.5 us
    dot_general x1, matrix products, local(): jnp.dot(normalized_hidden_states, query_weight_matrix, preferred_element_...  6.89 us
    all_to_all x1, starting transfers between devices, local(): got = lax.all_to_all(send, axes, 0, 0, tiled=True)  5.25 us
    all_to_all x1, waiting for transfers between devices, local(): lax.all_to_all(jnp.tile(slot_for_owner, serve_count).reshape(device_total...  4.95 us
    concatenate x1, other arithmetic, fused_attention(): qkv = jnp.concatenate([q_base, k_base, v_base], axis=1)  3.35 us
    dot_general x1, matrix products, local(): jnp.dot(normalized_hidden_states, value_weight_matrix, preferred_element_...  2.98 us
  transfers between devices with their start and end apart: 2, of which 2 were waited for; matrix products, arithmetic and copies ran while one was open for 25% of the time, Pallas kernels for 0%

profile of v14, /device:TPU:1, one launch (start us, length us, event | category | flops | bytes accessed | tf_op | source)
XLA Modules:
  0.0 106.1 jit_solution(2290159331853598296)
XLA Ops:
  0.0 0.0 copy-start
  0.0 1.0 select_reduce_fusion.2
  1.0 0.1 select_reduce_fusion.3
  1.2 0.8 all_to_all.15
  1.9 11.5 %all-to-all-start = ((s32[128,1,1]{2,1,0:T(1,128)}), s32[128,1,1]{2,1,0:T(1,128)S(1)}, u32[]{:S(2)}, u32[]{:S(2)}) async-start(s32[128,1,1]{2,1,0:T(1,128)} %all_to_all.15), calls=%async_computation | async-start | bytes 131072 | tf_op jit(solution)/shard_map/all_to_all | solution.py:150
  13.4 0.7 copy.40
  14.2 0.1 reduce.15
  14.3 0.1 convert_reduce_fusion
  14.4 0.7 fusion.1
  15.1 1.1 %fusion.2 = (bf16[32,16,256]{2,1,0:T(8,128)(2,1)S(1)}, bf16[32,16,256]{2,1,0:T(8,128)(2,1)S(1)}) fusion(bf16[32,32,256]{2,1,0:T(8,128)(2,1)} %param.18), kind=kLoop, calls=%fused_computation.30 | loop fusion | bytes 1048576 | tf_op jit(solution)/shard_map/slice | solution.py:134
  16.1 1.1 %pad_maximum_fusion.1 = bf16[32,16,832]{2,1,0:T(8,128)(2,1)S(1)} fusion(bf16[32,16,64]{2,1,0:T(8,128)(2,1)} %param.20, bf16[32,16,256]{2,1,0:T(8,128)(2,1)} %param.19, bf16[32,16,256]{2,1,0:T(8,128)(2,1)S(1)} %get-tuple-element.32, bf16[32,16,256]{2,1,0:T(8,128)(2,1)S(1)} %get-tuple-element.31), kind=kLoop, calls=%fused_computation.2 | loop fusion | flops 3407872 | bytes 1703936 | tf_op jit(solution)/shard_map/concatenate | solution.py:132
  17.2 0.1 select_reduce_fusion
  17.3 0.1 copy.42
  17.5 0.7 compare_reduce_fusion
  18.2 4.9 %all-to-all-done = s32[128,1,1]{2,1,0:T(1,128)S(1)} async-done(((s32[128,1,1]{2,1,0:T(1,128)}), s32[128,1,1]{2,1,0:T(1,128)S(1)}, u32[]{:S(2)}, u32[]{:S(2)}) %all-to-all-start) | async-done | bytes 544 | tf_op jit(solution)/shard_map/all_to_all | solution.py:150
  23.2 2.3 %reduce.14 = s32[128]{0:T(128)S(1)} reduce(s32[128,1,1]{2,1,0:T(1,128)S(1)} %all-to-all-done, s32[]{:T(128)} %constant.91.clone.1), dimensions={1,2}, to_apply=%all_to_all.12.reduce_sub_computation | reduce | bytes 1028 | tf_op jit(solution)/shard_map/all_to_all | solution.py:150
  25.5 2.9 %gather_fusion = bf16[128,16,832]{2,1,0:T(8,128)(2,1)} fusion(bf16[32,16,832]{2,1,0:T(8,128)(2,1)S(1)} %pad_maximum_fusion.1, s32[1024]{0:T(1024)S(1)} %pad_clamp_fusion), kind=kCustom, calls=%fused_computation | custom fusion | bytes 6816256 | tf_op jit(solution)/shard_map/jit(_take)/gather | solution.py:153
  28.4 5.2 %all-to-all-start.1 = ((bf16[128,16,832]{2,1,0:T(8,128)(2,1)}), bf16[128,16,832]{2,1,0:T(8,128)(2,1)}, u32[]{:S(2)}, u32[]{:S(2)}) async-start(bf16[128,16,832]{2,1,0:T(8,128)(2,1)} %gather_fusion), calls=%async_computation.1 | async-start | bytes 7340032 | tf_op jit(solution)/shard_map/all_to_all | solution.py:154
  33.7 0.7 convert_select_fusion.1
  34.4 0.1 copy.43
  34.5 0.6 compare_reduce_fusion.1
  35.1 0.7 convert_select_fusion
  35.9 1.3 %scatter.9 = f32[512,128]{1,0:T(8,128)S(1)} dynamic-update-slice(f32[512,128]{1,0:T(8,128)S(1)} %scatter.6, f32[512,1]{1,0:T(8,128)S(1)} %copy.43, s32[]{:T(128)} %constant.91.clone.1, s32[]{:T(128)} %constant.92.clone.1) | dynamic-update-slice | bytes 4100 | tf_op jit(solution)/shard_map/scatter | solution.py:305
  37.2 0.0 copy-start.3
  37.2 1.8 %multiply_sine_fusion = (f32[512,32]{1,0:T(8,128)S(1)}, f32[512,32]{1,0:T(8,128)}, f32[512,32]{1,0:T(8,128)S(1)}) fusion(f32[512]{0:T(512)S(1)} %subtract_convert_fusion, f32[32]{0:T(128)S(1)} %negate_power_fusion), kind=kLoop, calls=%fused_computation.3 | loop fusion | flops 32768 | bytes 198784 | tf_op jit(solution)/shard_map/sin | solution.py:295
  39.0 0.0 copy-done.3
  39.0 1.7 %concatenate.15.aux_ref = f32[512,384]{1,0:T(8,128)S(1)} concatenate(f32[512,32]{1,0:T(8,128)S(1)} %get-tuple-element.35, f32[512,32]{1,0:T(8,128)S(1)} %get-tuple-element.35, f32[512,32]{1,0:T(8,128)S(1)} %get-tuple-element.35, f32[512,32]{1,0:T(8,128)S(1)} %get-tuple-element.35, f32[512,32]{1,0:T(8,128)} %get-tuple-element.34, f32[512,32]{1,0:T(8,128)S(1)} %get-tuple-element.33, ...), dimensions={1} | concatenate | bytes 1572864 | tf_op jit(solution)/shard_map/concatenate | solution.py:306
  40.7 0.0 copy-done
  40.7 0.0 copy-start.1
  40.7 0.0 copy-start.4
  40.7 3.0 %fusion.5 = f32[512,512]{1,0:T(8,128)S(1)} fusion(bf16[512,2048]{1,0:T(8,128)(2,1)} %x_ref.1, bf16[2048,512]{1,0:T(8,128)(2,1)S(1)} %copy-done), kind=kOutput, calls=%fused_computation.33 | convolution fusion | flops 1073741824 | bytes 5242880 | tf_op jit(solution)/shard_map/dot_general | solution.py:173
  43.7 0.0 copy-done.1
  43.7 0.0 copy-done.4
  43.7 1.2 %fusion.4 = f32[512,512]{1,0:T(8,128)S(1)} fusion(bf16[512,2048]{1,0:T(8,128)(2,1)S(1)} %copy-done.1, bf16[2048,512]{1,0:T(8,128)(2,1)S(1)} %copy-done.4), kind=kOutput, calls=%fused_computation.32 | convolution fusion | flops 1073741824 | bytes 5242880 | tf_op jit(solution)/shard_map/dot_general | solution.py:170
  44.9 6.9 %fusion.3 = f32[512,2048]{1,0:T(8,128)S(1)} fusion(bf16[512,2048]{1,0:T(8,128)(2,1)S(1)} %copy-done.1, bf16[2048,2048]{1,0:T(8,128)(2,1)} %param.15), kind=kOutput, calls=%fused_computation.31 | convolution fusion | flops 4294967296 | bytes 14680064 | tf_op jit(solution)/shard_map/dot_general | solution.py:167
  51.8 3.3 %pad_maximum_fusion.qkv_ref = f32[512,3072]{1,0:T(8,128)} fusion(f32[512,512]{1,0:T(8,128)S(1)} %fusion.5, f32[512,512]{1,0:T(8,128)S(1)} %fusion.4, f32[512,2048]{1,0:T(8,128)S(1)} %fusion.3), kind=kLoop, calls=%fused_computation.1 | loop fusion | flops 3145728 | bytes 12582912 | tf_op jit(solution)/shard_map/concatenate | solution.py:307
  55.2 24.4 %all-to-all-done.1 = bf16[128,16,832]{2,1,0:T(8,128)(2,1)} async-done(((bf16[128,16,832]{2,1,0:T(8,128)(2,1)}), bf16[128,16,832]{2,1,0:T(8,128)(2,1)}, u32[]{:S(2)}, u32[]{:S(2)}) %all-to-all-start.1) | async-done | bytes 3407904 | tf_op jit(solution)/shard_map/all_to_all | solution.py:154
  79.6 0.0 copy-start.2
  79.6 1.6 %copy-done.2 = bf16[512,2048]{1,0:T(8,128)(2,1)S(1)} copy-done((bf16[512,2048]{1,0:T(8,128)(2,1)S(1)}, bf16[512,2048]{1,0:T(8,128)(2,1)}, u32[]{:S(2)}) %copy-start.2) | copy-done | bytes 2097176
  81.2 24.9 %shard_map.100 = bf16[512,2048]{1,0:T(8,128)(2,1)} custom-call(f32[512,3072]{1,0:T(8,128)} %pad_maximum_fusion.qkv_ref, bf16[512,2048]{1,0:T(8,128)(2,1)S(1)} %copy-done.2, bf16[2048,832]{1,0:T(8,128)(2,1)} %bitcast.1.got_ref, f32[512,384]{1,0:T(8,128)S(1)} %concatenate.15.aux_ref), custom_call_target="tpu_custom_call" | custom-call | flops 3892314112 | bytes 14417920 | tf_op jit(solution)/shard_map/pallas_call | solution.py:311
  (7 shorter events, 0.1 us)
Async XLA Ops:
  0.0 40.7 %copy-start = (bf16[2048,512]{1,0:T(8,128)(2,1)S(1)}, bf16[2048,512]{1,0:T(8,128)(2,1)}, u32[]{:S(2)}) copy-start(bf16[2048,512]{1,0:T(8,128)(2,1)} %param.17) | copy-start | bytes 6291460
  1.9 21.2 %all-to-all-start = ((s32[128,1,1]{2,1,0:T(1,128)}), s32[128,1,1]{2,1,0:T(1,128)S(1)}, u32[]{:S(2)}, u32[]{:S(2)}) async-start(s32[128,1,1]{2,1,0:T(1,128)} %all_to_all.15), calls=%async_computation | async-start | bytes 131072 | tf_op jit(solution)/shard_map/all_to_all | solution.py:150
  28.4 51.2 %all-to-all-start.1 = ((bf16[128,16,832]{2,1,0:T(8,128)(2,1)}), bf16[128,16,832]{2,1,0:T(8,128)(2,1)}, u32[]{:S(2)}, u32[]{:S(2)}) async-start(bf16[128,16,832]{2,1,0:T(8,128)(2,1)} %gather_fusion), calls=%async_computation.1 | async-start | bytes 7340032 | tf_op jit(solution)/shard_map/all_to_all | solution.py:154
  37.2 1.8 %copy-start.3 = (f32[512,128]{1,0:T(8,128)}, f32[512,128]{1,0:T(8,128)S(1)}, u32[]{:S(2)}) copy-start(f32[512,128]{1,0:T(8,128)S(1)} %scatter.9) | copy-start | bytes 786436
  40.7 3.0 %copy-start.1 = (bf16[512,2048]{1,0:T(8,128)(2,1)S(1)}, bf16[512,2048]{1,0:T(8,128)(2,1)}, u32[]{:S(2)}) copy-start(bf16[512,2048]{1,0:T(8,128)(2,1)} %x_ref.1) | copy-start | bytes 6291460
  40.7 3.0 %copy-start.4 = (bf16[2048,512]{1,0:T(8,128)(2,1)S(1)}, bf16[2048,512]{1,0:T(8,128)(2,1)}, u32[]{:S(2)}) copy-start(bf16[2048,512]{1,0:T(8,128)(2,1)} %param.16) | copy-start | bytes 6291460
  79.6 1.6 %copy-start.2 = (bf16[512,2048]{1,0:T(8,128)(2,1)S(1)}, bf16[512,2048]{1,0:T(8,128)(2,1)}, u32[]{:S(2)}) copy-start(bf16[512,2048]{1,0:T(8,128)(2,1)} %x_ref.1) | copy-start | bytes 6291460

commit v15 on v14

--- a/solution.py
+++ b/solution.py
@@ -183,12 +183,13 @@
     return jnp.concatenate([x[:, 32:64], x[:, 0:32], x[:, 96:128], x[:, 64:96]], axis=1)
 
 
-def _attend_kernel(qkv_ref, x_ref, got_ref, aux_ref, out_ref, q_s, kd_s, vd_s, dq_ref, dv_ref, dt_s):
+def _attend_kernel(qkv_ref, got_ref, aux_ref, out_ref, q_s, kd_s, vd_s, dq_ref, dv_ref, dt_s):
     q_width = dq_ref.shape[1]
     kv_width = dv_ref.shape[1]
     qb_ref = qkv_ref.at[:, 0:q_width]
     kb_ref = qkv_ref.at[:, q_width:q_width + kv_width]
     vb_ref = qkv_ref.at[:, q_width + kv_width:q_width + 2 * kv_width]
+    x_ref = qkv_ref.at[:, q_width + 2 * kv_width:]
     blk = qb_ref.shape[0]
     rows = kd_s.shape[2]
     b = pl.program_id(0)
@@ -212,7 +213,8 @@
     low = jnp.zeros((blk, 2 * cols), jnp.float32)
     nt = (((1,), (1,)), ((), ()))
     for sl in range(slices):
-        low += jnp.dot(x_ref[:, sl * cols:(sl + 1) * cols], dt_s[sl], preferred_element_type=jnp.float32)
+        low += jnp.dot(x_ref[:, sl * cols:(sl + 1) * cols].astype(jnp.bfloat16), dt_s[sl],
+                       preferred_element_type=jnp.float32)
     low_q = low[:, 0:cols]
     low_v = low[:, cols:2 * cols]
     mine = owner_lane == aux_ref[:, 257:258].astype(jnp.int32)
@@ -304,7 +306,7 @@
     side = jnp.zeros((rows, 128), jnp.float32)
     side = side.at[:, 0].set(positions.astype(jnp.float32)).at[:, 1].set(owner_token.astype(jnp.float32))
     aux = jnp.concatenate([cos_t, sin_t, side], axis=1)
-    qkv = jnp.concatenate([q_base, k_base, v_base], axis=1)
+    qkv = jnp.concatenate([q_base, k_base, v_base, states.astype(jnp.float32)], axis=1)
     flops = 2 * rows * 256 * 64 * 2 * HEADS * 2 + 2 * rows * 256 * (2 * 2048 + 2048 + 512)
     blk = 128
     row_block = lambda width: pl.BlockSpec((blk, width), lambda b: (b, 0))
@@ -314,7 +316,6 @@
         grid=(rows // blk,),
         in_specs=[
             row_block(qkv.shape[1]),
-            row_block(states.shape[1]),
             pl.BlockSpec(got.shape, lambda b: (0, 0)),
             row_block(aux.shape[1]),
         ],
@@ -332,7 +333,7 @@
         ),
         cost_estimate=pl.CostEstimate(flops=flops, transcendentals=rows * 256 * HEADS,
                                       bytes_accessed=rows * (2048 * 8 + 512 * 8 + 256 * 4) + got.size * 2),
-    )(qkv, states, got, aux)
+    )(qkv, got, aux)
 
 
 def solution(mesh):

time: 106 us -> 108 us (1.019)
  other arithmetic: 13.5 us -> 19.2 us
  waiting for transfers between devices: 29.3 us -> 23.6 us
  starting transfers between devices: 16.7 us -> 19 us
    convert_element_type x0 -> x1, other arithmetic: none -> 4.04 us  [fused_attention(): states.astype(jnp.float32)]
    all_to_all x1, waiting for transfers between devices: 24.4 us -> 20.4 us  [local(): got = lax.all_to_all(send, axes, 0, 0, tiled=True)]
    all_to_all x1, waiting for transfers between devices: 4.95 us -> 3.13 us  [local(): lax.all_to_all(jnp.tile(slot_for_owner, serve_count).reshape(device_total...]
    all_to_all x1, starting transfers between devices: 5.25 us -> 7.03 us  [local(): got = lax.all_to_all(send, axes, 0, 0, tiled=True)]
    unnamed x10, local copies, waits for them, and re-layouts: 1.61 us -> 0.03 us
  transfers between devices with their start and end apart: 2 -> 2, of which waited for: 2 -> 2; matrix products, arithmetic and copies ran while one was open for 25% -> 30% of each run, Pallas kernels for 0% -> 0%
where the time goes in v15:
time: 108 us
  Pallas kernels  25.2 us (23%)
  waiting for transfers between devices  23.6 us (22%)
  other arithmetic  19.2 us (18%)
  starting transfers between devices  19 us (18%)
  matrix products  11.3 us (10%)
  local copies, waits for them, and re-layouts  9.31 us (9%)
    pallas_call x1, Pallas kernels, fused_attention(): pl.pallas_call(_attend_kernel, out_shape=jax.ShapeDtypeStruct((rows, HEAD...  25.2 us
    all_to_all x1, waiting for transfers between devices, local(): got = lax.all_to_all(send, axes, 0, 0, tiled=True)  20.4 us
    all_to_all x1, starting transfers between devices, local(): lax.all_to_all(jnp.tile(slot_for_owner, serve_count).reshape(device_total...  11.9 us
    dot_general x1, matrix products, local(): jnp.dot(normalized_hidden_states, query_weight_matrix, preferred_element_...  7.04 us
    all_to_all x1, starting transfers between devices, local(): got = lax.all_to_all(send, axes, 0, 0, tiled=True)  7.03 us
    concatenate x1, other arithmetic, fused_attention(): jnp.concatenate([q_base, k_base, v_base, states.astype(jnp.float32)], axi...  4.33 us
    convert_element_type x1, other arithmetic, fused_attention(): states.astype(jnp.float32)  4.04 us
    all_to_all x1, other arithmetic, local(): lax.all_to_all(jnp.tile(slot_for_owner, serve_count).reshape(device_total...  3.19 us
  transfers between devices with their start and end apart: 2, of which 2 were waited for; matrix products, arithmetic and copies ran while one was open for 30% of the time, Pallas kernels for 0%

profile of v15, /device:TPU:1, one launch (start us, length us, event | category | flops | bytes accessed | tf_op | source)
XLA Modules:
  0.0 107.7 jit_solution(5741419348243893823)
XLA Ops:
  0.0 0.0 copy-start
  0.0 1.0 select_reduce_fusion.2
  1.0 0.1 select_reduce_fusion.3
  1.2 0.8 all_to_all.15
  1.9 11.9 %all-to-all-start = ((s32[128,1,1]{2,1,0:T(1,128)}), s32[128,1,1]{2,1,0:T(1,128)}, u32[]{:S(2)}, u32[]{:S(2)}) async-start(s32[128,1,1]{2,1,0:T(1,128)} %all_to_all.15), calls=%async_computation | async-start | bytes 131072 | tf_op jit(solution)/shard_map/all_to_all | solution.py:150
  13.9 0.7 copy.40
  14.7 0.1 reduce.15
  14.8 0.1 convert_reduce_fusion
  14.9 0.7 fusion.1
  15.5 0.6 compare_reduce_fusion.1
  16.2 1.8 %fusion.2 = (bf16[32,16,256]{2,1,0:T(8,128)(2,1)S(1)}, bf16[32,16,256]{2,1,0:T(8,128)(2,1)}) fusion(bf16[32,32,256]{2,1,0:T(8,128)(2,1)} %param.18), kind=kLoop, calls=%fused_computation.30 | loop fusion | bytes 1048576 | tf_op jit(solution)/shard_map/slice | solution.py:134
  17.9 0.1 select_reduce_fusion
  18.0 0.1 copy.42
  18.2 0.6 convert_select_fusion
  18.8 1.2 %pad_maximum_fusion.1 = bf16[32,16,832]{2,1,0:T(8,128)(2,1)S(1)} fusion(bf16[32,16,64]{2,1,0:T(8,128)(2,1)} %param.20, bf16[32,16,256]{2,1,0:T(8,128)(2,1)} %param.19, bf16[32,16,256]{2,1,0:T(8,128)(2,1)} %get-tuple-element.32, bf16[32,16,256]{2,1,0:T(8,128)(2,1)S(1)} %get-tuple-element.31), kind=kLoop, calls=%fused_computation.2 | loop fusion | flops 3407872 | bytes 1703936 | tf_op jit(solution)/shard_map/concatenate | solution.py:132
  20.0 0.6 compare_reduce_fusion
  20.6 3.1 %all-to-all-done = s32[128,1,1]{2,1,0:T(1,128)} async-done(((s32[128,1,1]{2,1,0:T(1,128)}), s32[128,1,1]{2,1,0:T(1,128)}, u32[]{:S(2)}, u32[]{:S(2)}) %all-to-all-start) | async-done | bytes 544 | tf_op jit(solution)/shard_map/all_to_all | solution.py:150
  23.7 3.2 %reduce.14 = s32[128]{0:T(128)S(1)} reduce(s32[128,1,1]{2,1,0:T(1,128)} %all-to-all-done, s32[]{:T(128)} %constant.91.clone.1), dimensions={1,2}, to_apply=%all_to_all.12.reduce_sub_computation | reduce | bytes 1028 | tf_op jit(solution)/shard_map/all_to_all | solution.py:150
  26.9 2.7 %gather_fusion = bf16[128,16,832]{2,1,0:T(8,128)(2,1)} fusion(bf16[32,16,832]{2,1,0:T(8,128)(2,1)S(1)} %pad_maximum_fusion.1, s32[1024]{0:T(1024)S(1)} %pad_clamp_fusion), kind=kCustom, calls=%fused_computation | custom fusion | bytes 6816256 | tf_op jit(solution)/shard_map/jit(_take)/gather | solution.py:153
  29.7 7.0 %all-to-all-start.1 = ((bf16[128,16,832]{2,1,0:T(8,128)(2,1)}), bf16[128,16,832]{2,1,0:T(8,128)(2,1)}, u32[]{:S(2)}, u32[]{:S(2)}) async-start(bf16[128,16,832]{2,1,0:T(8,128)(2,1)} %gather_fusion), calls=%async_computation.1 | async-start | bytes 7340032 | tf_op jit(solution)/shard_map/all_to_all | solution.py:154
  36.7 0.7 convert_select_fusion.1
  37.4 4.0 %convert_element_type.37 = f32[512,2048]{1,0:T(8,128)} convert(bf16[512,2048]{1,0:T(8,128)(2,1)} %param.14) | non-fusion elementwise | flops 1048576 | bytes 6291456 | tf_op jit(solution)/shard_map/convert_element_type | solution.py:309
  41.4 0.1 copy.43
  41.6 1.3 %scatter.9 = f32[512,128]{1,0:T(8,128)S(1)} dynamic-update-slice(f32[512,128]{1,0:T(8,128)S(1)} %scatter.6, f32[512,1]{1,0:T(8,128)S(1)} %copy.43, s32[]{:T(128)} %constant.91.clone.1, s32[]{:T(128)} %constant.92.clone.1) | dynamic-update-slice | bytes 4100 | tf_op jit(solution)/shard_map/scatter | solution.py:307
  42.9 0.0 copy-start.3
  42.9 1.8 %multiply_sine_fusion = (f32[512,32]{1,0:T(8,128)S(1)}, f32[512,32]{1,0:T(8,128)}, f32[512,32]{1,0:T(8,128)S(1)}) fusion(f32[512]{0:T(512)S(1)} %subtract_convert_fusion, f32[32]{0:T(128)S(1)} %negate_power_fusion), kind=kLoop, calls=%fused_computation.3 | loop fusion | flops 32768 | bytes 198784 | tf_op jit(solution)/shard_map/sin | solution.py:297
  44.7 0.0 copy-done.3
  44.7 1.7 %concatenate.15.aux_ref = f32[512,384]{1,0:T(8,128)S(1)} concatenate(f32[512,32]{1,0:T(8,128)S(1)} %get-tuple-element.35, f32[512,32]{1,0:T(8,128)S(1)} %get-tuple-element.35, f32[512,32]{1,0:T(8,128)S(1)} %get-tuple-element.35, f32[512,32]{1,0:T(8,128)S(1)} %get-tuple-element.35, f32[512,32]{1,0:T(8,128)} %get-tuple-element.34, f32[512,32]{1,0:T(8,128)S(1)} %get-tuple-element.33, ...), dimensions={1} | concatenate | bytes 1572864 | tf_op jit(solution)/shard_map/concatenate | solution.py:308
  46.4 0.0 copy-done
  46.4 0.0 copy-start.2
  46.4 0.0 copy-start.4
  46.4 3.0 %fusion.5 = f32[512,512]{1,0:T(8,128)S(1)} fusion(bf16[512,2048]{1,0:T(8,128)(2,1)} %param.14, bf16[2048,512]{1,0:T(8,128)(2,1)S(1)} %copy-done), kind=kOutput, calls=%fused_computation.33 | convolution fusion | flops 1073741824 | bytes 5242880 | tf_op jit(solution)/shard_map/dot_general | solution.py:173
  49.4 0.0 copy-done.2
  49.4 0.0 copy-done.4
  49.4 1.3 %fusion.4 = f32[512,512]{1,0:T(8,128)S(1)} fusion(bf16[512,2048]{1,0:T(8,128)(2,1)S(1)} %copy-done.2, bf16[2048,512]{1,0:T(8,128)(2,1)S(1)} %copy-done.4), kind=kOutput, calls=%fused_computation.32 | convolution fusion | flops 1073741824 | bytes 5242880 | tf_op jit(solution)/shard_map/dot_general | solution.py:170
  50.7 0.0 copy-start.1
  50.7 7.0 %fusion.3 = f32[512,2048]{1,0:T(8,128)S(1)} fusion(bf16[512,2048]{1,0:T(8,128)(2,1)S(1)} %copy-done.2, bf16[2048,2048]{1,0:T(8,128)(2,1)} %param.15), kind=kOutput, calls=%fused_computation.31 | convolution fusion | flops 4294967296 | bytes 14680064 | tf_op jit(solution)/shard_map/dot_general | solution.py:167
  57.7 0.0 copy-done.1
  57.7 4.3 %pad_maximum_fusion.qkv_ref = f32[512,5120]{1,0:T(8,128)} fusion(f32[512,2048]{1,0:T(8,128)S(1)} %copy-done.1, f32[512,512]{1,0:T(8,128)S(1)} %fusion.5, f32[512,512]{1,0:T(8,128)S(1)} %fusion.4, f32[512,2048]{1,0:T(8,128)S(1)} %fusion.3), kind=kLoop, calls=%fused_computation.1 | loop fusion | flops 7864320 | bytes 20971520 | tf_op jit(solution)/shard_map/concatenate | solution.py:309
  62.1 20.4 %all-to-all-done.1 = bf16[128,16,832]{2,1,0:T(8,128)(2,1)} async-done(((bf16[128,16,832]{2,1,0:T(8,128)(2,1)}), bf16[128,16,832]{2,1,0:T(8,128)(2,1)}, u32[]{:S(2)}, u32[]{:S(2)}) %all-to-all-start.1) | async-done | bytes 3407904 | tf_op jit(solution)/shard_map/all_to_all | solution.py:154
  82.5 25.2 %shard_map.100 = bf16[512,2048]{1,0:T(8,128)(2,1)} custom-call(f32[512,5120]{1,0:T(8,128)} %pad_maximum_fusion.qkv_ref, bf16[2048,832]{1,0:T(8,128)(2,1)} %bitcast.1.got_ref, f32[512,384]{1,0:T(8,128)S(1)} %concatenate.15.aux_ref), custom_call_target="tpu_custom_call" | custom-call | flops 3892314112 | bytes 14417920 | tf_op jit(solution)/shard_map/pallas_call | solution.py:313
  (7 shorter events, 0.1 us)
Async XLA Ops:
  0.0 46.4 %copy-start = (bf16[2048,512]{1,0:T(8,128)(2,1)S(1)}, bf16[2048,512]{1,0:T(8,128)(2,1)}, u32[]{:S(2)}) copy-start(bf16[2048,512]{1,0:T(8,128)(2,1)} %param.17) | copy-start | bytes 6291460
  1.9 21.8 %all-to-all-start = ((s32[128,1,1]{2,1,0:T(1,128)}), s32[128,1,1]{2,1,0:T(1,128)}, u32[]{:S(2)}, u32[]{:S(2)}) async-start(s32[128,1,1]{2,1,0:T(1,128)} %all_to_all.15), calls=%async_computation | async-start | bytes 131072 | tf_op jit(solution)/shard_map/all_to_all | solution.py:150
  29.7 52.8 %all-to-all-start.1 = ((bf16[128,16,832]{2,1,0:T(8,128)(2,1)}), bf16[128,16,832]{2,1,0:T(8,128)(2,1)}, u32[]{:S(2)}, u32[]{:S(2)}) async-start(bf16[128,16,832]{2,1,0:T(8,128)(2,1)} %gather_fusion), calls=%async_computation.1 | async-start | bytes 7340032 | tf_op jit(solution)/shard_map/all_to_all | solution.py:154
  42.9 1.8 %copy-start.3 = (f32[512,128]{1,0:T(8,128)}, f32[512,128]{1,0:T(8,128)S(1)}, u32[]{:S(2)}) copy-start(f32[512,128]{1,0:T(8,128)S(1)} %scatter.9) | copy-start | bytes 786436
  46.4 3.0 %copy-start.2 = (bf16[512,2048]{1,0:T(8,128)(2,1)S(1)}, bf16[512,2048]{1,0:T(8,128)(2,1)}, u32[]{:S(2)}) copy-start(bf16[512,2048]{1,0:T(8,128)(2,1)} %param.14) | copy-start | bytes 6291460
  46.4 3.0 %copy-start.4 = (bf16[2048,512]{1,0:T(8,128)(2,1)S(1)}, bf16[2048,512]{1,0:T(8,128)(2,1)}, u32[]{:S(2)}) copy-start(bf16[2048,512]{1,0:T(8,128)(2,1)} %param.16) | copy-start | bytes 6291460
  50.7 7.1 %copy-start.1 = (f32[512,2048]{1,0:T(8,128)S(1)}, f32[512,2048]{1,0:T(8,128)}, u32[]{:S(2)}) copy-start(f32[512,2048]{1,0:T(8,128)} %convert_element_type.37) | copy-start | bytes 12582916

commit v16 on v14

--- a/solution.py
+++ b/solution.py
@@ -179,8 +179,8 @@
     )
 
 
-def _swap_halves(x):
-    return jnp.concatenate([x[:, 32:64], x[:, 0:32], x[:, 96:128], x[:, 64:96]], axis=1)
+def _swap_halves(x, use_first):
+    return jnp.where(use_first, pltpu.roll(x, 32, 1), pltpu.roll(x, 96, 1))
 
 
 def _attend_kernel(qkv_ref, x_ref, got_ref, aux_ref, out_ref, q_s, kd_s, vd_s, dq_ref, dv_ref, dt_s):
@@ -229,20 +229,23 @@
         dv_ref[:, c * 128:(c + 1) * 128] = jnp.concatenate(
             [pieces[2 * c], pieces[2 * c + 1]], axis=1).astype(jnp.bfloat16)
 
+    lane_of = lax.broadcasted_iota(jnp.int32, (blk, 128), 1)
+    partner = jnp.where(lane_of % 64 < 32, lane_of + 32, lane_of - 32)
+    use_first = pltpu.roll(lane_of, 32, 1) == partner
     cos = aux_ref[:, 0:128]
     sin = aux_ref[:, 128:256]
 
     def q_col(c, carry2):
         c0 = pl.multiple_of(c * 128, 128)
         x = qb_ref[:, pl.ds(c0, 128)] + dq_ref[:, pl.ds(c0, 128)].astype(jnp.float32)
-        q_s[:, pl.ds(c0, 128)] = (x * cos + _swap_halves(x) * sin).astype(jnp.bfloat16)
+        q_s[:, pl.ds(c0, 128)] = (x * cos + _swap_halves(x, use_first) * sin).astype(jnp.bfloat16)
         return carry2
 
     lax.fori_loop(0, q_chunks, q_col, 0, unroll=True)
     zeros = jnp.zeros((blk, 64), jnp.float32)
     for c in range(k_chunks):
         x = kb_ref[:, c * 128:(c + 1) * 128]
-        k = (x * cos + _swap_halves(x) * sin).astype(jnp.bfloat16).astype(jnp.float32)
+        k = (x * cos + _swap_halves(x, use_first) * sin).astype(jnp.bfloat16).astype(jnp.float32)
         v = vb_ref[:, c * 128:(c + 1) * 128] + dv_ref[:, c * 128:(c + 1) * 128].astype(jnp.float32)
         v = v.astype(jnp.bfloat16).astype(jnp.float32)
         for half in range(2):

time: 106 us -> 107 us (level)
  no operation moved by 1% of the time
where the time goes in v16:
time: 107 us; the launch traced here: 106 us
  waiting for transfers between devices  29.3 us (27%)
  Pallas kernels  25.3 us (24%)
  starting transfers between devices  16.7 us (16%)
  other arithmetic  13.5 us (13%)
  matrix products  11.1 us (10%)
  local copies, waits for them, and re-layouts  10.3 us (10%)
    pallas_call x1, Pallas kernels, fused_attention(): pl.pallas_call(_attend_kernel, out_shape=jax.ShapeDtypeStruct((rows, HEAD...  25.3 us
    all_to_all x1, waiting for transfers between devices, local(): got = lax.all_to_all(send, axes, 0, 0, tiled=True)  24.4 us
    all_to_all x1, starting transfers between devices, local(): lax.all_to_all(jnp.tile(slot_for_owner, serve_count).reshape(device_total...  11.5 us
    dot_general x1, matrix products, local(): jnp.dot(normalized_hidden_states, query_weight_matrix, preferred_element_...  6.89 us
    all_to_all x1, starting transfers between devices, local(): got = lax.all_to_all(send, axes, 0, 0, tiled=True)  5.25 us
    all_to_all x1, waiting for transfers between devices, local(): lax.all_to_all(jnp.tile(slot_for_owner, serve_count).reshape(device_total...  4.95 us
    concatenate x1, other arithmetic, fused_attention(): qkv = jnp.concatenate([q_base, k_base, v_base], axis=1)  3.35 us
    dot_general x1, matrix products, local(): jnp.dot(normalized_hidden_states, value_weight_matrix, preferred_element_...  2.98 us
  transfers between devices with their start and end apart: 2, of which 2 were waited for; matrix products, arithmetic and copies ran while one was open for 25% of the time, Pallas kernels for 0%

profile of v16, /device:TPU:1, one launch (start us, length us, event | category | flops | bytes accessed | tf_op | source)
XLA Modules:
  0.0 106.5 jit_solution(8861475476324278995)
XLA Ops:
  0.0 0.0 copy-start
  0.0 1.0 select_reduce_fusion.2
  1.0 0.1 select_reduce_fusion.3
  1.2 0.8 all_to_all.15
  1.9 11.5 %all-to-all-start = ((s32[128,1,1]{2,1,0:T(1,128)}), s32[128,1,1]{2,1,0:T(1,128)S(1)}, u32[]{:S(2)}, u32[]{:S(2)}) async-start(s32[128,1,1]{2,1,0:T(1,128)} %all_to_all.15), calls=%async_computation | async-start | bytes 131072 | tf_op jit(solution)/shard_map/all_to_all | solution.py:150
  13.4 0.7 copy.40
  14.2 0.1 reduce.15
  14.3 0.1 convert_reduce_fusion
  14.4 0.7 fusion.1
  15.1 1.1 %fusion.2 = (bf16[32,16,256]{2,1,0:T(8,128)(2,1)S(1)}, bf16[32,16,256]{2,1,0:T(8,128)(2,1)S(1)}) fusion(bf16[32,32,256]{2,1,0:T(8,128)(2,1)} %param.18), kind=kLoop, calls=%fused_computation.30 | loop fusion | bytes 1048576 | tf_op jit(solution)/shard_map/slice | solution.py:134
  16.1 1.1 %pad_maximum_fusion.1 = bf16[32,16,832]{2,1,0:T(8,128)(2,1)S(1)} fusion(bf16[32,16,64]{2,1,0:T(8,128)(2,1)} %param.20, bf16[32,16,256]{2,1,0:T(8,128)(2,1)} %param.19, bf16[32,16,256]{2,1,0:T(8,128)(2,1)S(1)} %get-tuple-element.32, bf16[32,16,256]{2,1,0:T(8,128)(2,1)S(1)} %get-tuple-element.31), kind=kLoop, calls=%fused_computation.2 | loop fusion | flops 3407872 | bytes 1703936 | tf_op jit(solution)/shard_map/concatenate | solution.py:132
  17.2 0.1 select_reduce_fusion
  17.3 0.1 copy.42
  17.5 0.7 compare_reduce_fusion
  18.2 4.9 %all-to-all-done = s32[128,1,1]{2,1,0:T(1,128)S(1)} async-done(((s32[128,1,1]{2,1,0:T(1,128)}), s32[128,1,1]{2,1,0:T(1,128)S(1)}, u32[]{:S(2)}, u32[]{:S(2)}) %all-to-all-start) | async-done | bytes 544 | tf_op jit(solution)/shard_map/all_to_all | solution.py:150
  23.2 2.3 %reduce.14 = s32[128]{0:T(128)S(1)} reduce(s32[128,1,1]{2,1,0:T(1,128)S(1)} %all-to-all-done, s32[]{:T(128)} %constant.91.clone.1), dimensions={1,2}, to_apply=%all_to_all.12.reduce_sub_computation | reduce | bytes 1028 | tf_op jit(solution)/shard_map/all_to_all | solution.py:150
  25.5 2.9 %gather_fusion = bf16[128,16,832]{2,1,0:T(8,128)(2,1)} fusion(bf16[32,16,832]{2,1,0:T(8,128)(2,1)S(1)} %pad_maximum_fusion.1, s32[1024]{0:T(1024)S(1)} %pad_clamp_fusion), kind=kCustom, calls=%fused_computation | custom fusion | bytes 6816256 | tf_op jit(solution)/shard_map/jit(_take)/gather | solution.py:153
  28.4 5.2 %all-to-all-start.1 = ((bf16[128,16,832]{2,1,0:T(8,128)(2,1)}), bf16[128,16,832]{2,1,0:T(8,128)(2,1)}, u32[]{:S(2)}, u32[]{:S(2)}) async-start(bf16[128,16,832]{2,1,0:T(8,128)(2,1)} %gather_fusion), calls=%async_computation.1 | async-start | bytes 7340032 | tf_op jit(solution)/shard_map/all_to_all | solution.py:154
  33.7 0.7 convert_select_fusion.1
  34.4 0.1 copy.43
  34.5 0.6 compare_reduce_fusion.1
  35.1 0.7 convert_select_fusion
  35.9 1.3 %scatter.9 = f32[512,128]{1,0:T(8,128)S(1)} dynamic-update-slice(f32[512,128]{1,0:T(8,128)S(1)} %scatter.6, f32[512,1]{1,0:T(8,128)S(1)} %copy.43, s32[]{:T(128)} %constant.91.clone.1, s32[]{:T(128)} %constant.92.clone.1) | dynamic-update-slice | bytes 4100 | tf_op jit(solution)/shard_map/scatter | solution.py:308
  37.2 0.0 copy-start.3
  37.2 1.8 %multiply_sine_fusion = (f32[512,32]{1,0:T(8,128)S(1)}, f32[512,32]{1,0:T(8,128)}, f32[512,32]{1,0:T(8,128)S(1)}) fusion(f32[512]{0:T(512)S(1)} %subtract_convert_fusion, f32[32]{0:T(128)S(1)} %negate_power_fusion), kind=kLoop, calls=%fused_computation.3 | loop fusion | flops 32768 | bytes 198784 | tf_op jit(solution)/shard_map/sin | solution.py:298
  39.0 0.0 copy-done.3
  39.0 1.7 %concatenate.15.aux_ref = f32[512,384]{1,0:T(8,128)S(1)} concatenate(f32[512,32]{1,0:T(8,128)S(1)} %get-tuple-element.35, f32[512,32]{1,0:T(8,128)S(1)} %get-tuple-element.35, f32[512,32]{1,0:T(8,128)S(1)} %get-tuple-element.35, f32[512,32]{1,0:T(8,128)S(1)} %get-tuple-element.35, f32[512,32]{1,0:T(8,128)} %get-tuple-element.34, f32[512,32]{1,0:T(8,128)S(1)} %get-tuple-element.33, ...), dimensions={1} | concatenate | bytes 1572864 | tf_op jit(solution)/shard_map/concatenate | solution.py:309
  40.7 0.0 copy-done
  40.7 0.0 copy-start.1
  40.7 0.0 copy-start.4
  40.7 3.0 %fusion.5 = f32[512,512]{1,0:T(8,128)S(1)} fusion(bf16[512,2048]{1,0:T(8,128)(2,1)} %x_ref.1, bf16[2048,512]{1,0:T(8,128)(2,1)S(1)} %copy-done), kind=kOutput, calls=%fused_computation.33 | convolution fusion | flops 1073741824 | bytes 5242880 | tf_op jit(solution)/shard_map/dot_general | solution.py:173
  43.7 0.0 copy-done.1
  43.7 0.0 copy-done.4
  43.7 1.2 %fusion.4 = f32[512,512]{1,0:T(8,128)S(1)} fusion(bf16[512,2048]{1,0:T(8,128)(2,1)S(1)} %copy-done.1, bf16[2048,512]{1,0:T(8,128)(2,1)S(1)} %copy-done.4), kind=kOutput, calls=%fused_computation.32 | convolution fusion | flops 1073741824 | bytes 5242880 | tf_op jit(solution)/shard_map/dot_general | solution.py:170
  44.9 6.9 %fusion.3 = f32[512,2048]{1,0:T(8,128)S(1)} fusion(bf16[512,2048]{1,0:T(8,128)(2,1)S(1)} %copy-done.1, bf16[2048,2048]{1,0:T(8,128)(2,1)} %param.15), kind=kOutput, calls=%fused_computation.31 | convolution fusion | flops 4294967296 | bytes 14680064 | tf_op jit(solution)/shard_map/dot_general | solution.py:167
  51.8 3.3 %pad_maximum_fusion.qkv_ref = f32[512,3072]{1,0:T(8,128)} fusion(f32[512,512]{1,0:T(8,128)S(1)} %fusion.5, f32[512,512]{1,0:T(8,128)S(1)} %fusion.4, f32[512,2048]{1,0:T(8,128)S(1)} %fusion.3), kind=kLoop, calls=%fused_computation.1 | loop fusion | flops 3145728 | bytes 12582912 | tf_op jit(solution)/shard_map/concatenate | solution.py:310
  55.2 24.4 %all-to-all-done.1 = bf16[128,16,832]{2,1,0:T(8,128)(2,1)} async-done(((bf16[128,16,832]{2,1,0:T(8,128)(2,1)}), bf16[128,16,832]{2,1,0:T(8,128)(2,1)}, u32[]{:S(2)}, u32[]{:S(2)}) %all-to-all-start.1) | async-done | bytes 3407904 | tf_op jit(solution)/shard_map/all_to_all | solution.py:154
  79.6 0.0 copy-start.2
  79.6 1.6 %copy-done.2 = bf16[512,2048]{1,0:T(8,128)(2,1)S(1)} copy-done((bf16[512,2048]{1,0:T(8,128)(2,1)S(1)}, bf16[512,2048]{1,0:T(8,128)(2,1)}, u32[]{:S(2)}) %copy-start.2) | copy-done | bytes 2097176
  81.2 25.3 %shard_map.100 = bf16[512,2048]{1,0:T(8,128)(2,1)} custom-call(f32[512,3072]{1,0:T(8,128)} %pad_maximum_fusion.qkv_ref, bf16[512,2048]{1,0:T(8,128)(2,1)S(1)} %copy-done.2, bf16[2048,832]{1,0:T(8,128)(2,1)} %bitcast.1.got_ref, f32[512,384]{1,0:T(8,128)S(1)} %concatenate.15.aux_ref), custom_call_target="tpu_custom_call" | custom-call | flops 3892314112 | bytes 14417920 | tf_op jit(solution)/shard_map/pallas_call | solution.py:314
  (7 shorter events, 0.1 us)
Async XLA Ops:
  0.0 40.7 %copy-start = (bf16[2048,512]{1,0:T(8,128)(2,1)S(1)}, bf16[2048,512]{1,0:T(8,128)(2,1)}, u32[]{:S(2)}) copy-start(bf16[2048,512]{1,0:T(8,128)(2,1)} %param.17) | copy-start | bytes 6291460
  1.9 21.2 %all-to-all-start = ((s32[128,1,1]{2,1,0:T(1,128)}), s32[128,1,1]{2,1,0:T(1,128)S(1)}, u32[]{:S(2)}, u32[]{:S(2)}) async-start(s32[128,1,1]{2,1,0:T(1,128)} %all_to_all.15), calls=%async_computation | async-start | bytes 131072 | tf_op jit(solution)/shard_map/all_to_all | solution.py:150
  28.4 51.2 %all-to-all-start.1 = ((bf16[128,16,832]{2,1,0:T(8,128)(2,1)}), bf16[128,16,832]{2,1,0:T(8,128)(2,1)}, u32[]{:S(2)}, u32[]{:S(2)}) async-start(bf16[128,16,832]{2,1,0:T(8,128)(2,1)} %gather_fusion), calls=%async_computation.1 | async-start | bytes 7340032 | tf_op jit(solution)/shard_map/all_to_all | solution.py:154
  37.2 1.8 %copy-start.3 = (f32[512,128]{1,0:T(8,128)}, f32[512,128]{1,0:T(8,128)S(1)}, u32[]{:S(2)}) copy-start(f32[512,128]{1,0:T(8,128)S(1)} %scatter.9) | copy-start | bytes 786436
  40.7 3.0 %copy-start.1 = (bf16[512,2048]{1,0:T(8,128)(2,1)S(1)}, bf16[512,2048]{1,0:T(8,128)(2,1)}, u32[]{:S(2)}) copy-start(bf16[512,2048]{1,0:T(8,128)(2,1)} %x_ref.1) | copy-start | bytes 6291460
  40.7 3.0 %copy-start.4 = (bf16[2048,512]{1,0:T(8,128)(2,1)S(1)}, bf16[2048,512]{1,0:T(8,128)(2,1)}, u32[]{:S(2)}) copy-start(bf16[2048,512]{1,0:T(8,128)(2,1)} %param.16) | copy-start | bytes 6291460
  79.6 1.6 %copy-start.2 = (bf16[512,2048]{1,0:T(8,128)(2,1)S(1)}, bf16[512,2048]{1,0:T(8,128)(2,1)}, u32[]{:S(2)}) copy-start(bf16[512,2048]{1,0:T(8,128)(2,1)} %x_ref.1) | copy-start | bytes 6291460
